TPU v7x, 512 devices: a whole 4x4x16 slice. The times are simulated.
512 devices in a mesh: storey: 32 (over x_hi, z), plate: 16 (over x_lo, y, core).
Axes of the slice: x: 4 (x_hi: 2, x_lo: 2; x = x_hi * 2 + x_lo), y: 4, z: 16, core: 2. Of those that a mesh axis runs over, the one named last changes fastest.
Arguments:
- load: float32 [4096, 8192], P('storey', 'plate'), may hold values from -6 to 6
- disp: float32 [4096, 8192], P('storey', 'plate'), may hold values from -2 to 2
- mass: float32 [4096, 8192], P('storey', 'plate'), may hold values from 0.05 to 0.5
- wall_class: int32 [4096, 8192], P('storey', 'plate'), may hold values from 0 to 3
- class_stiff: float32 [4], replicated, may hold values from 0.5 to 2
- damper_map: int32 [4096, 8192], P('storey', 'plate'), may hold values from 0 to 63
- damper_coef: float32 [2048], P('storey'), may hold values from 0.2 to 2
- band_tile: float32 [16384, 8192], P('storey', 'plate')
- panel_store: float32 [16384, 8192], P('storey', 'plate')
- owner: int32 [32], P('storey'), may hold values from 0 to 15
- node_index: int32 [32, 512], P('storey', 'plate'), may hold values from 0 to 65535, as said below
Outputs:
- new_disp: float32 [4096, 8192], P('storey', 'plate')
- adjoint: float32 [4096, 8192], P('storey', 'plate')
- shear: float32 [4096], P('storey')
- grads: float32 [2048], P('storey')
Inputs may be any that keep to these rules, and one draw needn't show every extreme that they name: `node_index`: the 32 nodes of one plate block of a group lie in distinct rows of the block, each given as row * 512 + column within the block.
All inputs are finite; a program needn't handle non-finite values.
Results may differ from a plain program's by a relative error of at most 0.0003.
Values sent between devices are 32-bit elements; how exact they have to be, the bound alone decides.
No kernel may reach another device: no remote copies, remote signals or barrier semaphores. Data moves between devices by JAX's collectives and lax.ppermute only.
A program may use at most 64 MiB of HBM per device.

v0:
```python
import math

import jax
import jax.numpy as jnp
from jax import lax
from jax.sharding import PartitionSpec as P

ITERS = 6


KF = 5.0 / 9.0
CM = 2.16
CD = 1.1
HIGH = lax.Precision.HIGHEST


def with_halo(x, sides, width):
    for axis, dim in sides:
        devices, length = (lax.axis_size(axis), x.shape[dim])
        up = [(i, (i + 1) % devices) for i in range(devices - 1)]
        down = [(j, i) for i, j in up]
        last = lax.slice_in_dim(x, length - width, length, axis=dim)
        first = lax.slice_in_dim(x, 0, width, axis=dim)
        before = lax.ppermute(last, axis, up)
        after = lax.ppermute(first, axis, down)
        x = jnp.concatenate([before, x, after], axis=dim)
    return x


def from_root(value, axis, source):
    kept = jnp.where(lax.axis_index(axis) == source, value, 0).astype(value.dtype)
    return lax.psum(kept, axis)


def prefix(x, axis, combine, identity, reverse):
    devices, position = (lax.axis_size(axis), lax.axis_index(axis))
    everything = lax.all_gather(x, axis)
    start = jnp.broadcast_to(jnp.asarray(identity, x.dtype), x.shape)

    def hop(k, before):
        at = devices - 1 - k if reverse else k
        reached = at > position if reverse else at < position
        new = combine(before, everything[at])
        return jnp.where(reached, new, before)

    return lax.fori_loop(0, devices, hop, start)


def neighbours(field):
    padded = with_halo(field, (("storey", 0), ("plate", 1)), 1)
    return padded[2:, 1:-1] + padded[:-2, 1:-1] + padded[1:-1, 2:] + padded[1:-1, :-2]


def add_values(left, right):
    return left + right


def damper_lookup(ids, coef):
    rows, cols = ids.shape
    blocks = ids.reshape(rows // 16, 16, cols)
    labels = jnp.arange(coef.shape[0], dtype=jnp.int32)

    def one_block(block):
        match = block[None, :, :] == labels[:, None, None]
        return jnp.sum(jnp.where(match, coef[:, None, None], 0.0), axis=0)

    return lax.map(one_block, blocks).reshape(rows, cols)


def damper_totals(ids, values, count):
    rows, cols = ids.shape
    labels = jnp.arange(count, dtype=jnp.int32)

    def one_block(pair):
        match = pair[0][None, :, :] == labels[:, None, None]
        return jnp.sum(jnp.where(match, pair[1][None, :, :], 0.0), axis=(1, 2))

    parts = lax.map(
        one_block, (ids.reshape(rows // 16, 16, cols), values.reshape(rows // 16, 16, cols))
    )
    return jnp.sum(parts, axis=0)


def on_device(
    load,
    disp,
    mass,
    wall_class,
    class_stiff,
    damper_map,
    damper_coef,
    band_tile,
    panel_store,
    owner,
    node_index,
):
    rows, cols = load.shape
    n_storey = lax.axis_size("storey")
    n_plate = lax.axis_size("plate")
    total_rows = rows * n_storey
    total_cols = cols * n_plate
    nodes = node_index.shape[1]
    stiff = jnp.zeros_like(load)
    for level in range(class_stiff.shape[0]):
        stiff = stiff + jnp.where(wall_class == level, class_stiff[level], 0.0)
    stiff = KF * stiff
    inertia = CM * mass
    damping = CD * damper_lookup(damper_map, damper_coef)
    diag = 4.0 * stiff + inertia + damping
    root = owner[0]
    places = node_index[0]
    here_plate = lax.axis_index("plate")
    panel_use = from_root(panel_store, "plate", root)

    def correct(resid, transpose):
        scaled = resid / diag
        if transpose:
            result = lax.dot_general(scaled, band_tile, (((1,), (1,)), ((), ())), precision=HIGH)
        else:
            result = jnp.dot(scaled, band_tile, precision=HIGH)
        picked = resid.reshape(-1)[places]
        values = lax.all_gather(picked, "plate", axis=0, tiled=True)
        if transpose:
            local_coarse = jnp.dot(values, panel_use, precision=HIGH)
        else:
            local_coarse = jnp.dot(panel_use, values, precision=HIGH)
        mine = lax.dynamic_slice_in_dim(local_coarse, here_plate * nodes, nodes)
        return result.reshape(-1).at[places].add(mine).reshape(rows, cols)

    new_disp = disp
    resid = load - (diag * new_disp - stiff * neighbours(new_disp))
    for step in range(ITERS):
        new_disp = new_disp + correct(resid, False)
        if step < ITERS - 1:
            resid = load - (diag * new_disp - stiff * neighbours(new_disp))
    partial_force = jnp.sum(inertia * new_disp, axis=1)
    force = lax.psum(partial_force, "plate") * (8.0 / math.sqrt(total_cols * total_rows))
    local_shear = jnp.cumsum(force[::-1])[::-1]
    above = prefix(jnp.sum(force), "storey", add_values, jnp.float32(0.0), True)
    shear = local_shear + above
    below = prefix(jnp.sum(shear), "storey", add_values, jnp.float32(0.0), False)
    drift = (jnp.cumsum(shear) + below) / total_rows
    target = inertia * drift[:, None]
    adjoint = jnp.zeros_like(load)
    resid = target
    for step in range(ITERS):
        adjoint = adjoint + correct(resid, True)
        if step < ITERS - 1:
            resid = target - (diag * adjoint - neighbours(stiff * adjoint))
    partial_sums = damper_totals(damper_map, adjoint * new_disp, damper_coef.shape[0])
    sums = lax.psum(partial_sums, "plate")
    grads = -CD * 64.0 / math.sqrt(rows * total_cols / damper_coef.shape[0]) * sums
    return (new_disp, adjoint, shear, grads)


def solution(mesh):
    return jax.shard_map(
        on_device,
        mesh=mesh,
        in_specs=(
            P("storey", "plate"),
            P("storey", "plate"),
            P("storey", "plate"),
            P("storey", "plate"),
            P(),
            P("storey", "plate"),
            P("storey"),
            P("storey", "plate"),
            P("storey", "plate"),
            P("storey"),
            P("storey", "plate"),
        ),
        out_specs=(P("storey", "plate"), P("storey", "plate"), P("storey"), P("storey")),
        check_vma=False,
    )
```

profile of v0, /device:TPU:7, one launch (start us, length us, event | category | flops | bytes accessed | tf_op | source)
XLA Modules:
  0.0 1087.4 jit_solution(1000961398261748344)
XLA Ops:
  8.0 12.0 %collective-permute-start = (f32[1,512]{1,0:T(1,128)S(1)}, f32[1,512]{1,0:T(1,128)S(1)}, u32[]{:S(2)}, u32[]{:S(2)}) collective-permute-start(f32[1,512]{1,0:T(1,128)S(1)} %get-tuple-element.362), channel_id=1, source_target_pairs={{16,0},{32,16},{48,32},{64,48},{80,64},{96,80},{112,96},{128,112},... | collective-permute-start | bytes 6152 | tf_op jit(solution)/shard_map/ppermute | solution.py:25
  24.4 8.6 while.52
  46.7 31.6 %all-reduce = f32[512]{0:T(512)S(1)} all-reduce(f32[512]{0:T(512)S(1)} %dynamic-update-slice), channel_id=2, replica_groups=mesh['storey'=32,'plate'=16] {'plate'}, use_global_device_ids=true, to_apply=%add | all-reduce | flops 512 | bytes 4096
  78.3 76.7 %all-reduce.16.cloned.1.call-done = f32[512,512]{1,0:T(8,128)} async-done(((f32[512,512]{1,0:T(8,128)}), f32[512,512]{1,0:T(8,128)}) %all-reduce.16.cloned.1.call-update) | async-done | bytes 1048592 | tf_op jit(solution)/shard_map/psum | solution.py:32
  158.2 6.3 collective-permute-start.4
  166.5 6.0 collective-permute-done.5
  172.6 4.6 collective-permute-start.6
  186.2 31.6 %all-reduce.1 = f32[512]{0:T(512)S(1)} all-reduce(f32[512]{0:T(512)S(1)} %dynamic-update-slice.1), channel_id=3, replica_groups=mesh['storey'=32,'plate'=16] {'plate'}, use_global_device_ids=true, to_apply=%add.1 | all-reduce | flops 512 | bytes 4096
  226.9 4.9 collective-permute-done.9
  246.0 31.0 %all-reduce.2 = f32[512]{0:T(512)S(1)} all-reduce(f32[512]{0:T(512)S(1)} %dynamic-update-slice.2), channel_id=4, replica_groups=mesh['storey'=32,'plate'=16] {'plate'}, use_global_device_ids=true, to_apply=%add.2 | all-reduce | flops 512 | bytes 4096
  289.2 4.6 collective-permute-done.13
  306.0 31.4 %all-reduce.3 = f32[512]{0:T(512)S(1)} all-reduce(f32[512]{0:T(512)S(1)} %dynamic-update-slice.3), channel_id=5, replica_groups=mesh['storey'=32,'plate'=16] {'plate'}, use_global_device_ids=true, to_apply=%add.3 | all-reduce | flops 512 | bytes 4096
  349.6 4.6 collective-permute-done.17
  366.4 31.0 %all-reduce.4 = f32[512]{0:T(512)S(1)} all-reduce(f32[512]{0:T(512)S(1)} %dynamic-update-slice.4), channel_id=6, replica_groups=mesh['storey'=32,'plate'=16] {'plate'}, use_global_device_ids=true, to_apply=%add.4 | all-reduce | flops 512 | bytes 4096
  410.2 4.6 collective-permute-done.21
  429.5 31.0 %all-reduce.5 = f32[512]{0:T(512)S(1)} all-reduce(f32[512]{0:T(512)S(1)} %dynamic-update-slice.5), channel_id=7, replica_groups=mesh['storey'=32,'plate'=16] {'plate'}, use_global_device_ids=true, to_apply=%add.5 | all-reduce | flops 512 | bytes 4096
  465.9 27.1 %psum.22 = f32[128]{0:T(128)S(1)} all-reduce(f32[128]{0:T(128)S(1)} %get-tuple-element.315), channel_id=1, replica_groups=mesh['storey'=32,'plate'=16] {'plate'}, use_global_device_ids=true, to_apply=%region_11.12 | all-reduce | flops 128 | bytes 1024 | tf_op jit(solution)/shard_map/psum | solution.py:137
  495.7 58.3 %all-reduce.6 = f32[32]{0:T(128)S(1)} all-reduce(f32[32]{0:T(128)S(1)} %dynamic-update-slice.6), channel_id=1, replica_groups=mesh['storey'=32,'plate'=16] {'storey'}, use_global_device_ids=true, to_apply=%add.6 | all-reduce | flops 32 | bytes 256
  554.0 40.6 %while.50 = (s32[]{:T(128)}, f32[]{:T(128)}, s32[]{:T(128)}, f32[32]{0:T(128)S(1)}, s32[]{:T(128)}, /*index=5*/s32[]{:T(128)}, s32[]{:T(128)}, s32[]{:T(128)}) while((s32[]{:T(128)}, f32[]{:T(128)}, s32[]{:T(128)}, f32[32]{0:T(128)S(1)}, s32[]{:T(128)}, /*index=5*/s32[]{:T(128)}, s32[]{:T(128)}, s32[]{:T(128)}) %tuple.131), condition=%wide.region_15.16_spmd, body=%wide.region_14.15_spmd.sunk | while | flops 9 | bytes 177 | solution.py:46
  596.7 59.9 %all-reduce.7 = f32[32]{0:T(128)S(1)} all-reduce(f32[32]{0:T(128)S(1)} %dynamic-update-slice.7), channel_id=1, replica_groups=mesh['storey'=32,'plate'=16] {'storey'}, use_global_device_ids=true, to_apply=%add.7 | all-reduce | flops 32 | bytes 256
  656.6 40.2 %while.51 = (s32[]{:T(128)}, f32[]{:T(128)}, s32[]{:T(128)}, f32[32]{0:T(128)S(1)}, s32[]{:T(128)}) while((s32[]{:T(128)}, f32[]{:T(128)}, s32[]{:T(128)}, f32[32]{0:T(128)S(1)}, s32[]{:T(128)}) %tuple.134), condition=%wide.region_19.20_spmd, body=%wide.region_18.19_spmd.sunk | while | flops 5 | bytes 107 | solution.py:46
  700.1 54.8 %all-reduce.8 = f32[512]{0:T(512)S(1)} all-reduce(f32[512]{0:T(512)S(1)} %dynamic-update-slice.8), channel_id=8, replica_groups=mesh['storey'=32,'plate'=16] {'plate'}, use_global_device_ids=true, to_apply=%add.8 | all-reduce | flops 512 | bytes 4096
  764.5 4.6 collective-permute-done.25
  779.3 31.0 %all-reduce.9 = f32[512]{0:T(512)S(1)} all-reduce(f32[512]{0:T(512)S(1)} %dynamic-update-slice.9), channel_id=9, replica_groups=mesh['storey'=32,'plate'=16] {'plate'}, use_global_device_ids=true, to_apply=%add.9 | all-reduce | flops 512 | bytes 4096
  821.7 4.6 collective-permute-done.29
  836.5 31.0 %all-reduce.10 = f32[512]{0:T(512)S(1)} all-reduce(f32[512]{0:T(512)S(1)} %dynamic-update-slice.10), channel_id=10, replica_groups=mesh['storey'=32,'plate'=16] {'plate'}, use_global_device_ids=true, to_apply=%add.10 | all-reduce | flops 512 | bytes 4096
  878.9 4.6 collective-permute-done.33
  893.7 31.0 %all-reduce.11 = f32[512]{0:T(512)S(1)} all-reduce(f32[512]{0:T(512)S(1)} %dynamic-update-slice.11), channel_id=11, replica_groups=mesh['storey'=32,'plate'=16] {'plate'}, use_global_device_ids=true, to_apply=%add.11 | all-reduce | flops 512 | bytes 4096
  950.9 31.0 %all-reduce.12 = f32[512]{0:T(512)S(1)} all-reduce(f32[512]{0:T(512)S(1)} %dynamic-update-slice.12), channel_id=12, replica_groups=mesh['storey'=32,'plate'=16] {'plate'}, use_global_device_ids=true, to_apply=%add.12 | all-reduce | flops 512 | bytes 4096
  1008.1 31.0 %all-reduce.13 = f32[512]{0:T(512)S(1)} all-reduce(f32[512]{0:T(512)S(1)} %dynamic-update-slice.13), channel_id=13, replica_groups=mesh['storey'=32,'plate'=16] {'plate'}, use_global_device_ids=true, to_apply=%add.13 | all-reduce | flops 512 | bytes 4096
  1041.6 11.0 %while.53 = (s32[]{:T(128)}, f32[8,64]{1,0:T(8,128)S(1)}, s32[8,16,512]{2,1,0:T(8,128)}, f32[8,16,512]{2,1,0:T(8,128)S(1)}, s32[]{:T(128)}, /*index=5*/s32[]{:T(128)}) while((s32[]{:T(128)}, f32[8,64]{1,0:T(8,128)S(1)}, s32[8,16,512]{2,1,0:T(8,128)}, f32[8,16,512]{2,1,0:T(8,128)S(1)}, s32[]{:T(128)}, ...), condition=%wide.region_28.29_spmd.clone, body=%wide.region_26.28_spmd.clone.sunk | while | flops 1572802 | bytes 197457 | solution.py:78
  1052.6 27.1 %psum.23 = f32[64]{0:T(128)S(1)} all-reduce(f32[64]{0:T(128)S(1)} %reduce_sum.57), channel_id=1, replica_groups=mesh['storey'=32,'plate'=16] {'plate'}, use_global_device_ids=true, to_apply=%region_30.31 | all-reduce | flops 64 | bytes 512 | tf_op jit(solution)/shard_map/psum | solution.py:151
  (455 shorter events, 319.5 us)
Async XLA Ops:
  7.2 147.8 %all-reduce.16.cloned.1.call-start = ((), (), s32[]{:S(2)}) async-start(), calls=%async_computation | async-start | bytes 2097152 | tf_op jit(solution)/shard_map/psum | solution.py:32
  8.0 25.6 %collective-permute-start = (f32[1,512]{1,0:T(1,128)S(1)}, f32[1,512]{1,0:T(1,128)S(1)}, u32[]{:S(2)}, u32[]{:S(2)}) collective-permute-start(f32[1,512]{1,0:T(1,128)S(1)} %get-tuple-element.362), channel_id=1, source_target_pairs={{16,0},{32,16},{48,32},{64,48},{80,64},{96,80},{112,96},{128,112},... | collective-permute-start | bytes 6152 | tf_op jit(solution)/shard_map/ppermute | solution.py:25
  20.0 13.7 %collective-permute-start.1 = (f32[1,512]{1,0:T(1,128)S(1)}, f32[1,512]{1,0:T(1,128)S(1)}, u32[]{:S(2)}, u32[]{:S(2)}) collective-permute-start(f32[1,512]{1,0:T(1,128)S(1)} %get-tuple-element.361), channel_id=1, source_target_pairs={{0,16},{16,32},{32,48},{48,64},{64,80},{80,96},{96,112},{112,128},... | collective-permute-start | bytes 6152 | tf_op jit(solution)/shard_map/ppermute | solution.py:24
  33.8 7.9 collective-permute-start.2
  36.7 5.4 collective-permute-start.3
  158.2 8.2 collective-permute-start.4
  164.5 7.9 collective-permute-start.5
  172.6 6.5 collective-permute-start.6
  221.6 5.3 collective-permute-start.8
  223.9 7.9 collective-permute-start.9
  231.9 5.9 collective-permute-start.10
  283.9 5.3 collective-permute-start.12
  285.8 7.9 collective-permute-start.13
  293.8 5.6 collective-permute-start.14
  344.3 5.3 collective-permute-start.16
  346.2 7.9 collective-permute-start.17
  354.2 5.6 collective-permute-start.18
  406.9 7.9 collective-permute-start.21
  415.8 7.0 collective-permute-start.22
  759.2 5.3 collective-permute-start.24
  761.1 7.9 collective-permute-start.25
  769.2 5.8 collective-permute-start.26
  816.4 5.3 collective-permute-start.28
  818.3 7.9 collective-permute-start.29
  826.4 5.6 collective-permute-start.30
  875.5 7.9 collective-permute-start.33
  883.6 5.6 collective-permute-start.34
  931.5 5.3 collective-permute-start.36
  933.5 7.9 collective-permute-start.37
  941.5 5.6 collective-permute-start.38
  989.8 7.9 collective-permute-start.41
  997.8 5.9 collective-permute-start.42
  (45 other events, 1426.1 us)
Sparse Core Ops, SparseCore 0:
  23.9 131.0 all-reduce.15
where the time goes:
time: 1100 us; the launch traced here: 1090 us
  blocking collectives  570 us (52%)
  waiting for transfers between devices  137 us (12%)
  starting transfers between devices  133 us (12%)
  local copies, waits for them, and re-layouts  88.8 us (8%)
  other arithmetic  70 us (6%)
  loops' own time  43.6 us (4%)
  matrix products  28.3 us (3%)
  between operations  16.9 us (2%)
    unnamed x14, blocking collectives  515 us
    ppermute x22, starting transfers between devices, with_halo(): after = lax.ppermute(first, axis, down)  76.9 us
    psum x1, waiting for transfers between devices, from_root(): return lax.psum(kept, axis)  76.7 us
    ppermute x22, waiting for transfers between devices, with_halo(): before = lax.ppermute(last, axis, up)  60 us
    ppermute x22, starting transfers between devices, with_halo(): before = lax.ppermute(last, axis, up)  56.4 us
    another operation x2, loops' own time, prefix(): return lax.fori_loop(0, devices, hop, start)  43.2 us
    dynamic_slice x64, local copies, waits for them, and re-layouts, hop(): new = combine(before, everything[at])  37.5 us
    psum x1, blocking collectives, on_device(): sums = lax.psum(partial_sums, 'plate')  27.1 us
  transfers between devices with their start and end apart: 45, of which 21 were waited for; matrix products, arithmetic and copies ran while one was open for 2% of the time, Pallas kernels for 0%

commit v1 on v0

--- a/solution.py
+++ b/solution.py
@@ -27,32 +27,32 @@
     return x
 
 
-def from_root(value, axis, source):
-    kept = jnp.where(lax.axis_index(axis) == source, value, 0).astype(value.dtype)
-    return lax.psum(kept, axis)
+def by_shift(value, axis):
+    devices = lax.axis_size(axis)
+    got = [value]
+    for shift in range(1, devices):
+        pairs = [(a, (a + shift) % devices) for a in range(devices)]
+        got.append(lax.ppermute(value, axis, pairs))
+    return jnp.stack(got)
 
 
-def prefix(x, axis, combine, identity, reverse):
+def to_source_order(stacked, axis):
     devices, position = (lax.axis_size(axis), lax.axis_index(axis))
-    everything = lax.all_gather(x, axis)
-    start = jnp.broadcast_to(jnp.asarray(identity, x.dtype), x.shape)
+    order = (position - jnp.arange(devices, dtype=jnp.int32)) % devices
+    return jnp.take(stacked, order, axis=0)
 
-    def hop(k, before):
-        at = devices - 1 - k if reverse else k
-        reached = at > position if reverse else at < position
-        new = combine(before, everything[at])
-        return jnp.where(reached, new, before)
 
-    return lax.fori_loop(0, devices, hop, start)
+def gather_all(value, axis):
+    return to_source_order(by_shift(value, axis), axis)
+
+
+def sum_all(value, axis):
+    return jnp.sum(gather_all(value, axis), axis=0)
 
 
 def neighbours(field):
     padded = with_halo(field, (("storey", 0), ("plate", 1)), 1)
     return padded[2:, 1:-1] + padded[:-2, 1:-1] + padded[1:-1, 2:] + padded[1:-1, :-2]
-
-
-def add_values(left, right):
-    return left + right
 
 
 def damper_lookup(ids, coef):
@@ -81,6 +81,30 @@
     return jnp.sum(parts, axis=0)
 
 
+def panel_slabs(panel_store, owner, nodes):
+    n_plate = lax.axis_size("plate")
+    here = lax.axis_index("plate")
+    mine = here == owner
+    rows_of = panel_store.reshape(n_plate, nodes, -1)
+    cols_of = jnp.swapaxes(panel_store.reshape(-1, n_plate, nodes), 0, 1)
+    cols_of = jnp.swapaxes(cols_of, 1, 2)
+
+    def fetch(slabs):
+        got = [jnp.where(mine, slabs[here], 0.0)]
+        for shift in range(1, n_plate):
+            pairs = [(a, (a + shift) % n_plate) for a in range(n_plate)]
+            target = (here + shift) % n_plate
+            got.append(lax.ppermute(jnp.where(mine, slabs[target], 0.0), "plate", pairs))
+        total = got[0]
+        for piece in got[1:]:
+            total = total + piece
+        order = (here - jnp.arange(n_plate, dtype=jnp.int32)) % n_plate
+        total = total.reshape(nodes, n_plate, nodes)
+        return jnp.take(total, order, axis=1).reshape(nodes, n_plate * nodes)
+
+    return fetch(rows_of), fetch(cols_of)
+
+
 def on_device(
     load,
     disp,
@@ -107,10 +131,8 @@
     inertia = CM * mass
     damping = CD * damper_lookup(damper_map, damper_coef)
     diag = 4.0 * stiff + inertia + damping
-    root = owner[0]
     places = node_index[0]
-    here_plate = lax.axis_index("plate")
-    panel_use = from_root(panel_store, "plate", root)
+    row_slab, col_slab = panel_slabs(panel_store, owner[0], nodes)
 
     def correct(resid, transpose):
         scaled = resid / diag
@@ -119,12 +141,9 @@
         else:
             result = jnp.dot(scaled, band_tile, precision=HIGH)
         picked = resid.reshape(-1)[places]
-        values = lax.all_gather(picked, "plate", axis=0, tiled=True)
-        if transpose:
-            local_coarse = jnp.dot(values, panel_use, precision=HIGH)
-        else:
-            local_coarse = jnp.dot(panel_use, values, precision=HIGH)
-        mine = lax.dynamic_slice_in_dim(local_coarse, here_plate * nodes, nodes)
+        values = by_shift(picked, "plate").reshape(-1)
+        slab = col_slab if transpose else row_slab
+        mine = jnp.dot(slab, values, precision=HIGH)
         return result.reshape(-1).at[places].add(mine).reshape(rows, cols)
 
     new_disp = disp
@@ -134,12 +153,13 @@
         if step < ITERS - 1:
             resid = load - (diag * new_disp - stiff * neighbours(new_disp))
     partial_force = jnp.sum(inertia * new_disp, axis=1)
-    force = lax.psum(partial_force, "plate") * (8.0 / math.sqrt(total_cols * total_rows))
-    local_shear = jnp.cumsum(force[::-1])[::-1]
-    above = prefix(jnp.sum(force), "storey", add_values, jnp.float32(0.0), True)
-    shear = local_shear + above
-    below = prefix(jnp.sum(shear), "storey", add_values, jnp.float32(0.0), False)
-    drift = (jnp.cumsum(shear) + below) / total_rows
+    force = sum_all(partial_force, "plate") * (8.0 / math.sqrt(total_cols * total_rows))
+    every_force = gather_all(force, "storey").reshape(-1)
+    every_shear = jnp.cumsum(every_force[::-1])[::-1]
+    every_drift = jnp.cumsum(every_shear) / total_rows
+    here_storey = lax.axis_index("storey")
+    shear = lax.dynamic_slice_in_dim(every_shear, here_storey * rows, rows)
+    drift = lax.dynamic_slice_in_dim(every_drift, here_storey * rows, rows)
     target = inertia * drift[:, None]
     adjoint = jnp.zeros_like(load)
     resid = target
@@ -148,7 +168,7 @@
         if step < ITERS - 1:
             resid = target - (diag * adjoint - neighbours(stiff * adjoint))
     partial_sums = damper_totals(damper_map, adjoint * new_disp, damper_coef.shape[0])
-    sums = lax.psum(partial_sums, "plate")
+    sums = sum_all(partial_sums, "plate")
     grads = -CD * 64.0 / math.sqrt(rows * total_cols / damper_coef.shape[0]) * sums
     return (new_disp, adjoint, shear, grads)
 

time: 1100 us -> 1600 us (1.45)
  starting transfers between devices: 133 us -> 1370 us
  blocking collectives: 570 us -> 0 us
  local copies, waits for them, and re-layouts: 88.8 us -> 33.4 us
  loops' own time: 43.6 us -> 0.32 us
  waiting for transfers between devices: 137 us -> 94.1 us
    ppermute x0 -> x271, starting transfers between devices: none -> 1230 us  [the longest x241 1130 us: by_shift(): got.append(lax.ppermute(value, axis, pairs))]
    unnamed x14 -> x0, blocking collectives: 515 us -> none
    psum x1 -> x0, waiting for transfers between devices: 76.7 us -> none  [from_root(): return lax.psum(kept, axis)]
    psum x2 -> x0, blocking collectives: 54.3 us -> none  [the longest x1 27.1 us: on_device(): sums = lax.psum(partial_sums, 'plate')]
    another operation x2 -> x0, loops' own time: 43.2 us -> none  [prefix(): return lax.fori_loop(0, devices, hop, start)]
    dynamic_slice x76 -> x1, local copies, waits for them, and re-layouts: 38.5 us -> 0.59 us  [on_device(): shear = lax.dynamic_slice_in_dim(every_shear, here_storey * rows, rows)]
    ppermute x0 -> x271, waiting for transfers between devices: none -> 18.2 us  [the longest x241 16.4 us: by_shift(): got.append(lax.ppermute(value, axis, pairs))]
  transfers between devices with their start and end apart: 45 -> 315, of which waited for: 21 -> 39; matrix products, arithmetic and copies ran while one was open for 2% -> 2% of each run, Pallas kernels for 0% -> 0%
where the time goes in v1:
time: 1600 us; the launch traced here: 1580 us
  starting transfers between devices  1370 us (86%)
  waiting for transfers between devices  94.1 us (6%)
  other arithmetic  59.7 us (4%)
  local copies, waits for them, and re-layouts  33.4 us (2%)
    ppermute x241, starting transfers between devices, by_shift(): got.append(lax.ppermute(value, axis, pairs))  1130 us
    ppermute x30, starting transfers between devices, fetch(): lax.ppermute(jnp.where(mine, slabs[target], 0.0), 'plate', pairs)  98 us
    ppermute x22, starting transfers between devices, with_halo(): after = lax.ppermute(first, axis, down)  85.2 us
    ppermute x22, waiting for transfers between devices, with_halo(): before = lax.ppermute(last, axis, up)  75.7 us
    ppermute x22, starting transfers between devices, with_halo(): before = lax.ppermute(last, axis, up)  54.8 us
  transfers between devices with their start and end apart: 315, of which 39 were waited for; matrix products, arithmetic and copies ran while one was open for 2% of the time, Pallas kernels for 0%

profile of v1, /device:TPU:7, one launch (start us, length us, event | category | flops | bytes accessed | tf_op | source)
XLA Modules:
  0.0 1575.9 jit_solution(1002397016968660092)
XLA Ops:
  13.2 11.8 collective-permute-start
  27.6 8.6 while.22
  270.6 9.8 collective-permute-start.61
  350.5 9.8 collective-permute-start.80
  429.9 9.8 collective-permute-start.99
  509.3 9.8 collective-permute-start.118
  673.2 20.6 %collective-permute-start.151 = (f32[128]{0:T(128)S(1)}, f32[128]{0:T(128)S(1)}, u32[]{:S(2)}, u32[]{:S(2)}) collective-permute-start(f32[128]{0:T(128)S(1)} %get-tuple-element.185), channel_id=1, source_target_pairs={{0,128},{16,144},{32,160},{48,176},{64,192},{80,208},{96,224},{112... | collective-permute-start | bytes 1544 | tf_op jit(solution)/shard_map/ppermute | solution.py:35
  697.7 17.8 %collective-permute-start.154 = (f32[128]{0:T(128)S(1)}, f32[128]{0:T(128)S(1)}, u32[]{:S(2)}, u32[]{:S(2)}) collective-permute-start(f32[128]{0:T(128)S(1)} %get-tuple-element.185), channel_id=1, source_target_pairs={{0,176},{16,192},{32,208},{48,224},{64,240},{80,256},{96,272},{112... | collective-permute-start | bytes 1544 | tf_op jit(solution)/shard_map/ppermute | solution.py:35
  726.3 17.4 %collective-permute-start.158 = (f32[128]{0:T(128)S(1)}, f32[128]{0:T(128)S(1)}, u32[]{:S(2)}, u32[]{:S(2)}) collective-permute-start(f32[128]{0:T(128)S(1)} %get-tuple-element.185), channel_id=1, source_target_pairs={{0,240},{16,256},{32,272},{48,288},{64,304},{80,320},{96,336},{112... | collective-permute-start | bytes 1544 | tf_op jit(solution)/shard_map/ppermute | solution.py:35
  743.7 19.0 %collective-permute-start.159 = (f32[128]{0:T(128)S(1)}, f32[128]{0:T(128)S(1)}, u32[]{:S(2)}, u32[]{:S(2)}) collective-permute-start(f32[128]{0:T(128)S(1)} %get-tuple-element.185), channel_id=1, source_target_pairs={{0,256},{16,272},{32,288},{48,304},{64,320},{80,336},{96,352},{112... | collective-permute-start | bytes 1544 | tf_op jit(solution)/shard_map/ppermute | solution.py:35
  762.8 19.0 %collective-permute-start.160 = (f32[128]{0:T(128)S(1)}, f32[128]{0:T(128)S(1)}, u32[]{:S(2)}, u32[]{:S(2)}) collective-permute-start(f32[128]{0:T(128)S(1)} %get-tuple-element.185), channel_id=1, source_target_pairs={{0,272},{16,288},{32,304},{48,320},{64,336},{80,352},{96,368},{112... | collective-permute-start | bytes 1544 | tf_op jit(solution)/shard_map/ppermute | solution.py:35
  781.8 19.0 %collective-permute-start.161 = (f32[128]{0:T(128)S(1)}, f32[128]{0:T(128)S(1)}, u32[]{:S(2)}, u32[]{:S(2)}) collective-permute-start(f32[128]{0:T(128)S(1)} %get-tuple-element.185), channel_id=1, source_target_pairs={{0,288},{16,304},{32,320},{48,336},{64,352},{80,368},{96,384},{112... | collective-permute-start | bytes 1544 | tf_op jit(solution)/shard_map/ppermute | solution.py:35
  800.8 19.0 %collective-permute-start.162 = (f32[128]{0:T(128)S(1)}, f32[128]{0:T(128)S(1)}, u32[]{:S(2)}, u32[]{:S(2)}) collective-permute-start(f32[128]{0:T(128)S(1)} %get-tuple-element.185), channel_id=1, source_target_pairs={{0,304},{16,320},{32,336},{48,352},{64,368},{80,384},{96,400},{112... | collective-permute-start | bytes 1544 | tf_op jit(solution)/shard_map/ppermute | solution.py:35
  819.9 19.0 %collective-permute-start.163 = (f32[128]{0:T(128)S(1)}, f32[128]{0:T(128)S(1)}, u32[]{:S(2)}, u32[]{:S(2)}) collective-permute-start(f32[128]{0:T(128)S(1)} %get-tuple-element.185), channel_id=1, source_target_pairs={{0,320},{16,336},{32,352},{48,368},{64,384},{80,400},{96,416},{112... | collective-permute-start | bytes 1544 | tf_op jit(solution)/shard_map/ppermute | solution.py:35
  838.9 19.0 %collective-permute-start.164 = (f32[128]{0:T(128)S(1)}, f32[128]{0:T(128)S(1)}, u32[]{:S(2)}, u32[]{:S(2)}) collective-permute-start(f32[128]{0:T(128)S(1)} %get-tuple-element.185), channel_id=1, source_target_pairs={{0,336},{16,352},{32,368},{48,384},{64,400},{80,416},{96,432},{112... | collective-permute-start | bytes 1544 | tf_op jit(solution)/shard_map/ppermute | solution.py:35
  857.9 19.0 %collective-permute-start.165 = (f32[128]{0:T(128)S(1)}, f32[128]{0:T(128)S(1)}, u32[]{:S(2)}, u32[]{:S(2)}) collective-permute-start(f32[128]{0:T(128)S(1)} %get-tuple-element.185), channel_id=1, source_target_pairs={{0,352},{16,368},{32,384},{48,400},{64,416},{80,432},{96,448},{112... | collective-permute-start | bytes 1544 | tf_op jit(solution)/shard_map/ppermute | solution.py:35
  876.9 19.0 %collective-permute-start.166 = (f32[128]{0:T(128)S(1)}, f32[128]{0:T(128)S(1)}, u32[]{:S(2)}, u32[]{:S(2)}) collective-permute-start(f32[128]{0:T(128)S(1)} %get-tuple-element.185), channel_id=1, source_target_pairs={{0,368},{16,384},{32,400},{48,416},{64,432},{80,448},{96,464},{112... | collective-permute-start | bytes 1544 | tf_op jit(solution)/shard_map/ppermute | solution.py:35
  896.0 19.0 %collective-permute-start.167 = (f32[128]{0:T(128)S(1)}, f32[128]{0:T(128)S(1)}, u32[]{:S(2)}, u32[]{:S(2)}) collective-permute-start(f32[128]{0:T(128)S(1)} %get-tuple-element.185), channel_id=1, source_target_pairs={{0,384},{16,400},{32,416},{48,432},{64,448},{80,464},{96,480},{112... | collective-permute-start | bytes 1544 | tf_op jit(solution)/shard_map/ppermute | solution.py:35
  915.0 19.0 %collective-permute-start.168 = (f32[128]{0:T(128)S(1)}, f32[128]{0:T(128)S(1)}, u32[]{:S(2)}, u32[]{:S(2)}) collective-permute-start(f32[128]{0:T(128)S(1)} %get-tuple-element.185), channel_id=1, source_target_pairs={{0,400},{16,416},{32,432},{48,448},{64,464},{80,480},{96,496},{112... | collective-permute-start | bytes 1544 | tf_op jit(solution)/shard_map/ppermute | solution.py:35
  934.0 19.0 %collective-permute-start.169 = (f32[128]{0:T(128)S(1)}, f32[128]{0:T(128)S(1)}, u32[]{:S(2)}, u32[]{:S(2)}) collective-permute-start(f32[128]{0:T(128)S(1)} %get-tuple-element.185), channel_id=1, source_target_pairs={{0,416},{16,432},{32,448},{48,464},{64,480},{80,496},{96,0},{112,1... | collective-permute-start | bytes 1544 | tf_op jit(solution)/shard_map/ppermute | solution.py:35
  953.0 19.0 %collective-permute-start.170 = (f32[128]{0:T(128)S(1)}, f32[128]{0:T(128)S(1)}, u32[]{:S(2)}, u32[]{:S(2)}) collective-permute-start(f32[128]{0:T(128)S(1)} %get-tuple-element.185), channel_id=1, source_target_pairs={{0,432},{16,448},{32,464},{48,480},{64,496},{80,0},{96,16},{112,32... | collective-permute-start | bytes 1544 | tf_op jit(solution)/shard_map/ppermute | solution.py:35
  972.1 19.0 %collective-permute-start.171 = (f32[128]{0:T(128)S(1)}, f32[128]{0:T(128)S(1)}, u32[]{:S(2)}, u32[]{:S(2)}) collective-permute-start(f32[128]{0:T(128)S(1)} %get-tuple-element.185), channel_id=1, source_target_pairs={{0,448},{16,464},{32,480},{48,496},{64,0},{80,16},{96,32},{112,48}... | collective-permute-start | bytes 1544 | tf_op jit(solution)/shard_map/ppermute | solution.py:35
  991.1 19.0 %collective-permute-start.172 = (f32[128]{0:T(128)S(1)}, f32[128]{0:T(128)S(1)}, u32[]{:S(2)}, u32[]{:S(2)}) collective-permute-start(f32[128]{0:T(128)S(1)} %get-tuple-element.185), channel_id=1, source_target_pairs={{0,464},{16,480},{32,496},{48,0},{64,16},{80,32},{96,48},{112,64},... | collective-permute-start | bytes 1544 | tf_op jit(solution)/shard_map/ppermute | solution.py:35
  1010.1 19.0 %collective-permute-start.173 = (f32[128]{0:T(128)S(1)}, f32[128]{0:T(128)S(1)}, u32[]{:S(2)}, u32[]{:S(2)}) collective-permute-start(f32[128]{0:T(128)S(1)} %get-tuple-element.185), channel_id=1, source_target_pairs={{0,480},{16,496},{32,0},{48,16},{64,32},{80,48},{96,64},{112,80},{... | collective-permute-start | bytes 1544 | tf_op jit(solution)/shard_map/ppermute | solution.py:35
  1029.1 19.0 %collective-permute-start.174 = (f32[128]{0:T(128)S(1)}, f32[128]{0:T(128)S(1)}, u32[]{:S(2)}, u32[]{:S(2)}) collective-permute-start(f32[128]{0:T(128)S(1)} %get-tuple-element.185), channel_id=1, source_target_pairs={{0,496},{16,0},{32,16},{48,32},{64,48},{80,64},{96,80},{112,96},{1... | collective-permute-start | bytes 1544 | tf_op jit(solution)/shard_map/ppermute | solution.py:35
  1110.4 7.7 collective-permute-start.205
  1147.7 9.1 collective-permute-start.213
  1226.9 9.8 collective-permute-start.232
  1306.8 9.8 collective-permute-start.251
  1386.7 9.8 collective-permute-start.270
  1466.6 9.8 collective-permute-start.289
  1512.6 11.0 while.23
  (927 shorter events, 1100.9 us)
Async XLA Ops:
  3.8 111.5 %collective-permute-start.10 = (f32[32,512]{1,0:T(8,128)}, f32[32,512]{1,0:T(8,128)S(1)}, u32[]{:S(2)}, u32[]{:S(2)}) collective-permute-start(f32[32,512]{1,0:T(8,128)} %get-tuple-element.135), channel_id=1, source_target_pairs={{0,7},{1,8},{2,9},{3,10},{4,11},{5,12},{6,13},{7,14},{8,15},{9,0},... | collective-permute-start | bytes 196616 | tf_op jit(solution)/shard_map/ppermute | solution.py:97
  7.0 110.3 %collective-permute-start.11 = (f32[32,512]{1,0:T(8,128)}, f32[32,512]{1,0:T(8,128)S(1)}, u32[]{:S(2)}, u32[]{:S(2)}) collective-permute-start(f32[32,512]{1,0:T(8,128)} %get-tuple-element.134), channel_id=1, source_target_pairs={{0,8},{1,9},{2,10},{3,11},{4,12},{5,13},{6,14},{7,15},{8,0},{9,1},... | collective-permute-start | bytes 196616 | tf_op jit(solution)/shard_map/ppermute | solution.py:97
  9.8 110.2 %collective-permute-start.12 = (f32[32,512]{1,0:T(8,128)}, f32[32,512]{1,0:T(8,128)S(1)}, u32[]{:S(2)}, u32[]{:S(2)}) collective-permute-start(f32[32,512]{1,0:T(8,128)} %get-tuple-element.133), channel_id=1, source_target_pairs={{0,9},{1,10},{2,11},{3,12},{4,13},{5,14},{6,15},{7,0},{8,1},{9,2},... | collective-permute-start | bytes 196616 | tf_op jit(solution)/shard_map/ppermute | solution.py:97
  660.4 33.4 %collective-permute-start.147 = (f32[128]{0:T(128)S(1)}, f32[128]{0:T(128)S(1)}, u32[]{:S(2)}, u32[]{:S(2)}) collective-permute-start(f32[128]{0:T(128)S(1)} %get-tuple-element.185), channel_id=1, source_target_pairs={{0,64},{16,80},{32,96},{48,112},{64,128},{80,144},{96,160},{112,17... | collective-permute-start | bytes 1544 | tf_op jit(solution)/shard_map/ppermute | solution.py:35
  662.3 33.4 %collective-permute-start.148 = (f32[128]{0:T(128)S(1)}, f32[128]{0:T(128)S(1)}, u32[]{:S(2)}, u32[]{:S(2)}) collective-permute-start(f32[128]{0:T(128)S(1)} %get-tuple-element.185), channel_id=1, source_target_pairs={{0,80},{16,96},{32,112},{48,128},{64,144},{80,160},{96,176},{112,1... | collective-permute-start | bytes 1544 | tf_op jit(solution)/shard_map/ppermute | solution.py:35
  664.3 33.4 %collective-permute-start.149 = (f32[128]{0:T(128)S(1)}, f32[128]{0:T(128)S(1)}, u32[]{:S(2)}, u32[]{:S(2)}) collective-permute-start(f32[128]{0:T(128)S(1)} %get-tuple-element.185), channel_id=1, source_target_pairs={{0,96},{16,112},{32,128},{48,144},{64,160},{80,176},{96,192},{112,... | collective-permute-start | bytes 1544 | tf_op jit(solution)/shard_map/ppermute | solution.py:35
  666.2 49.2 %collective-permute-start.150 = (f32[128]{0:T(128)S(1)}, f32[128]{0:T(128)S(1)}, u32[]{:S(2)}, u32[]{:S(2)}) collective-permute-start(f32[128]{0:T(128)S(1)} %get-tuple-element.185), channel_id=1, source_target_pairs={{0,112},{16,128},{32,144},{48,160},{64,176},{80,192},{96,208},{112... | collective-permute-start | bytes 1544 | tf_op jit(solution)/shard_map/ppermute | solution.py:35
  673.2 44.2 %collective-permute-start.151 = (f32[128]{0:T(128)S(1)}, f32[128]{0:T(128)S(1)}, u32[]{:S(2)}, u32[]{:S(2)}) collective-permute-start(f32[128]{0:T(128)S(1)} %get-tuple-element.185), channel_id=1, source_target_pairs={{0,128},{16,144},{32,160},{48,176},{64,192},{80,208},{96,224},{112... | collective-permute-start | bytes 1544 | tf_op jit(solution)/shard_map/ppermute | solution.py:35
  693.8 25.5 %collective-permute-start.152 = (f32[128]{0:T(128)S(1)}, f32[128]{0:T(128)S(1)}, u32[]{:S(2)}, u32[]{:S(2)}) collective-permute-start(f32[128]{0:T(128)S(1)} %get-tuple-element.185), channel_id=1, source_target_pairs={{0,144},{16,160},{32,176},{48,192},{64,208},{80,224},{96,240},{112... | collective-permute-start | bytes 1544 | tf_op jit(solution)/shard_map/ppermute | solution.py:35
  695.7 30.6 %collective-permute-start.153 = (f32[128]{0:T(128)S(1)}, f32[128]{0:T(128)S(1)}, u32[]{:S(2)}, u32[]{:S(2)}) collective-permute-start(f32[128]{0:T(128)S(1)} %get-tuple-element.185), channel_id=1, source_target_pairs={{0,160},{16,176},{32,192},{48,208},{64,224},{80,240},{96,256},{112... | collective-permute-start | bytes 1544 | tf_op jit(solution)/shard_map/ppermute | solution.py:35
  697.7 46.1 %collective-permute-start.154 = (f32[128]{0:T(128)S(1)}, f32[128]{0:T(128)S(1)}, u32[]{:S(2)}, u32[]{:S(2)}) collective-permute-start(f32[128]{0:T(128)S(1)} %get-tuple-element.185), channel_id=1, source_target_pairs={{0,176},{16,192},{32,208},{48,224},{64,240},{80,256},{96,272},{112... | collective-permute-start | bytes 1544 | tf_op jit(solution)/shard_map/ppermute | solution.py:35
  715.5 47.3 %collective-permute-start.155 = (f32[128]{0:T(128)S(1)}, f32[128]{0:T(128)S(1)}, u32[]{:S(2)}, u32[]{:S(2)}) collective-permute-start(f32[128]{0:T(128)S(1)} %get-tuple-element.185), channel_id=1, source_target_pairs={{0,192},{16,208},{32,224},{48,240},{64,256},{80,272},{96,288},{112... | collective-permute-start | bytes 1544 | tf_op jit(solution)/shard_map/ppermute | solution.py:35
  717.4 64.4 %collective-permute-start.156 = (f32[128]{0:T(128)S(1)}, f32[128]{0:T(128)S(1)}, u32[]{:S(2)}, u32[]{:S(2)}) collective-permute-start(f32[128]{0:T(128)S(1)} %get-tuple-element.185), channel_id=1, source_target_pairs={{0,208},{16,224},{32,240},{48,256},{64,272},{80,288},{96,304},{112... | collective-permute-start | bytes 1544 | tf_op jit(solution)/shard_map/ppermute | solution.py:35
  719.3 81.5 %collective-permute-start.157 = (f32[128]{0:T(128)S(1)}, f32[128]{0:T(128)S(1)}, u32[]{:S(2)}, u32[]{:S(2)}) collective-permute-start(f32[128]{0:T(128)S(1)} %get-tuple-element.185), channel_id=1, source_target_pairs={{0,224},{16,240},{32,256},{48,272},{64,288},{80,304},{96,320},{112... | collective-permute-start | bytes 1544 | tf_op jit(solution)/shard_map/ppermute | solution.py:35
  726.3 93.6 %collective-permute-start.158 = (f32[128]{0:T(128)S(1)}, f32[128]{0:T(128)S(1)}, u32[]{:S(2)}, u32[]{:S(2)}) collective-permute-start(f32[128]{0:T(128)S(1)} %get-tuple-element.185), channel_id=1, source_target_pairs={{0,240},{16,256},{32,272},{48,288},{64,304},{80,320},{96,336},{112... | collective-permute-start | bytes 1544 | tf_op jit(solution)/shard_map/ppermute | solution.py:35
  743.7 95.1 %collective-permute-start.159 = (f32[128]{0:T(128)S(1)}, f32[128]{0:T(128)S(1)}, u32[]{:S(2)}, u32[]{:S(2)}) collective-permute-start(f32[128]{0:T(128)S(1)} %get-tuple-element.185), channel_id=1, source_target_pairs={{0,256},{16,272},{32,288},{48,304},{64,320},{80,336},{96,352},{112... | collective-permute-start | bytes 1544 | tf_op jit(solution)/shard_map/ppermute | solution.py:35
  762.8 95.1 %collective-permute-start.160 = (f32[128]{0:T(128)S(1)}, f32[128]{0:T(128)S(1)}, u32[]{:S(2)}, u32[]{:S(2)}) collective-permute-start(f32[128]{0:T(128)S(1)} %get-tuple-element.185), channel_id=1, source_target_pairs={{0,272},{16,288},{32,304},{48,320},{64,336},{80,352},{96,368},{112... | collective-permute-start | bytes 1544 | tf_op jit(solution)/shard_map/ppermute | solution.py:35
  781.8 95.1 %collective-permute-start.161 = (f32[128]{0:T(128)S(1)}, f32[128]{0:T(128)S(1)}, u32[]{:S(2)}, u32[]{:S(2)}) collective-permute-start(f32[128]{0:T(128)S(1)} %get-tuple-element.185), channel_id=1, source_target_pairs={{0,288},{16,304},{32,320},{48,336},{64,352},{80,368},{96,384},{112... | collective-permute-start | bytes 1544 | tf_op jit(solution)/shard_map/ppermute | solution.py:35
  800.8 95.1 %collective-permute-start.162 = (f32[128]{0:T(128)S(1)}, f32[128]{0:T(128)S(1)}, u32[]{:S(2)}, u32[]{:S(2)}) collective-permute-start(f32[128]{0:T(128)S(1)} %get-tuple-element.185), channel_id=1, source_target_pairs={{0,304},{16,320},{32,336},{48,352},{64,368},{80,384},{96,400},{112... | collective-permute-start | bytes 1544 | tf_op jit(solution)/shard_map/ppermute | solution.py:35
  819.9 95.1 %collective-permute-start.163 = (f32[128]{0:T(128)S(1)}, f32[128]{0:T(128)S(1)}, u32[]{:S(2)}, u32[]{:S(2)}) collective-permute-start(f32[128]{0:T(128)S(1)} %get-tuple-element.185), channel_id=1, source_target_pairs={{0,320},{16,336},{32,352},{48,368},{64,384},{80,400},{96,416},{112... | collective-permute-start | bytes 1544 | tf_op jit(solution)/shard_map/ppermute | solution.py:35
  838.9 95.1 %collective-permute-start.164 = (f32[128]{0:T(128)S(1)}, f32[128]{0:T(128)S(1)}, u32[]{:S(2)}, u32[]{:S(2)}) collective-permute-start(f32[128]{0:T(128)S(1)} %get-tuple-element.185), channel_id=1, source_target_pairs={{0,336},{16,352},{32,368},{48,384},{64,400},{80,416},{96,432},{112... | collective-permute-start | bytes 1544 | tf_op jit(solution)/shard_map/ppermute | solution.py:35
  857.9 95.1 %collective-permute-start.165 = (f32[128]{0:T(128)S(1)}, f32[128]{0:T(128)S(1)}, u32[]{:S(2)}, u32[]{:S(2)}) collective-permute-start(f32[128]{0:T(128)S(1)} %get-tuple-element.185), channel_id=1, source_target_pairs={{0,352},{16,368},{32,384},{48,400},{64,416},{80,432},{96,448},{112... | collective-permute-start | bytes 1544 | tf_op jit(solution)/shard_map/ppermute | solution.py:35
  876.9 95.1 %collective-permute-start.166 = (f32[128]{0:T(128)S(1)}, f32[128]{0:T(128)S(1)}, u32[]{:S(2)}, u32[]{:S(2)}) collective-permute-start(f32[128]{0:T(128)S(1)} %get-tuple-element.185), channel_id=1, source_target_pairs={{0,368},{16,384},{32,400},{48,416},{64,432},{80,448},{96,464},{112... | collective-permute-start | bytes 1544 | tf_op jit(solution)/shard_map/ppermute | solution.py:35
  896.0 95.1 %collective-permute-start.167 = (f32[128]{0:T(128)S(1)}, f32[128]{0:T(128)S(1)}, u32[]{:S(2)}, u32[]{:S(2)}) collective-permute-start(f32[128]{0:T(128)S(1)} %get-tuple-element.185), channel_id=1, source_target_pairs={{0,384},{16,400},{32,416},{48,432},{64,448},{80,464},{96,480},{112... | collective-permute-start | bytes 1544 | tf_op jit(solution)/shard_map/ppermute | solution.py:35
  915.0 95.1 %collective-permute-start.168 = (f32[128]{0:T(128)S(1)}, f32[128]{0:T(128)S(1)}, u32[]{:S(2)}, u32[]{:S(2)}) collective-permute-start(f32[128]{0:T(128)S(1)} %get-tuple-element.185), channel_id=1, source_target_pairs={{0,400},{16,416},{32,432},{48,448},{64,464},{80,480},{96,496},{112... | collective-permute-start | bytes 1544 | tf_op jit(solution)/shard_map/ppermute | solution.py:35
  934.0 95.1 %collective-permute-start.169 = (f32[128]{0:T(128)S(1)}, f32[128]{0:T(128)S(1)}, u32[]{:S(2)}, u32[]{:S(2)}) collective-permute-start(f32[128]{0:T(128)S(1)} %get-tuple-element.185), channel_id=1, source_target_pairs={{0,416},{16,432},{32,448},{48,464},{64,480},{80,496},{96,0},{112,1... | collective-permute-start | bytes 1544 | tf_op jit(solution)/shard_map/ppermute | solution.py:35
  953.0 97.0 %collective-permute-start.170 = (f32[128]{0:T(128)S(1)}, f32[128]{0:T(128)S(1)}, u32[]{:S(2)}, u32[]{:S(2)}) collective-permute-start(f32[128]{0:T(128)S(1)} %get-tuple-element.185), channel_id=1, source_target_pairs={{0,432},{16,448},{32,464},{48,480},{64,496},{80,0},{96,16},{112,32... | collective-permute-start | bytes 1544 | tf_op jit(solution)/shard_map/ppermute | solution.py:35
  972.1 77.9 %collective-permute-start.171 = (f32[128]{0:T(128)S(1)}, f32[128]{0:T(128)S(1)}, u32[]{:S(2)}, u32[]{:S(2)}) collective-permute-start(f32[128]{0:T(128)S(1)} %get-tuple-element.185), channel_id=1, source_target_pairs={{0,448},{16,464},{32,480},{48,496},{64,0},{80,16},{96,32},{112,48}... | collective-permute-start | bytes 1544 | tf_op jit(solution)/shard_map/ppermute | solution.py:35
  991.1 58.9 %collective-permute-start.172 = (f32[128]{0:T(128)S(1)}, f32[128]{0:T(128)S(1)}, u32[]{:S(2)}, u32[]{:S(2)}) collective-permute-start(f32[128]{0:T(128)S(1)} %get-tuple-element.185), channel_id=1, source_target_pairs={{0,464},{16,480},{32,496},{48,0},{64,16},{80,32},{96,48},{112,64},... | collective-permute-start | bytes 1544 | tf_op jit(solution)/shard_map/ppermute | solution.py:35
  1010.1 39.9 %collective-permute-start.173 = (f32[128]{0:T(128)S(1)}, f32[128]{0:T(128)S(1)}, u32[]{:S(2)}, u32[]{:S(2)}) collective-permute-start(f32[128]{0:T(128)S(1)} %get-tuple-element.185), channel_id=1, source_target_pairs={{0,480},{16,496},{32,0},{48,16},{64,32},{80,48},{96,64},{112,80},{... | collective-permute-start | bytes 1544 | tf_op jit(solution)/shard_map/ppermute | solution.py:35
  1294.7 23.2 %collective-permute-start.247 = (f32[32]{0:T(128)S(1)}, f32[32]{0:T(128)S(1)}, u32[]{:S(2)}, u32[]{:S(2)}) collective-permute-start(f32[32]{0:T(128)S(1)} %gather_fusion.11), channel_id=1, source_target_pairs={{0,1},{1,2},{2,3},{3,4},{4,5},{5,6},{6,7},{7,8},{8,9},{9,10},{10,1... | collective-permute-start | bytes 392 | tf_op jit(solution)/shard_map/ppermute | solution.py:35
  1374.5 23.2 %collective-permute-start.266 = (f32[32]{0:T(128)S(1)}, f32[32]{0:T(128)S(1)}, u32[]{:S(2)}, u32[]{:S(2)}) collective-permute-start(f32[32]{0:T(128)S(1)} %gather_fusion.12), channel_id=1, source_target_pairs={{0,1},{1,2},{2,3},{3,4},{4,5},{5,6},{6,7},{7,8},{8,9},{9,10},{10,1... | collective-permute-start | bytes 392 | tf_op jit(solution)/shard_map/ppermute | solution.py:35
  (322 other events, 6653.0 us)

commit v2 on v1

--- a/solution.py
+++ b/solution.py
@@ -27,23 +27,10 @@
     return x
 
 
-def by_shift(value, axis):
+def gather_all(value, axis):
     devices = lax.axis_size(axis)
-    got = [value]
-    for shift in range(1, devices):
-        pairs = [(a, (a + shift) % devices) for a in range(devices)]
-        got.append(lax.ppermute(value, axis, pairs))
-    return jnp.stack(got)
-
-
-def to_source_order(stacked, axis):
-    devices, position = (lax.axis_size(axis), lax.axis_index(axis))
-    order = (position - jnp.arange(devices, dtype=jnp.int32)) % devices
-    return jnp.take(stacked, order, axis=0)
-
-
-def gather_all(value, axis):
-    return to_source_order(by_shift(value, axis), axis)
+    spread = jnp.broadcast_to(value[None], (devices,) + value.shape)
+    return lax.all_to_all(spread, axis, 0, 0, tiled=False)
 
 
 def sum_all(value, axis):
@@ -83,24 +70,14 @@
 
 def panel_slabs(panel_store, owner, nodes):
     n_plate = lax.axis_size("plate")
-    here = lax.axis_index("plate")
-    mine = here == owner
+    mine = lax.axis_index("plate") == owner
     rows_of = panel_store.reshape(n_plate, nodes, -1)
     cols_of = jnp.swapaxes(panel_store.reshape(-1, n_plate, nodes), 0, 1)
     cols_of = jnp.swapaxes(cols_of, 1, 2)
 
     def fetch(slabs):
-        got = [jnp.where(mine, slabs[here], 0.0)]
-        for shift in range(1, n_plate):
-            pairs = [(a, (a + shift) % n_plate) for a in range(n_plate)]
-            target = (here + shift) % n_plate
-            got.append(lax.ppermute(jnp.where(mine, slabs[target], 0.0), "plate", pairs))
-        total = got[0]
-        for piece in got[1:]:
-            total = total + piece
-        order = (here - jnp.arange(n_plate, dtype=jnp.int32)) % n_plate
-        total = total.reshape(nodes, n_plate, nodes)
-        return jnp.take(total, order, axis=1).reshape(nodes, n_plate * nodes)
+        sent = jnp.where(mine, slabs, 0.0)
+        return jnp.sum(lax.all_to_all(sent, "plate", 0, 0, tiled=False), axis=0)
 
     return fetch(rows_of), fetch(cols_of)
 
@@ -141,7 +118,7 @@
         else:
             result = jnp.dot(scaled, band_tile, precision=HIGH)
         picked = resid.reshape(-1)[places]
-        values = by_shift(picked, "plate").reshape(-1)
+        values = gather_all(picked, "plate").reshape(-1)
         slab = col_slab if transpose else row_slab
         mine = jnp.dot(slab, values, precision=HIGH)
         return result.reshape(-1).at[places].add(mine).reshape(rows, cols)

time: 1600 us -> 530 us (0.33); the launches traced: 1580 us -> 525 us
  starting transfers between devices: 1370 us -> 252 us
  waiting for transfers between devices: 94.1 us -> 147 us
    ppermute x271 -> x0, starting transfers between devices: 1230 us -> none  [the longest x241 1130 us: by_shift(): got.append(lax.ppermute(value, axis, pairs))]
    all_to_all x0 -> x17, starting transfers between devices: none -> 113 us  [the longest x15 102 us: gather_all(): return lax.all_to_all(spread, axis, 0, 0, tiled=False)]
    all_to_all x0 -> x17, waiting for transfers between devices: none -> 83.1 us  [the longest x15 55.7 us: gather_all(): return lax.all_to_all(spread, axis, 0, 0, tiled=False)]
    ppermute x271 -> x0, waiting for transfers between devices: 18.2 us -> none  [the longest x241 16.4 us: by_shift(): got.append(lax.ppermute(value, axis, pairs))]
  transfers between devices with their start and end apart: 315 -> 61, of which waited for: 39 -> 38; matrix products, arithmetic and copies ran while one was open for 2% -> 6% of each run, Pallas kernels for 0% -> 0%
where the time goes in v2:
time: 530 us; the launch traced here: 525 us
  starting transfers between devices  252 us (48%)
  waiting for transfers between devices  147 us (28%)
  other arithmetic  69 us (13%)
  local copies, waits for them, and re-layouts  40.2 us (8%)
  matrix products  13.1 us (2%)
    all_to_all x15, starting transfers between devices, gather_all(): return lax.all_to_all(spread, axis, 0, 0, tiled=False)  102 us
    ppermute x22, starting transfers between devices, with_halo(): after = lax.ppermute(first, axis, down)  84.7 us
    ppermute x22, waiting for transfers between devices, with_halo(): before = lax.ppermute(last, axis, up)  63.9 us
    all_to_all x15, waiting for transfers between devices, gather_all(): return lax.all_to_all(spread, axis, 0, 0, tiled=False)  55.7 us
    ppermute x22, starting transfers between devices, with_halo(): before = lax.ppermute(last, axis, up)  54.9 us
    all_to_all x2, waiting for transfers between devices, fetch(): return jnp.sum(lax.all_to_all(sent, 'plate', 0, 0, tiled=False), axis=0)  27.4 us
    sub x6, other arithmetic, on_device(): resid = load - (diag * new_disp - stiff * neighbours(new_disp))  18.6 us
    mul x5, other arithmetic, on_device(): resid = target - (diag * adjoint - neighbours(stiff * adjoint))  13.8 us
  transfers between devices with their start and end apart: 61, of which 38 were waited for; matrix products, arithmetic and copies ran while one was open for 6% of the time, Pallas kernels for 0%

profile of v2, /device:TPU:7, one launch (start us, length us, event | category | flops | bytes accessed | tf_op | source)
XLA Modules:
  0.0 525.4 jit_solution(8123337127240392901)
XLA Ops:
  1.6 12.0 %collective-permute-start = (f32[1,512]{1,0:T(1,128)S(1)}, f32[1,512]{1,0:T(1,128)S(1)}, u32[]{:S(2)}, u32[]{:S(2)}) collective-permute-start(f32[1,512]{1,0:T(1,128)S(1)} %get-tuple-element.153), channel_id=1, source_target_pairs={{16,0},{32,16},{48,32},{64,48},{80,64},{96,80},{112,96},{128,112},... | collective-permute-start | bytes 6152 | tf_op jit(solution)/shard_map/ppermute | solution.py:25
  15.5 13.8 %while.22 = (s32[]{:T(128)}, f32[8,16,512]{2,1,0:T(8,128)S(1)}, s32[8,16,512]{2,1,0:T(8,128)}, f32[64]{0:T(128)}, s32[]{:T(128)}) while((s32[]{:T(128)}, f32[8,16,512]{2,1,0:T(8,128)S(1)}, s32[8,16,512]{2,1,0:T(8,128)}, f32[64]{0:T(128)}, s32[]{:T(128)}) %tuple.80), condition=%wide.region_2.3_spmd.clone, body=%wide.region_0.2_spmd.clone.sunk | while | flops 1564674 | bytes 196933 | solution.py:54
  44.8 7.8 %all-to-all-start.1 = ((f32[16,1,32]{2,1,0:T(1,128)}), f32[16,1,32]{2,1,0:T(1,128)S(1)}, u32[]{:S(2)}, u32[]{:S(2)}) async-start(f32[16,1,32]{2,1,0:T(1,128)} %broadcast_in_dim.98), calls=%async_computation.1 | async-start | bytes 16384 | tf_op jit(solution)/shard_map/all_to_all | solution.py:33
  56.9 5.4 %all-to-all-start = ((f32[16,32,512]{2,1,0:T(8,128)}), f32[16,32,512]{2,1,0:T(8,128)S(1)}, u32[]{:S(2)}, u32[]{:S(2)}) async-start(f32[16,32,512]{2,1,0:T(8,128)} %bitcast.9), calls=%async_computation | async-start | bytes 2097152 | tf_op jit(solution)/shard_map/all_to_all | solution.py:80
  64.2 12.7 %all-to-all-done = f32[16,32,512]{2,1,0:T(8,128)S(1)} async-done(((f32[16,32,512]{2,1,0:T(8,128)}), f32[16,32,512]{2,1,0:T(8,128)S(1)}, u32[]{:S(2)}, u32[]{:S(2)}) %all-to-all-start) | async-done | bytes 1048608 | tf_op jit(solution)/shard_map/all_to_all | solution.py:80
  78.2 7.6 %collective-permute-start.4 = (f32[1,512]{1,0:T(1,128)S(1)}, f32[1,512]{1,0:T(1,128)S(1)}, u32[]{:S(2)}, u32[]{:S(2)}) collective-permute-start(f32[1,512]{1,0:T(1,128)S(1)} %get-tuple-element.151), channel_id=1, source_target_pairs={{16,0},{32,16},{48,32},{64,48},{80,64},{96,80},{112,96},{128,112},... | collective-permute-start | bytes 6152 | tf_op jit(solution)/shard_map/ppermute | solution.py:25
  87.7 6.0 %collective-permute-done.5 = f32[1,512]{1,0:T(1,128)S(1)} collective-permute-done((f32[1,512]{1,0:T(1,128)S(1)}, f32[1,512]{1,0:T(1,128)S(1)}, u32[]{:S(2)}, u32[]{:S(2)}) %collective-permute-start.5) | collective-permute-done | bytes 2080 | tf_op jit(solution)/shard_map/ppermute | solution.py:24
  105.6 7.6 %all-to-all-start.2 = ((f32[16,1,32]{2,1,0:T(1,128)}), f32[16,1,32]{2,1,0:T(1,128)S(1)}, u32[]{:S(2)}, u32[]{:S(2)}) async-start(f32[16,1,32]{2,1,0:T(1,128)} %broadcast_in_dim.99), calls=%async_computation.2 | async-start | bytes 16384 | tf_op jit(solution)/shard_map/all_to_all | solution.py:33
  124.7 4.9 collective-permute-done.9
  141.5 7.3 %all-to-all-start.3 = ((f32[16,1,32]{2,1,0:T(1,128)}), f32[16,1,32]{2,1,0:T(1,128)S(1)}, u32[]{:S(2)}, u32[]{:S(2)}) async-start(f32[16,1,32]{2,1,0:T(1,128)} %broadcast_in_dim.100), calls=%async_computation.3 | async-start | bytes 16384 | tf_op jit(solution)/shard_map/all_to_all | solution.py:33
  160.2 4.6 collective-permute-done.13
  176.7 7.3 %all-to-all-start.4 = ((f32[16,1,32]{2,1,0:T(1,128)}), f32[16,1,32]{2,1,0:T(1,128)S(1)}, u32[]{:S(2)}, u32[]{:S(2)}) async-start(f32[16,1,32]{2,1,0:T(1,128)} %broadcast_in_dim.101), calls=%async_computation.4 | async-start | bytes 16384 | tf_op jit(solution)/shard_map/all_to_all | solution.py:33
  195.4 4.9 collective-permute-done.17
  212.1 7.3 %all-to-all-start.5 = ((f32[16,1,32]{2,1,0:T(1,128)}), f32[16,1,32]{2,1,0:T(1,128)S(1)}, u32[]{:S(2)}, u32[]{:S(2)}) async-start(f32[16,1,32]{2,1,0:T(1,128)} %broadcast_in_dim.102), calls=%async_computation.5 | async-start | bytes 16384 | tf_op jit(solution)/shard_map/all_to_all | solution.py:33
  230.8 4.6 collective-permute-done.21
  247.3 7.3 %all-to-all-start.6 = ((f32[16,1,32]{2,1,0:T(1,128)}), f32[16,1,32]{2,1,0:T(1,128)S(1)}, u32[]{:S(2)}, u32[]{:S(2)}) async-start(f32[16,1,32]{2,1,0:T(1,128)} %broadcast_in_dim.103), calls=%async_computation.6 | async-start | bytes 16384 | tf_op jit(solution)/shard_map/all_to_all | solution.py:33
  261.4 5.1 all-to-all-start.7
  270.8 5.3 %all-to-all-start.9 = ((f32[16,32,512]{2,1,0:T(8,128)}), f32[16,32,512]{2,1,0:T(8,128)S(1)}, u32[]{:S(2)}, u32[]{:S(2)}) async-start(f32[16,32,512]{2,1,0:T(8,128)} %bitcast.180), calls=%async_computation.9 | async-start | bytes 2097152 | tf_op jit(solution)/shard_map/all_to_all | solution.py:80
  276.1 14.7 %all-to-all-done.9 = f32[16,32,512]{2,1,0:T(8,128)S(1)} async-done(((f32[16,32,512]{2,1,0:T(8,128)}), f32[16,32,512]{2,1,0:T(8,128)S(1)}, u32[]{:S(2)}, u32[]{:S(2)}) %all-to-all-start.9) | async-done | bytes 1048608 | tf_op jit(solution)/shard_map/all_to_all | solution.py:80
  295.9 11.1 %all-to-all-done.8 = f32[32,1,128]{2,1,0:T(1,128)S(1)} async-done(((f32[32,1,128]{2,1,0:T(1,128)}), f32[32,1,128]{2,1,0:T(1,128)S(1)}, u32[]{:S(2)}, u32[]{:S(2)}) %all-to-all-start.8) | async-done | bytes 16416 | tf_op jit(solution)/shard_map/all_to_all | solution.py:33
  309.9 6.7 %all-to-all-start.10 = ((f32[16,1,32]{2,1,0:T(1,128)}), f32[16,1,32]{2,1,0:T(1,128)S(1)}, u32[]{:S(2)}, u32[]{:S(2)}) async-start(f32[16,1,32]{2,1,0:T(1,128)} %broadcast_in_dim.106), calls=%async_computation.10 | async-start | bytes 16384 | tf_op jit(solution)/shard_map/all_to_all | solution.py:33
  325.5 5.1 collective-permute-start.24
  332.6 6.0 %collective-permute-done.25 = f32[1,512]{1,0:T(1,128)S(1)} collective-permute-done((f32[1,512]{1,0:T(1,128)S(1)}, f32[1,512]{1,0:T(1,128)S(1)}, u32[]{:S(2)}, u32[]{:S(2)}) %collective-permute-start.25) | collective-permute-done | bytes 2080 | tf_op jit(solution)/shard_map/ppermute | solution.py:24
  347.8 7.2 %all-to-all-start.11 = ((f32[16,1,32]{2,1,0:T(1,128)}), f32[16,1,32]{2,1,0:T(1,128)S(1)}, u32[]{:S(2)}, u32[]{:S(2)}) async-start(f32[16,1,32]{2,1,0:T(1,128)} %broadcast_in_dim.107), calls=%async_computation.11 | async-start | bytes 16384 | tf_op jit(solution)/shard_map/all_to_all | solution.py:33
  382.9 7.5 %all-to-all-start.12 = ((f32[16,1,32]{2,1,0:T(1,128)}), f32[16,1,32]{2,1,0:T(1,128)S(1)}, u32[]{:S(2)}, u32[]{:S(2)}) async-start(f32[16,1,32]{2,1,0:T(1,128)} %broadcast_in_dim.108), calls=%async_computation.12 | async-start | bytes 16384 | tf_op jit(solution)/shard_map/all_to_all | solution.py:33
  404.7 4.9 collective-permute-done.33
  418.9 7.3 %all-to-all-start.13 = ((f32[16,1,32]{2,1,0:T(1,128)}), f32[16,1,32]{2,1,0:T(1,128)S(1)}, u32[]{:S(2)}, u32[]{:S(2)}) async-start(f32[16,1,32]{2,1,0:T(1,128)} %broadcast_in_dim.109), calls=%async_computation.13 | async-start | bytes 16384 | tf_op jit(solution)/shard_map/all_to_all | solution.py:33
  454.2 7.3 %all-to-all-start.14 = ((f32[16,1,32]{2,1,0:T(1,128)}), f32[16,1,32]{2,1,0:T(1,128)S(1)}, u32[]{:S(2)}, u32[]{:S(2)}) async-start(f32[16,1,32]{2,1,0:T(1,128)} %broadcast_in_dim.110), calls=%async_computation.14 | async-start | bytes 16384 | tf_op jit(solution)/shard_map/all_to_all | solution.py:33
  475.6 4.9 collective-permute-done.41
  489.7 7.3 %all-to-all-start.15 = ((f32[16,1,32]{2,1,0:T(1,128)}), f32[16,1,32]{2,1,0:T(1,128)S(1)}, u32[]{:S(2)}, u32[]{:S(2)}) async-start(f32[16,1,32]{2,1,0:T(1,128)} %broadcast_in_dim.111), calls=%async_computation.15 | async-start | bytes 16384 | tf_op jit(solution)/shard_map/all_to_all | solution.py:33
  503.8 11.0 %while.23 = (s32[]{:T(128)}, f32[8,64]{1,0:T(8,128)S(1)}, s32[8,16,512]{2,1,0:T(8,128)}, f32[8,16,512]{2,1,0:T(8,128)S(1)}, s32[]{:T(128)}, /*index=5*/s32[]{:T(128)}) while((s32[]{:T(128)}, f32[8,64]{1,0:T(8,128)S(1)}, s32[8,16,512]{2,1,0:T(8,128)}, f32[8,16,512]{2,1,0:T(8,128)S(1)}, s32[]{:T(128)}, /*index=5*/s32[]{:T(128)}) %tuple.81), condition=%wide.region_25.26_spmd.clone, body=%wide.region_23.25_spmd.clone.sunk | while | flops 1572802 | bytes 197457 | solution.py:65
  515.5 5.0 all-to-all-start.16
  (375 shorter events, 309.6 us)
Async XLA Ops:
  1.6 29.1 %collective-permute-start = (f32[1,512]{1,0:T(1,128)S(1)}, f32[1,512]{1,0:T(1,128)S(1)}, u32[]{:S(2)}, u32[]{:S(2)}) collective-permute-start(f32[1,512]{1,0:T(1,128)S(1)} %get-tuple-element.153), channel_id=1, source_target_pairs={{16,0},{32,16},{48,32},{64,48},{80,64},{96,80},{112,96},{128,112},... | collective-permute-start | bytes 6152 | tf_op jit(solution)/shard_map/ppermute | solution.py:25
  13.5 17.2 %collective-permute-start.1 = (f32[1,512]{1,0:T(1,128)S(1)}, f32[1,512]{1,0:T(1,128)S(1)}, u32[]{:S(2)}, u32[]{:S(2)}) collective-permute-start(f32[1,512]{1,0:T(1,128)S(1)} %get-tuple-element.152), channel_id=1, source_target_pairs={{0,16},{16,32},{32,48},{48,64},{64,80},{80,96},{96,112},{112,128},... | collective-permute-start | bytes 6152 | tf_op jit(solution)/shard_map/ppermute | solution.py:24
  31.3 6.6 %collective-permute-start.2 = (f32[130,1]{1,0:T(8,128)S(1)}, f32[130,1]{1,0:T(8,128)S(1)}, u32[]{:S(2)}, u32[]{:S(2)}) collective-permute-start(f32[130,1]{1,0:T(8,128)S(1)} %get-tuple-element.130), channel_id=1, source_target_pairs={{1,0},{2,1},{3,2},{4,3},{5,4},{6,5},{7,6},{8,7},{9,8},{10,9},{11,1... | collective-permute-start | bytes 1568 | tf_op jit(solution)/shard_map/ppermute | solution.py:25
  44.8 12.1 %all-to-all-start.1 = ((f32[16,1,32]{2,1,0:T(1,128)}), f32[16,1,32]{2,1,0:T(1,128)S(1)}, u32[]{:S(2)}, u32[]{:S(2)}) async-start(f32[16,1,32]{2,1,0:T(1,128)} %broadcast_in_dim.98), calls=%async_computation.1 | async-start | bytes 16384 | tf_op jit(solution)/shard_map/all_to_all | solution.py:33
  56.9 20.1 %all-to-all-start = ((f32[16,32,512]{2,1,0:T(8,128)}), f32[16,32,512]{2,1,0:T(8,128)S(1)}, u32[]{:S(2)}, u32[]{:S(2)}) async-start(f32[16,32,512]{2,1,0:T(8,128)} %bitcast.9), calls=%async_computation | async-start | bytes 2097152 | tf_op jit(solution)/shard_map/all_to_all | solution.py:80
  78.2 9.5 %collective-permute-start.4 = (f32[1,512]{1,0:T(1,128)S(1)}, f32[1,512]{1,0:T(1,128)S(1)}, u32[]{:S(2)}, u32[]{:S(2)}) collective-permute-start(f32[1,512]{1,0:T(1,128)S(1)} %get-tuple-element.151), channel_id=1, source_target_pairs={{16,0},{32,16},{48,32},{64,48},{80,64},{96,80},{112,96},{128,112},... | collective-permute-start | bytes 6152 | tf_op jit(solution)/shard_map/ppermute | solution.py:25
  85.8 7.9 %collective-permute-start.5 = (f32[1,512]{1,0:T(1,128)S(1)}, f32[1,512]{1,0:T(1,128)S(1)}, u32[]{:S(2)}, u32[]{:S(2)}) collective-permute-start(f32[1,512]{1,0:T(1,128)S(1)} %get-tuple-element.150), channel_id=1, source_target_pairs={{0,16},{16,32},{32,48},{48,64},{64,80},{80,96},{96,112},{112,128},... | collective-permute-start | bytes 6152 | tf_op jit(solution)/shard_map/ppermute | solution.py:24
  105.6 12.0 %all-to-all-start.2 = ((f32[16,1,32]{2,1,0:T(1,128)}), f32[16,1,32]{2,1,0:T(1,128)S(1)}, u32[]{:S(2)}, u32[]{:S(2)}) async-start(f32[16,1,32]{2,1,0:T(1,128)} %broadcast_in_dim.99), calls=%async_computation.2 | async-start | bytes 16384 | tf_op jit(solution)/shard_map/all_to_all | solution.py:33
  121.7 7.9 %collective-permute-start.9 = (f32[1,512]{1,0:T(1,128)S(1)}, f32[1,512]{1,0:T(1,128)S(1)}, u32[]{:S(2)}, u32[]{:S(2)}) collective-permute-start(f32[1,512]{1,0:T(1,128)S(1)} %get-tuple-element.148), channel_id=1, source_target_pairs={{0,16},{16,32},{32,48},{48,64},{64,80},{80,96},{96,112},{112,128},... | collective-permute-start | bytes 6152 | tf_op jit(solution)/shard_map/ppermute | solution.py:24
  141.5 11.6 %all-to-all-start.3 = ((f32[16,1,32]{2,1,0:T(1,128)}), f32[16,1,32]{2,1,0:T(1,128)S(1)}, u32[]{:S(2)}, u32[]{:S(2)}) async-start(f32[16,1,32]{2,1,0:T(1,128)} %broadcast_in_dim.100), calls=%async_computation.3 | async-start | bytes 16384 | tf_op jit(solution)/shard_map/all_to_all | solution.py:33
  156.9 7.9 %collective-permute-start.13 = (f32[1,512]{1,0:T(1,128)S(1)}, f32[1,512]{1,0:T(1,128)S(1)}, u32[]{:S(2)}, u32[]{:S(2)}) collective-permute-start(f32[1,512]{1,0:T(1,128)S(1)} %get-tuple-element.146), channel_id=1, source_target_pairs={{0,16},{16,32},{32,48},{48,64},{64,80},{80,96},{96,112},{112,128},... | collective-permute-start | bytes 6152 | tf_op jit(solution)/shard_map/ppermute | solution.py:24
  176.7 11.6 %all-to-all-start.4 = ((f32[16,1,32]{2,1,0:T(1,128)}), f32[16,1,32]{2,1,0:T(1,128)S(1)}, u32[]{:S(2)}, u32[]{:S(2)}) async-start(f32[16,1,32]{2,1,0:T(1,128)} %broadcast_in_dim.101), calls=%async_computation.4 | async-start | bytes 16384 | tf_op jit(solution)/shard_map/all_to_all | solution.py:33
  192.3 7.9 %collective-permute-start.17 = (f32[1,512]{1,0:T(1,128)S(1)}, f32[1,512]{1,0:T(1,128)S(1)}, u32[]{:S(2)}, u32[]{:S(2)}) collective-permute-start(f32[1,512]{1,0:T(1,128)S(1)} %get-tuple-element.144), channel_id=1, source_target_pairs={{0,16},{16,32},{32,48},{48,64},{64,80},{80,96},{96,112},{112,128},... | collective-permute-start | bytes 6152 | tf_op jit(solution)/shard_map/ppermute | solution.py:24
  212.1 11.6 %all-to-all-start.5 = ((f32[16,1,32]{2,1,0:T(1,128)}), f32[16,1,32]{2,1,0:T(1,128)S(1)}, u32[]{:S(2)}, u32[]{:S(2)}) async-start(f32[16,1,32]{2,1,0:T(1,128)} %broadcast_in_dim.102), calls=%async_computation.5 | async-start | bytes 16384 | tf_op jit(solution)/shard_map/all_to_all | solution.py:33
  227.5 7.9 %collective-permute-start.21 = (f32[1,512]{1,0:T(1,128)S(1)}, f32[1,512]{1,0:T(1,128)S(1)}, u32[]{:S(2)}, u32[]{:S(2)}) collective-permute-start(f32[1,512]{1,0:T(1,128)S(1)} %get-tuple-element.142), channel_id=1, source_target_pairs={{0,16},{16,32},{32,48},{48,64},{64,80},{80,96},{96,112},{112,128},... | collective-permute-start | bytes 6152 | tf_op jit(solution)/shard_map/ppermute | solution.py:24
  247.3 11.6 %all-to-all-start.6 = ((f32[16,1,32]{2,1,0:T(1,128)}), f32[16,1,32]{2,1,0:T(1,128)S(1)}, u32[]{:S(2)}, u32[]{:S(2)}) async-start(f32[16,1,32]{2,1,0:T(1,128)} %broadcast_in_dim.103), calls=%async_computation.6 | async-start | bytes 16384 | tf_op jit(solution)/shard_map/all_to_all | solution.py:33
  261.4 9.4 %all-to-all-start.7 = ((f32[16,1,128]{2,1,0:T(1,128)}), f32[16,1,128]{2,1,0:T(1,128)S(1)}, u32[]{:S(2)}, u32[]{:S(2)}) async-start(f32[16,1,128]{2,1,0:T(1,128)} %broadcast_in_dim.104), calls=%async_computation.7 | async-start | bytes 16384 | tf_op jit(solution)/shard_map/all_to_all | solution.py:33
  270.8 20.0 %all-to-all-start.9 = ((f32[16,32,512]{2,1,0:T(8,128)}), f32[16,32,512]{2,1,0:T(8,128)S(1)}, u32[]{:S(2)}, u32[]{:S(2)}) async-start(f32[16,32,512]{2,1,0:T(8,128)} %bitcast.180), calls=%async_computation.9 | async-start | bytes 2097152 | tf_op jit(solution)/shard_map/all_to_all | solution.py:80
  291.4 15.6 %all-to-all-start.8 = ((f32[32,1,128]{2,1,0:T(1,128)}), f32[32,1,128]{2,1,0:T(1,128)S(1)}, u32[]{:S(2)}, u32[]{:S(2)}) async-start(f32[32,1,128]{2,1,0:T(1,128)} %broadcast_in_dim.105), calls=%async_computation.8 | async-start | bytes 32768 | tf_op jit(solution)/shard_map/all_to_all | solution.py:33
  309.9 11.1 %all-to-all-start.10 = ((f32[16,1,32]{2,1,0:T(1,128)}), f32[16,1,32]{2,1,0:T(1,128)S(1)}, u32[]{:S(2)}, u32[]{:S(2)}) async-start(f32[16,1,32]{2,1,0:T(1,128)} %broadcast_in_dim.106), calls=%async_computation.10 | async-start | bytes 16384 | tf_op jit(solution)/shard_map/all_to_all | solution.py:33
  325.5 7.1 %collective-permute-start.24 = (f32[1,512]{1,0:T(1,128)S(1)}, f32[1,512]{1,0:T(1,128)S(1)}, u32[]{:S(2)}, u32[]{:S(2)}) collective-permute-start(f32[1,512]{1,0:T(1,128)S(1)} %get-tuple-element.141), channel_id=1, source_target_pairs={{16,0},{32,16},{48,32},{64,48},{80,64},{96,80},{112,96},{128,112},... | collective-permute-start | bytes 6152 | tf_op jit(solution)/shard_map/ppermute | solution.py:25
  330.7 7.9 %collective-permute-start.25 = (f32[1,512]{1,0:T(1,128)S(1)}, f32[1,512]{1,0:T(1,128)S(1)}, u32[]{:S(2)}, u32[]{:S(2)}) collective-permute-start(f32[1,512]{1,0:T(1,128)S(1)} %get-tuple-element.140), channel_id=1, source_target_pairs={{0,16},{16,32},{32,48},{48,64},{64,80},{80,96},{96,112},{112,128},... | collective-permute-start | bytes 6152 | tf_op jit(solution)/shard_map/ppermute | solution.py:24
  347.8 11.6 %all-to-all-start.11 = ((f32[16,1,32]{2,1,0:T(1,128)}), f32[16,1,32]{2,1,0:T(1,128)S(1)}, u32[]{:S(2)}, u32[]{:S(2)}) async-start(f32[16,1,32]{2,1,0:T(1,128)} %broadcast_in_dim.107), calls=%async_computation.11 | async-start | bytes 16384 | tf_op jit(solution)/shard_map/all_to_all | solution.py:33
  365.9 7.9 %collective-permute-start.29 = (f32[1,512]{1,0:T(1,128)S(1)}, f32[1,512]{1,0:T(1,128)S(1)}, u32[]{:S(2)}, u32[]{:S(2)}) collective-permute-start(f32[1,512]{1,0:T(1,128)S(1)} %get-tuple-element.138), channel_id=1, source_target_pairs={{0,16},{16,32},{32,48},{48,64},{64,80},{80,96},{96,112},{112,128},... | collective-permute-start | bytes 6152 | tf_op jit(solution)/shard_map/ppermute | solution.py:24
  382.9 11.8 %all-to-all-start.12 = ((f32[16,1,32]{2,1,0:T(1,128)}), f32[16,1,32]{2,1,0:T(1,128)S(1)}, u32[]{:S(2)}, u32[]{:S(2)}) async-start(f32[16,1,32]{2,1,0:T(1,128)} %broadcast_in_dim.108), calls=%async_computation.12 | async-start | bytes 16384 | tf_op jit(solution)/shard_map/all_to_all | solution.py:33
  401.7 7.9 %collective-permute-start.33 = (f32[1,512]{1,0:T(1,128)S(1)}, f32[1,512]{1,0:T(1,128)S(1)}, u32[]{:S(2)}, u32[]{:S(2)}) collective-permute-start(f32[1,512]{1,0:T(1,128)S(1)} %get-tuple-element.136), channel_id=1, source_target_pairs={{0,16},{16,32},{32,48},{48,64},{64,80},{80,96},{96,112},{112,128},... | collective-permute-start | bytes 6152 | tf_op jit(solution)/shard_map/ppermute | solution.py:24
  418.9 11.6 %all-to-all-start.13 = ((f32[16,1,32]{2,1,0:T(1,128)}), f32[16,1,32]{2,1,0:T(1,128)S(1)}, u32[]{:S(2)}, u32[]{:S(2)}) async-start(f32[16,1,32]{2,1,0:T(1,128)} %broadcast_in_dim.109), calls=%async_computation.13 | async-start | bytes 16384 | tf_op jit(solution)/shard_map/all_to_all | solution.py:33
  437.0 7.9 %collective-permute-start.37 = (f32[1,512]{1,0:T(1,128)S(1)}, f32[1,512]{1,0:T(1,128)S(1)}, u32[]{:S(2)}, u32[]{:S(2)}) collective-permute-start(f32[1,512]{1,0:T(1,128)S(1)} %get-tuple-element.134), channel_id=1, source_target_pairs={{0,16},{16,32},{32,48},{48,64},{64,80},{80,96},{96,112},{112,128},... | collective-permute-start | bytes 6152 | tf_op jit(solution)/shard_map/ppermute | solution.py:24
  454.2 11.6 %all-to-all-start.14 = ((f32[16,1,32]{2,1,0:T(1,128)}), f32[16,1,32]{2,1,0:T(1,128)S(1)}, u32[]{:S(2)}, u32[]{:S(2)}) async-start(f32[16,1,32]{2,1,0:T(1,128)} %broadcast_in_dim.110), calls=%async_computation.14 | async-start | bytes 16384 | tf_op jit(solution)/shard_map/all_to_all | solution.py:33
  472.5 7.9 %collective-permute-start.41 = (f32[1,512]{1,0:T(1,128)S(1)}, f32[1,512]{1,0:T(1,128)S(1)}, u32[]{:S(2)}, u32[]{:S(2)}) collective-permute-start(f32[1,512]{1,0:T(1,128)S(1)} %get-tuple-element.132), channel_id=1, source_target_pairs={{0,16},{16,32},{32,48},{48,64},{64,80},{80,96},{96,112},{112,128},... | collective-permute-start | bytes 6152 | tf_op jit(solution)/shard_map/ppermute | solution.py:24
  489.7 11.6 %all-to-all-start.15 = ((f32[16,1,32]{2,1,0:T(1,128)}), f32[16,1,32]{2,1,0:T(1,128)S(1)}, u32[]{:S(2)}, u32[]{:S(2)}) async-start(f32[16,1,32]{2,1,0:T(1,128)} %broadcast_in_dim.111), calls=%async_computation.15 | async-start | bytes 16384 | tf_op jit(solution)/shard_map/all_to_all | solution.py:33
  515.5 9.4 %all-to-all-start.16 = ((f32[16,1,64]{2,1,0:T(1,128)}), f32[16,1,64]{2,1,0:T(1,128)S(1)}, u32[]{:S(2)}, u32[]{:S(2)}) async-start(f32[16,1,64]{2,1,0:T(1,128)} %broadcast_in_dim.121), calls=%async_computation.16 | async-start | bytes 16384 | tf_op jit(solution)/shard_map/all_to_all | solution.py:33
  (43 other events, 678.9 us)

commit v3 on v2

--- a/solution.py
+++ b/solution.py
@@ -14,17 +14,15 @@
 HIGH = lax.Precision.HIGHEST
 
 
-def with_halo(x, sides, width):
-    for axis, dim in sides:
-        devices, length = (lax.axis_size(axis), x.shape[dim])
-        up = [(i, (i + 1) % devices) for i in range(devices - 1)]
-        down = [(j, i) for i, j in up]
-        last = lax.slice_in_dim(x, length - width, length, axis=dim)
-        first = lax.slice_in_dim(x, 0, width, axis=dim)
-        before = lax.ppermute(last, axis, up)
-        after = lax.ppermute(first, axis, down)
-        x = jnp.concatenate([before, x, after], axis=dim)
-    return x
+def shifted(x, axis, dim, toward):
+    devices, length = (lax.axis_size(axis), x.shape[dim])
+    if toward > 0:
+        pairs = [(i, i + 1) for i in range(devices - 1)]
+        edge = lax.slice_in_dim(x, length - 1, length, axis=dim)
+    else:
+        pairs = [(i + 1, i) for i in range(devices - 1)]
+        edge = lax.slice_in_dim(x, 0, 1, axis=dim)
+    return lax.ppermute(edge, axis, pairs)
 
 
 def gather_all(value, axis):
@@ -38,8 +36,13 @@
 
 
 def neighbours(field):
-    padded = with_halo(field, (("storey", 0), ("plate", 1)), 1)
-    return padded[2:, 1:-1] + padded[:-2, 1:-1] + padded[1:-1, 2:] + padded[1:-1, :-2]
+    above = shifted(field, "storey", 0, 1)
+    below = shifted(field, "storey", 0, -1)
+    left = shifted(field, "plate", 1, 1)
+    right = shifted(field, "plate", 1, -1)
+    vertical = jnp.concatenate([above, field[:-1]], axis=0) + jnp.concatenate([field[1:], below], axis=0)
+    horizontal = jnp.concatenate([left, field[:, :-1]], axis=1) + jnp.concatenate([field[:, 1:], right], axis=1)
+    return vertical + horizontal
 
 
 def damper_lookup(ids, coef):
@@ -75,11 +78,10 @@
     cols_of = jnp.swapaxes(panel_store.reshape(-1, n_plate, nodes), 0, 1)
     cols_of = jnp.swapaxes(cols_of, 1, 2)
 
-    def fetch(slabs):
-        sent = jnp.where(mine, slabs, 0.0)
-        return jnp.sum(lax.all_to_all(sent, "plate", 0, 0, tiled=False), axis=0)
-
-    return fetch(rows_of), fetch(cols_of)
+    both = jnp.concatenate([rows_of, cols_of], axis=1)
+    sent = jnp.where(mine, both, 0.0)
+    got = jnp.sum(lax.all_to_all(sent, "plate", 0, 0, tiled=False), axis=0)
+    return got[:nodes], got[nodes:]
 
 
 def on_device(

time: 530 us -> 493 us (0.930)
  waiting for transfers between devices: 147 us -> 83.3 us
  starting transfers between devices: 252 us -> 268 us
  blocking collectives: 0 us -> 8.6 us
  local copies, waits for them, and re-layouts: 40.2 us -> 48 us
    ppermute x44, waiting for transfers between devices: 64.4 us -> 6.23 us  [shifted(): return lax.ppermute(edge, axis, pairs)]
    ppermute x44, starting transfers between devices: 140 us -> 161 us  [shifted(): return lax.ppermute(edge, axis, pairs)]
    all_to_all x0 -> x1, blocking collectives: none -> 8.6 us  [gather_all(): return lax.all_to_all(spread, axis, 0, 0, tiled=False)]
    slice x12 -> x45, local copies, waits for them, and re-layouts: 1.01 us -> 9.54 us  [the longest x22 3.94 us: shifted(): edge = lax.slice_in_dim(x, 0, 1, axis=dim)]
    all_to_all x2 -> x1, starting transfers between devices: 10.7 us -> 5.97 us  [panel_slabs(): got = jnp.sum(lax.all_to_all(sent, 'plate', 0, 0, tiled=False), axis=0)]
    all_to_all x15 -> x14, waiting for transfers between devices: 55.7 us -> 52.3 us  [gather_all(): return lax.all_to_all(spread, axis, 0, 0, tiled=False)]
    all_to_all x2 -> x1, waiting for transfers between devices: 27.4 us -> 24.7 us  [panel_slabs(): got = jnp.sum(lax.all_to_all(sent, 'plate', 0, 0, tiled=False), axis=0)]
    all_to_all x15 -> x14, starting transfers between devices: 102 us -> 101 us  [gather_all(): return lax.all_to_all(spread, axis, 0, 0, tiled=False)]
  transfers between devices with their start and end apart: 61 -> 59, of which waited for: 38 -> 25; matrix products, arithmetic and copies ran while one was open for 6% -> 7% of each run, Pallas kernels for 0% -> 0%
where the time goes in v3:
time: 493 us; the launch traced here: 489 us
  starting transfers between devices  268 us (54%)
  waiting for transfers between devices  83.3 us (17%)
  other arithmetic  64.6 us (13%)
  local copies, waits for them, and re-layouts  48 us (10%)
  matrix products  13 us (3%)
  blocking collectives  8.6 us (2%)
    ppermute x44, starting transfers between devices, shifted(): return lax.ppermute(edge, axis, pairs)  161 us
    all_to_all x14, starting transfers between devices, gather_all(): return lax.all_to_all(spread, axis, 0, 0, tiled=False)  101 us
    all_to_all x14, waiting for transfers between devices, gather_all(): return lax.all_to_all(spread, axis, 0, 0, tiled=False)  52.3 us
    all_to_all x1, waiting for transfers between devices, panel_slabs(): got = jnp.sum(lax.all_to_all(sent, 'plate', 0, 0, tiled=False), axis=0)  24.7 us
    sub x6, other arithmetic, on_device(): resid = load - (diag * new_disp - stiff * neighbours(new_disp))  18 us
    mul x5, other arithmetic, on_device(): resid = target - (diag * adjoint - neighbours(stiff * adjoint))  13.3 us
    scatter-add x12, other arithmetic, correct(): return result.reshape(-1).at[places].add(mine).reshape(rows, cols)  10.7 us
  transfers between devices with their start and end apart: 59, of which 25 were waited for; matrix products, arithmetic and copies ran while one was open for 7% of the time, Pallas kernels for 0%

profile of v3, /device:TPU:7, one launch (start us, length us, event | category | flops | bytes accessed | tf_op | source)
XLA Modules:
  0.0 488.8 jit_solution(16162339772809410566)
XLA Ops:
  13.0 10.3 %collective-permute-start.1 = (f32[1,512]{1,0:T(1,128)}, f32[1,512]{1,0:T(1,128)S(1)}, u32[]{:S(2)}, u32[]{:S(2)}) collective-permute-start(f32[1,512]{1,0:T(1,128)} %get-tuple-element.196), channel_id=1, source_target_pairs={{16,0},{32,16},{48,32},{64,48},{80,64},{96,80},{112,96},{128,112},... | collective-permute-start | bytes 6152 | tf_op jit(solution)/shard_map/ppermute | solution.py:25
  27.8 8.6 %while.22 = (s32[]{:T(128)}, f32[8,16,512]{2,1,0:T(8,128)S(1)}, s32[8,16,512]{2,1,0:T(8,128)}, f32[64]{0:T(128)S(1)}, s32[]{:T(128)}) while((s32[]{:T(128)}, f32[8,16,512]{2,1,0:T(8,128)S(1)}, s32[8,16,512]{2,1,0:T(8,128)}, f32[64]{0:T(128)S(1)}, s32[]{:T(128)}) %tuple.104), condition=%wide.region_2.3_spmd.clone, body=%wide.region_0.2_spmd.clone.sunk | while | flops 1564674 | bytes 196933 | solution.py:57
  39.2 4.1 fusion.7
  47.0 6.4 %all-to-all-start.1 = ((f32[16,1,32]{2,1,0:T(1,128)}), f32[16,1,32]{2,1,0:T(1,128)S(1)}, u32[]{:S(2)}, u32[]{:S(2)}) async-start(f32[16,1,32]{2,1,0:T(1,128)} %broadcast_in_dim.97), calls=%async_computation.1 | async-start | bytes 16384 | tf_op jit(solution)/shard_map/all_to_all | solution.py:31
  57.7 6.0 %all-to-all-start = ((f32[16,64,512]{2,1,0:T(8,128)}), f32[16,64,512]{2,1,0:T(8,128)}, u32[]{:S(2)}, u32[]{:S(2)}) async-start(f32[16,64,512]{2,1,0:T(8,128)} %maximum_select_fusion), calls=%async_computation | async-start | bytes 4194304 | tf_op jit(solution)/shard_map/all_to_all | solution.py:83
  65.7 24.7 %all-to-all-done = f32[16,64,512]{2,1,0:T(8,128)} async-done(((f32[16,64,512]{2,1,0:T(8,128)}), f32[16,64,512]{2,1,0:T(8,128)}, u32[]{:S(2)}, u32[]{:S(2)}) %all-to-all-start) | async-done | bytes 2097184 | tf_op jit(solution)/shard_map/all_to_all | solution.py:83
  101.2 7.0 %collective-permute-start.5 = (f32[1,512]{1,0:T(1,128)S(1)}, f32[1,512]{1,0:T(1,128)S(1)}, u32[]{:S(2)}, u32[]{:S(2)}) collective-permute-start(f32[1,512]{1,0:T(1,128)S(1)} %get-tuple-element.188), channel_id=1, source_target_pairs={{16,0},{32,16},{48,32},{64,48},{80,64},{96,80},{112,96},{128,112},... | collective-permute-start | bytes 6152 | tf_op jit(solution)/shard_map/ppermute | solution.py:25
  113.1 8.4 %all-to-all-start.2 = ((f32[16,1,32]{2,1,0:T(1,128)}), f32[16,1,32]{2,1,0:T(1,128)S(1)}, u32[]{:S(2)}, u32[]{:S(2)}) async-start(f32[16,1,32]{2,1,0:T(1,128)} %broadcast_in_dim.98), calls=%async_computation.2 | async-start | bytes 16384 | tf_op jit(solution)/shard_map/all_to_all | solution.py:31
  134.5 8.0 %collective-permute-start.9 = (f32[1,512]{1,0:T(1,128)S(1)}, f32[1,512]{1,0:T(1,128)S(1)}, u32[]{:S(2)}, u32[]{:S(2)}) collective-permute-start(f32[1,512]{1,0:T(1,128)S(1)} %get-tuple-element.180), channel_id=1, source_target_pairs={{16,0},{32,16},{48,32},{64,48},{80,64},{96,80},{112,96},{128,112},... | collective-permute-start | bytes 6152 | tf_op jit(solution)/shard_map/ppermute | solution.py:25
  147.3 7.5 %all-to-all-start.3 = ((f32[16,1,32]{2,1,0:T(1,128)}), f32[16,1,32]{2,1,0:T(1,128)S(1)}, u32[]{:S(2)}, u32[]{:S(2)}) async-start(f32[16,1,32]{2,1,0:T(1,128)} %broadcast_in_dim.99), calls=%async_computation.3 | async-start | bytes 16384 | tf_op jit(solution)/shard_map/all_to_all | solution.py:31
  167.8 7.5 %collective-permute-start.13 = (f32[1,512]{1,0:T(1,128)S(1)}, f32[1,512]{1,0:T(1,128)S(1)}, u32[]{:S(2)}, u32[]{:S(2)}) collective-permute-start(f32[1,512]{1,0:T(1,128)S(1)} %get-tuple-element.172), channel_id=1, source_target_pairs={{16,0},{32,16},{48,32},{64,48},{80,64},{96,80},{112,96},{128,112},... | collective-permute-start | bytes 6152 | tf_op jit(solution)/shard_map/ppermute | solution.py:25
  180.2 7.5 %all-to-all-start.4 = ((f32[16,1,32]{2,1,0:T(1,128)}), f32[16,1,32]{2,1,0:T(1,128)S(1)}, u32[]{:S(2)}, u32[]{:S(2)}) async-start(f32[16,1,32]{2,1,0:T(1,128)} %broadcast_in_dim.100), calls=%async_computation.4 | async-start | bytes 16384 | tf_op jit(solution)/shard_map/all_to_all | solution.py:31
  200.6 7.7 %collective-permute-start.17 = (f32[1,512]{1,0:T(1,128)S(1)}, f32[1,512]{1,0:T(1,128)S(1)}, u32[]{:S(2)}, u32[]{:S(2)}) collective-permute-start(f32[1,512]{1,0:T(1,128)S(1)} %get-tuple-element.164), channel_id=1, source_target_pairs={{16,0},{32,16},{48,32},{64,48},{80,64},{96,80},{112,96},{128,112},... | collective-permute-start | bytes 6152 | tf_op jit(solution)/shard_map/ppermute | solution.py:25
  213.0 7.5 %all-to-all-start.5 = ((f32[16,1,32]{2,1,0:T(1,128)}), f32[16,1,32]{2,1,0:T(1,128)S(1)}, u32[]{:S(2)}, u32[]{:S(2)}) async-start(f32[16,1,32]{2,1,0:T(1,128)} %broadcast_in_dim.101), calls=%async_computation.5 | async-start | bytes 16384 | tf_op jit(solution)/shard_map/all_to_all | solution.py:31
  233.4 7.5 %collective-permute-start.21 = (f32[1,512]{1,0:T(1,128)S(1)}, f32[1,512]{1,0:T(1,128)S(1)}, u32[]{:S(2)}, u32[]{:S(2)}) collective-permute-start(f32[1,512]{1,0:T(1,128)S(1)} %get-tuple-element.156), channel_id=1, source_target_pairs={{16,0},{32,16},{48,32},{64,48},{80,64},{96,80},{112,96},{128,112},... | collective-permute-start | bytes 6152 | tf_op jit(solution)/shard_map/ppermute | solution.py:25
  245.8 7.5 %all-to-all-start.6 = ((f32[16,1,32]{2,1,0:T(1,128)}), f32[16,1,32]{2,1,0:T(1,128)S(1)}, u32[]{:S(2)}, u32[]{:S(2)}) async-start(f32[16,1,32]{2,1,0:T(1,128)} %broadcast_in_dim.102), calls=%async_computation.6 | async-start | bytes 16384 | tf_op jit(solution)/shard_map/all_to_all | solution.py:31
  259.5 8.6 %all_to_all.95 = f32[16,1,128]{2,1,0:T(1,128)S(1)} all-to-all(f32[16,1,128]{2,1,0:T(1,128)S(1)} %broadcast_in_dim.103), channel_id=1, replica_groups=mesh['storey'=32,'plate'=16] {'plate'}, dimensions={0} | all-to-all | bytes 16384 | tf_op jit(solution)/shard_map/all_to_all | solution.py:31
  268.8 7.3 %all-to-all-start.8 = ((f32[32,1,128]{2,1,0:T(1,128)}), f32[32,1,128]{2,1,0:T(1,128)S(1)}, u32[]{:S(2)}, u32[]{:S(2)}) async-start(f32[32,1,128]{2,1,0:T(1,128)} %broadcast_in_dim.104), calls=%async_computation.8 | async-start | bytes 32768 | tf_op jit(solution)/shard_map/all_to_all | solution.py:31
  276.1 11.1 %all-to-all-done.8 = f32[32,1,128]{2,1,0:T(1,128)S(1)} async-done(((f32[32,1,128]{2,1,0:T(1,128)}), f32[32,1,128]{2,1,0:T(1,128)S(1)}, u32[]{:S(2)}, u32[]{:S(2)}) %all-to-all-start.8) | async-done | bytes 16416 | tf_op jit(solution)/shard_map/all_to_all | solution.py:31
  290.2 5.9 %all-to-all-start.9 = ((f32[16,1,32]{2,1,0:T(1,128)}), f32[16,1,32]{2,1,0:T(1,128)S(1)}, u32[]{:S(2)}, u32[]{:S(2)}) async-start(f32[16,1,32]{2,1,0:T(1,128)} %broadcast_in_dim.105), calls=%async_computation.9 | async-start | bytes 16384 | tf_op jit(solution)/shard_map/all_to_all | solution.py:31
  311.8 6.8 %collective-permute-start.25 = (f32[1,512]{1,0:T(1,128)S(1)}, f32[1,512]{1,0:T(1,128)S(1)}, u32[]{:S(2)}, u32[]{:S(2)}) collective-permute-start(f32[1,512]{1,0:T(1,128)S(1)} %get-tuple-element.148), channel_id=1, source_target_pairs={{16,0},{32,16},{48,32},{64,48},{80,64},{96,80},{112,96},{128,112},... | collective-permute-start | bytes 6152 | tf_op jit(solution)/shard_map/ppermute | solution.py:25
  321.0 7.8 %all-to-all-start.10 = ((f32[16,1,32]{2,1,0:T(1,128)}), f32[16,1,32]{2,1,0:T(1,128)S(1)}, u32[]{:S(2)}, u32[]{:S(2)}) async-start(f32[16,1,32]{2,1,0:T(1,128)} %broadcast_in_dim.106), calls=%async_computation.10 | async-start | bytes 16384 | tf_op jit(solution)/shard_map/all_to_all | solution.py:31
  344.3 7.5 %collective-permute-start.29 = (f32[1,512]{1,0:T(1,128)S(1)}, f32[1,512]{1,0:T(1,128)S(1)}, u32[]{:S(2)}, u32[]{:S(2)}) collective-permute-start(f32[1,512]{1,0:T(1,128)S(1)} %get-tuple-element.140), channel_id=1, source_target_pairs={{16,0},{32,16},{48,32},{64,48},{80,64},{96,80},{112,96},{128,112},... | collective-permute-start | bytes 6152 | tf_op jit(solution)/shard_map/ppermute | solution.py:25
  354.2 7.5 %all-to-all-start.11 = ((f32[16,1,32]{2,1,0:T(1,128)}), f32[16,1,32]{2,1,0:T(1,128)S(1)}, u32[]{:S(2)}, u32[]{:S(2)}) async-start(f32[16,1,32]{2,1,0:T(1,128)} %broadcast_in_dim.107), calls=%async_computation.11 | async-start | bytes 16384 | tf_op jit(solution)/shard_map/all_to_all | solution.py:31
  377.2 7.5 %collective-permute-start.33 = (f32[1,512]{1,0:T(1,128)S(1)}, f32[1,512]{1,0:T(1,128)S(1)}, u32[]{:S(2)}, u32[]{:S(2)}) collective-permute-start(f32[1,512]{1,0:T(1,128)S(1)} %get-tuple-element.132), channel_id=1, source_target_pairs={{16,0},{32,16},{48,32},{64,48},{80,64},{96,80},{112,96},{128,112},... | collective-permute-start | bytes 6152 | tf_op jit(solution)/shard_map/ppermute | solution.py:25
  387.1 7.5 %all-to-all-start.12 = ((f32[16,1,32]{2,1,0:T(1,128)}), f32[16,1,32]{2,1,0:T(1,128)S(1)}, u32[]{:S(2)}, u32[]{:S(2)}) async-start(f32[16,1,32]{2,1,0:T(1,128)} %broadcast_in_dim.108), calls=%async_computation.12 | async-start | bytes 16384 | tf_op jit(solution)/shard_map/all_to_all | solution.py:31
  410.1 7.5 %collective-permute-start.37 = (f32[1,512]{1,0:T(1,128)S(1)}, f32[1,512]{1,0:T(1,128)S(1)}, u32[]{:S(2)}, u32[]{:S(2)}) collective-permute-start(f32[1,512]{1,0:T(1,128)S(1)} %get-tuple-element.124), channel_id=1, source_target_pairs={{16,0},{32,16},{48,32},{64,48},{80,64},{96,80},{112,96},{128,112},... | collective-permute-start | bytes 6152 | tf_op jit(solution)/shard_map/ppermute | solution.py:25
  420.0 7.5 %all-to-all-start.13 = ((f32[16,1,32]{2,1,0:T(1,128)}), f32[16,1,32]{2,1,0:T(1,128)S(1)}, u32[]{:S(2)}, u32[]{:S(2)}) async-start(f32[16,1,32]{2,1,0:T(1,128)} %broadcast_in_dim.109), calls=%async_computation.13 | async-start | bytes 16384 | tf_op jit(solution)/shard_map/all_to_all | solution.py:31
  443.0 7.5 %collective-permute-start.41 = (f32[1,512]{1,0:T(1,128)S(1)}, f32[1,512]{1,0:T(1,128)S(1)}, u32[]{:S(2)}, u32[]{:S(2)}) collective-permute-start(f32[1,512]{1,0:T(1,128)S(1)} %get-tuple-element.116), channel_id=1, source_target_pairs={{16,0},{32,16},{48,32},{64,48},{80,64},{96,80},{112,96},{128,112},... | collective-permute-start | bytes 6152 | tf_op jit(solution)/shard_map/ppermute | solution.py:25
  452.9 7.5 %all-to-all-start.14 = ((f32[16,1,32]{2,1,0:T(1,128)}), f32[16,1,32]{2,1,0:T(1,128)S(1)}, u32[]{:S(2)}, u32[]{:S(2)}) async-start(f32[16,1,32]{2,1,0:T(1,128)} %broadcast_in_dim.110), calls=%async_computation.14 | async-start | bytes 16384 | tf_op jit(solution)/shard_map/all_to_all | solution.py:31
  467.2 11.0 %while.23 = (s32[]{:T(128)}, f32[8,64]{1,0:T(8,128)S(1)}, s32[8,16,512]{2,1,0:T(8,128)}, f32[8,16,512]{2,1,0:T(8,128)S(1)}, s32[]{:T(128)}, /*index=5*/s32[]{:T(128)}) while((s32[]{:T(128)}, f32[8,64]{1,0:T(8,128)S(1)}, s32[8,16,512]{2,1,0:T(8,128)}, f32[8,16,512]{2,1,0:T(8,128)S(1)}, s32[]{:T(128)}, ...), condition=%wide.region_24.25_spmd.clone, body=%wide.region_22.24_spmd.clone.sunk | while | flops 1572802 | bytes 197457 | solution.py:68
  478.8 5.0 %all-to-all-start.15 = ((f32[16,1,64]{2,1,0:T(1,128)}), f32[16,1,64]{2,1,0:T(1,128)S(1)}, u32[]{:S(2)}, u32[]{:S(2)}) async-start(f32[16,1,64]{2,1,0:T(1,128)} %broadcast_in_dim.116), calls=%async_computation.15 | async-start | bytes 16384 | tf_op jit(solution)/shard_map/all_to_all | solution.py:31
  (389 shorter events, 245.3 us)
Async XLA Ops:
  2.4 36.7 %collective-permute-start.2 = (f32[128,1]{1,0:T(8,128)}, f32[128,1]{1,0:T(8,128)S(1)}, u32[]{:S(2)}, u32[]{:S(2)}) collective-permute-start(f32[128,1]{1,0:T(8,128)} %get-tuple-element.193), channel_id=1, source_target_pairs={{0,1},{1,2},{2,3},{3,4},{4,5},{5,6},{6,7},{7,8},{8,9},{9,10},{10,1... | collective-permute-start | bytes 1544 | tf_op jit(solution)/shard_map/ppermute | solution.py:25
  6.2 32.9 %collective-permute-start.3 = (f32[128,1]{1,0:T(8,128)}, f32[128,1]{1,0:T(8,128)}, u32[]{:S(2)}, u32[]{:S(2)}) collective-permute-start(f32[128,1]{1,0:T(8,128)} %get-tuple-element.192), channel_id=1, source_target_pairs={{1,0},{2,1},{3,2},{4,3},{5,4},{6,5},{7,6},{8,7},{9,8},{10,9},{11,1... | collective-permute-start | bytes 1544 | tf_op jit(solution)/shard_map/ppermute | solution.py:25
  9.4 29.7 %collective-permute-start = (f32[1,512]{1,0:T(1,128)}, f32[1,512]{1,0:T(1,128)S(1)}, u32[]{:S(2)}, u32[]{:S(2)}) collective-permute-start(f32[1,512]{1,0:T(1,128)} %get-tuple-element.197), channel_id=1, source_target_pairs={{0,16},{16,32},{32,48},{48,64},{64,80},{80,96},{96,112},{112,128},... | collective-permute-start | bytes 6152 | tf_op jit(solution)/shard_map/ppermute | solution.py:25
  13.0 26.2 %collective-permute-start.1 = (f32[1,512]{1,0:T(1,128)}, f32[1,512]{1,0:T(1,128)S(1)}, u32[]{:S(2)}, u32[]{:S(2)}) collective-permute-start(f32[1,512]{1,0:T(1,128)} %get-tuple-element.196), channel_id=1, source_target_pairs={{16,0},{32,16},{48,32},{64,48},{80,64},{96,80},{112,96},{128,112},... | collective-permute-start | bytes 6152 | tf_op jit(solution)/shard_map/ppermute | solution.py:25
  57.7 32.7 %all-to-all-start = ((f32[16,64,512]{2,1,0:T(8,128)}), f32[16,64,512]{2,1,0:T(8,128)}, u32[]{:S(2)}, u32[]{:S(2)}) async-start(f32[16,64,512]{2,1,0:T(8,128)} %maximum_select_fusion), calls=%async_computation | async-start | bytes 4194304 | tf_op jit(solution)/shard_map/all_to_all | solution.py:83
  93.5 14.7 %collective-permute-start.6 = (f32[128,1]{1,0:T(8,128)S(1)}, f32[128,1]{1,0:T(8,128)S(1)}, u32[]{:S(2)}, u32[]{:S(2)}) collective-permute-start(f32[128,1]{1,0:T(8,128)S(1)} %get-tuple-element.185), channel_id=1, source_target_pairs={{0,1},{1,2},{2,3},{3,4},{4,5},{5,6},{6,7},{7,8},{8,9},{9,10},{10,1... | collective-permute-start | bytes 1544 | tf_op jit(solution)/shard_map/ppermute | solution.py:25
  113.1 12.7 %all-to-all-start.2 = ((f32[16,1,32]{2,1,0:T(1,128)}), f32[16,1,32]{2,1,0:T(1,128)S(1)}, u32[]{:S(2)}, u32[]{:S(2)}) async-start(f32[16,1,32]{2,1,0:T(1,128)} %broadcast_in_dim.98), calls=%async_computation.2 | async-start | bytes 16384 | tf_op jit(solution)/shard_map/all_to_all | solution.py:31
  127.8 14.7 %collective-permute-start.10 = (f32[128,1]{1,0:T(8,128)S(1)}, f32[128,1]{1,0:T(8,128)S(1)}, u32[]{:S(2)}, u32[]{:S(2)}) collective-permute-start(f32[128,1]{1,0:T(8,128)S(1)} %get-tuple-element.177), channel_id=1, source_target_pairs={{0,1},{1,2},{2,3},{3,4},{4,5},{5,6},{6,7},{7,8},{8,9},{9,10},{10,1... | collective-permute-start | bytes 1544 | tf_op jit(solution)/shard_map/ppermute | solution.py:25
  130.6 11.9 %collective-permute-start.11 = (f32[128,1]{1,0:T(8,128)S(1)}, f32[128,1]{1,0:T(8,128)S(1)}, u32[]{:S(2)}, u32[]{:S(2)}) collective-permute-start(f32[128,1]{1,0:T(8,128)S(1)} %get-tuple-element.176), channel_id=1, source_target_pairs={{1,0},{2,1},{3,2},{4,3},{5,4},{6,5},{7,6},{8,7},{9,8},{10,9},{11,1... | collective-permute-start | bytes 1544 | tf_op jit(solution)/shard_map/ppermute | solution.py:25
  147.3 11.8 %all-to-all-start.3 = ((f32[16,1,32]{2,1,0:T(1,128)}), f32[16,1,32]{2,1,0:T(1,128)S(1)}, u32[]{:S(2)}, u32[]{:S(2)}) async-start(f32[16,1,32]{2,1,0:T(1,128)} %broadcast_in_dim.99), calls=%async_computation.3 | async-start | bytes 16384 | tf_op jit(solution)/shard_map/all_to_all | solution.py:31
  161.1 14.2 %collective-permute-start.14 = (f32[128,1]{1,0:T(8,128)S(1)}, f32[128,1]{1,0:T(8,128)S(1)}, u32[]{:S(2)}, u32[]{:S(2)}) collective-permute-start(f32[128,1]{1,0:T(8,128)S(1)} %get-tuple-element.169), channel_id=1, source_target_pairs={{0,1},{1,2},{2,3},{3,4},{4,5},{5,6},{6,7},{7,8},{8,9},{9,10},{10,1... | collective-permute-start | bytes 1544 | tf_op jit(solution)/shard_map/ppermute | solution.py:25
  163.9 11.4 %collective-permute-start.15 = (f32[128,1]{1,0:T(8,128)S(1)}, f32[128,1]{1,0:T(8,128)S(1)}, u32[]{:S(2)}, u32[]{:S(2)}) collective-permute-start(f32[128,1]{1,0:T(8,128)S(1)} %get-tuple-element.168), channel_id=1, source_target_pairs={{1,0},{2,1},{3,2},{4,3},{5,4},{6,5},{7,6},{8,7},{9,8},{10,9},{11,1... | collective-permute-start | bytes 1544 | tf_op jit(solution)/shard_map/ppermute | solution.py:25
  180.2 11.8 %all-to-all-start.4 = ((f32[16,1,32]{2,1,0:T(1,128)}), f32[16,1,32]{2,1,0:T(1,128)S(1)}, u32[]{:S(2)}, u32[]{:S(2)}) async-start(f32[16,1,32]{2,1,0:T(1,128)} %broadcast_in_dim.100), calls=%async_computation.4 | async-start | bytes 16384 | tf_op jit(solution)/shard_map/all_to_all | solution.py:31
  194.0 14.4 %collective-permute-start.18 = (f32[128,1]{1,0:T(8,128)S(1)}, f32[128,1]{1,0:T(8,128)S(1)}, u32[]{:S(2)}, u32[]{:S(2)}) collective-permute-start(f32[128,1]{1,0:T(8,128)S(1)} %get-tuple-element.161), channel_id=1, source_target_pairs={{0,1},{1,2},{2,3},{3,4},{4,5},{5,6},{6,7},{7,8},{8,9},{9,10},{10,1... | collective-permute-start | bytes 1544 | tf_op jit(solution)/shard_map/ppermute | solution.py:25
  196.7 11.6 %collective-permute-start.19 = (f32[128,1]{1,0:T(8,128)S(1)}, f32[128,1]{1,0:T(8,128)S(1)}, u32[]{:S(2)}, u32[]{:S(2)}) collective-permute-start(f32[128,1]{1,0:T(8,128)S(1)} %get-tuple-element.160), channel_id=1, source_target_pairs={{1,0},{2,1},{3,2},{4,3},{5,4},{6,5},{7,6},{8,7},{9,8},{10,9},{11,1... | collective-permute-start | bytes 1544 | tf_op jit(solution)/shard_map/ppermute | solution.py:25
  213.0 11.8 %all-to-all-start.5 = ((f32[16,1,32]{2,1,0:T(1,128)}), f32[16,1,32]{2,1,0:T(1,128)S(1)}, u32[]{:S(2)}, u32[]{:S(2)}) async-start(f32[16,1,32]{2,1,0:T(1,128)} %broadcast_in_dim.101), calls=%async_computation.5 | async-start | bytes 16384 | tf_op jit(solution)/shard_map/all_to_all | solution.py:31
  226.8 14.2 %collective-permute-start.22 = (f32[128,1]{1,0:T(8,128)S(1)}, f32[128,1]{1,0:T(8,128)S(1)}, u32[]{:S(2)}, u32[]{:S(2)}) collective-permute-start(f32[128,1]{1,0:T(8,128)S(1)} %get-tuple-element.153), channel_id=1, source_target_pairs={{0,1},{1,2},{2,3},{3,4},{4,5},{5,6},{6,7},{7,8},{8,9},{9,10},{10,1... | collective-permute-start | bytes 1544 | tf_op jit(solution)/shard_map/ppermute | solution.py:25
  229.6 11.4 %collective-permute-start.23 = (f32[128,1]{1,0:T(8,128)S(1)}, f32[128,1]{1,0:T(8,128)S(1)}, u32[]{:S(2)}, u32[]{:S(2)}) collective-permute-start(f32[128,1]{1,0:T(8,128)S(1)} %get-tuple-element.152), channel_id=1, source_target_pairs={{1,0},{2,1},{3,2},{4,3},{5,4},{6,5},{7,6},{8,7},{9,8},{10,9},{11,1... | collective-permute-start | bytes 1544 | tf_op jit(solution)/shard_map/ppermute | solution.py:25
  245.8 11.8 %all-to-all-start.6 = ((f32[16,1,32]{2,1,0:T(1,128)}), f32[16,1,32]{2,1,0:T(1,128)S(1)}, u32[]{:S(2)}, u32[]{:S(2)}) async-start(f32[16,1,32]{2,1,0:T(1,128)} %broadcast_in_dim.102), calls=%async_computation.6 | async-start | bytes 16384 | tf_op jit(solution)/shard_map/all_to_all | solution.py:31
  268.8 18.5 %all-to-all-start.8 = ((f32[32,1,128]{2,1,0:T(1,128)}), f32[32,1,128]{2,1,0:T(1,128)S(1)}, u32[]{:S(2)}, u32[]{:S(2)}) async-start(f32[32,1,128]{2,1,0:T(1,128)} %broadcast_in_dim.104), calls=%async_computation.8 | async-start | bytes 32768 | tf_op jit(solution)/shard_map/all_to_all | solution.py:31
  305.1 13.7 %collective-permute-start.26 = (f32[128,1]{1,0:T(8,128)S(1)}, f32[128,1]{1,0:T(8,128)S(1)}, u32[]{:S(2)}, u32[]{:S(2)}) collective-permute-start(f32[128,1]{1,0:T(8,128)S(1)} %get-tuple-element.145), channel_id=1, source_target_pairs={{0,1},{1,2},{2,3},{3,4},{4,5},{5,6},{6,7},{7,8},{8,9},{9,10},{10,1... | collective-permute-start | bytes 1544 | tf_op jit(solution)/shard_map/ppermute | solution.py:25
  321.0 12.1 %all-to-all-start.10 = ((f32[16,1,32]{2,1,0:T(1,128)}), f32[16,1,32]{2,1,0:T(1,128)S(1)}, u32[]{:S(2)}, u32[]{:S(2)}) async-start(f32[16,1,32]{2,1,0:T(1,128)} %broadcast_in_dim.106), calls=%async_computation.10 | async-start | bytes 16384 | tf_op jit(solution)/shard_map/all_to_all | solution.py:31
  337.7 14.2 %collective-permute-start.30 = (f32[128,1]{1,0:T(8,128)S(1)}, f32[128,1]{1,0:T(8,128)S(1)}, u32[]{:S(2)}, u32[]{:S(2)}) collective-permute-start(f32[128,1]{1,0:T(8,128)S(1)} %get-tuple-element.137), channel_id=1, source_target_pairs={{0,1},{1,2},{2,3},{3,4},{4,5},{5,6},{6,7},{7,8},{8,9},{9,10},{10,1... | collective-permute-start | bytes 1544 | tf_op jit(solution)/shard_map/ppermute | solution.py:25
  340.5 11.4 %collective-permute-start.31 = (f32[128,1]{1,0:T(8,128)S(1)}, f32[128,1]{1,0:T(8,128)S(1)}, u32[]{:S(2)}, u32[]{:S(2)}) collective-permute-start(f32[128,1]{1,0:T(8,128)S(1)} %get-tuple-element.136), channel_id=1, source_target_pairs={{1,0},{2,1},{3,2},{4,3},{5,4},{6,5},{7,6},{8,7},{9,8},{10,9},{11,1... | collective-permute-start | bytes 1544 | tf_op jit(solution)/shard_map/ppermute | solution.py:25
  354.2 11.8 %all-to-all-start.11 = ((f32[16,1,32]{2,1,0:T(1,128)}), f32[16,1,32]{2,1,0:T(1,128)S(1)}, u32[]{:S(2)}, u32[]{:S(2)}) async-start(f32[16,1,32]{2,1,0:T(1,128)} %broadcast_in_dim.107), calls=%async_computation.11 | async-start | bytes 16384 | tf_op jit(solution)/shard_map/all_to_all | solution.py:31
  370.6 14.2 %collective-permute-start.34 = (f32[128,1]{1,0:T(8,128)S(1)}, f32[128,1]{1,0:T(8,128)S(1)}, u32[]{:S(2)}, u32[]{:S(2)}) collective-permute-start(f32[128,1]{1,0:T(8,128)S(1)} %get-tuple-element.129), channel_id=1, source_target_pairs={{0,1},{1,2},{2,3},{3,4},{4,5},{5,6},{6,7},{7,8},{8,9},{9,10},{10,1... | collective-permute-start | bytes 1544 | tf_op jit(solution)/shard_map/ppermute | solution.py:25
  373.4 11.4 %collective-permute-start.35 = (f32[128,1]{1,0:T(8,128)S(1)}, f32[128,1]{1,0:T(8,128)S(1)}, u32[]{:S(2)}, u32[]{:S(2)}) collective-permute-start(f32[128,1]{1,0:T(8,128)S(1)} %get-tuple-element.128), channel_id=1, source_target_pairs={{1,0},{2,1},{3,2},{4,3},{5,4},{6,5},{7,6},{8,7},{9,8},{10,9},{11,1... | collective-permute-start | bytes 1544 | tf_op jit(solution)/shard_map/ppermute | solution.py:25
  387.1 11.8 %all-to-all-start.12 = ((f32[16,1,32]{2,1,0:T(1,128)}), f32[16,1,32]{2,1,0:T(1,128)S(1)}, u32[]{:S(2)}, u32[]{:S(2)}) async-start(f32[16,1,32]{2,1,0:T(1,128)} %broadcast_in_dim.108), calls=%async_computation.12 | async-start | bytes 16384 | tf_op jit(solution)/shard_map/all_to_all | solution.py:31
  403.5 14.2 %collective-permute-start.38 = (f32[128,1]{1,0:T(8,128)S(1)}, f32[128,1]{1,0:T(8,128)S(1)}, u32[]{:S(2)}, u32[]{:S(2)}) collective-permute-start(f32[128,1]{1,0:T(8,128)S(1)} %get-tuple-element.121), channel_id=1, source_target_pairs={{0,1},{1,2},{2,3},{3,4},{4,5},{5,6},{6,7},{7,8},{8,9},{9,10},{10,1... | collective-permute-start | bytes 1544 | tf_op jit(solution)/shard_map/ppermute | solution.py:25
  420.0 11.8 %all-to-all-start.13 = ((f32[16,1,32]{2,1,0:T(1,128)}), f32[16,1,32]{2,1,0:T(1,128)S(1)}, u32[]{:S(2)}, u32[]{:S(2)}) async-start(f32[16,1,32]{2,1,0:T(1,128)} %broadcast_in_dim.109), calls=%async_computation.13 | async-start | bytes 16384 | tf_op jit(solution)/shard_map/all_to_all | solution.py:31
  436.4 14.2 %collective-permute-start.42 = (f32[128,1]{1,0:T(8,128)S(1)}, f32[128,1]{1,0:T(8,128)S(1)}, u32[]{:S(2)}, u32[]{:S(2)}) collective-permute-start(f32[128,1]{1,0:T(8,128)S(1)} %get-tuple-element.113), channel_id=1, source_target_pairs={{0,1},{1,2},{2,3},{3,4},{4,5},{5,6},{6,7},{7,8},{8,9},{9,10},{10,1... | collective-permute-start | bytes 1544 | tf_op jit(solution)/shard_map/ppermute | solution.py:25
  452.9 11.8 %all-to-all-start.14 = ((f32[16,1,32]{2,1,0:T(1,128)}), f32[16,1,32]{2,1,0:T(1,128)S(1)}, u32[]{:S(2)}, u32[]{:S(2)}) async-start(f32[16,1,32]{2,1,0:T(1,128)} %broadcast_in_dim.110), calls=%async_computation.14 | async-start | bytes 16384 | tf_op jit(solution)/shard_map/all_to_all | solution.py:31
  (39 other events, 705.0 us)

commit v4 on v3

--- a/solution.py
+++ b/solution.py
@@ -46,29 +46,15 @@
 
 
 def damper_lookup(ids, coef):
-    rows, cols = ids.shape
-    blocks = ids.reshape(rows // 16, 16, cols)
     labels = jnp.arange(coef.shape[0], dtype=jnp.int32)
-
-    def one_block(block):
-        match = block[None, :, :] == labels[:, None, None]
-        return jnp.sum(jnp.where(match, coef[:, None, None], 0.0), axis=0)
-
-    return lax.map(one_block, blocks).reshape(rows, cols)
+    match = ids[None, :, :] == labels[:, None, None]
+    return jnp.sum(jnp.where(match, coef[:, None, None], 0.0), axis=0)
 
 
 def damper_totals(ids, values, count):
-    rows, cols = ids.shape
     labels = jnp.arange(count, dtype=jnp.int32)
-
-    def one_block(pair):
-        match = pair[0][None, :, :] == labels[:, None, None]
-        return jnp.sum(jnp.where(match, pair[1][None, :, :], 0.0), axis=(1, 2))
-
-    parts = lax.map(
-        one_block, (ids.reshape(rows // 16, 16, cols), values.reshape(rows // 16, 16, cols))
-    )
-    return jnp.sum(parts, axis=0)
+    match = ids[None, :, :] == labels[:, None, None]
+    return jnp.sum(jnp.where(match, values[None, :, :], 0.0), axis=(1, 2))
 
 
 def panel_slabs(panel_store, owner, nodes):
@@ -113,13 +99,15 @@
     places = node_index[0]
     row_slab, col_slab = panel_slabs(panel_store, owner[0], nodes)
 
-    def correct(resid, transpose):
+    def correct(resid, transpose, first=False):
         scaled = resid / diag
         if transpose:
             result = lax.dot_general(scaled, band_tile, (((1,), (1,)), ((), ())), precision=HIGH)
         else:
             result = jnp.dot(scaled, band_tile, precision=HIGH)
         picked = resid.reshape(-1)[places]
+        if first:
+            picked, _ = lax.optimization_barrier((picked, row_slab))
         values = gather_all(picked, "plate").reshape(-1)
         slab = col_slab if transpose else row_slab
         mine = jnp.dot(slab, values, precision=HIGH)
@@ -128,7 +116,7 @@
     new_disp = disp
     resid = load - (diag * new_disp - stiff * neighbours(new_disp))
     for step in range(ITERS):
-        new_disp = new_disp + correct(resid, False)
+        new_disp = new_disp + correct(resid, False, first=step == 0)
         if step < ITERS - 1:
             resid = load - (diag * new_disp - stiff * neighbours(new_disp))
     partial_force = jnp.sum(inertia * new_disp, axis=1)

time: 493 us -> 489 us (level)
  local copies, waits for them, and re-layouts: 48 us -> 35.6 us
  waiting for transfers between devices: 83.3 us -> 90.9 us
    eq x16 -> x0, local copies, waits for them, and re-layouts: 12.2 us -> none  [the longest x8 6.13 us: one_block(): match = pair[0][None, :, :] == labels[:, None, None]]
    ppermute x44, waiting for transfers between devices: 6.23 us -> 13.9 us  [shifted(): return lax.ppermute(edge, axis, pairs)]
    ppermute x44, starting transfers between devices: 161 us -> 169 us  [shifted(): return lax.ppermute(edge, axis, pairs)]
  transfers between devices with their start and end apart: 59 -> 59, of which waited for: 25 -> 34; matrix products, arithmetic and copies ran while one was open for 7% -> 6% of each run, Pallas kernels for 0% -> 0%
where the time goes in v4:
time: 489 us; the launch traced here: 486 us
  starting transfers between devices  272 us (56%)
  waiting for transfers between devices  90.9 us (19%)
  other arithmetic  63 us (13%)
  local copies, waits for them, and re-layouts  35.6 us (7%)
  matrix products  13 us (3%)
  blocking collectives  8.6 us (2%)
    ppermute x44, starting transfers between devices, shifted(): return lax.ppermute(edge, axis, pairs)  169 us
    all_to_all x14, starting transfers between devices, gather_all(): return lax.all_to_all(spread, axis, 0, 0, tiled=False)  97.4 us
    all_to_all x14, waiting for transfers between devices, gather_all(): return lax.all_to_all(spread, axis, 0, 0, tiled=False)  52.3 us
    all_to_all x1, waiting for transfers between devices, panel_slabs(): got = jnp.sum(lax.all_to_all(sent, 'plate', 0, 0, tiled=False), axis=0)  24.7 us
    sub x6, other arithmetic, on_device(): resid = load - (diag * new_disp - stiff * neighbours(new_disp))  18.3 us
    ppermute x44, waiting for transfers between devices, shifted(): return lax.ppermute(edge, axis, pairs)  13.9 us
    mul x5, other arithmetic, on_device(): resid = target - (diag * adjoint - neighbours(stiff * adjoint))  13.6 us
    scatter-add x12, other arithmetic, correct(): return result.reshape(-1).at[places].add(mine).reshape(rows, cols)  10.7 us
  transfers between devices with their start and end apart: 59, of which 34 were waited for; matrix products, arithmetic and copies ran while one was open for 6% of the time, Pallas kernels for 0%

profile of v4, /device:TPU:7, one launch (start us, length us, event | category | flops | bytes accessed | tf_op | source)
XLA Modules:
  0.0 485.9 jit_solution(6176598676857223940)
XLA Ops:
  2.2 12.0 %collective-permute-start.1 = (f32[1,512]{1,0:T(1,128)}, f32[1,512]{1,0:T(1,128)S(1)}, u32[]{:S(2)}, u32[]{:S(2)}) collective-permute-start(f32[1,512]{1,0:T(1,128)} %get-tuple-element.106), channel_id=1, source_target_pairs={{16,0},{32,16},{48,32},{64,48},{80,64},{96,80},{112,96},{128,112},... | collective-permute-start | bytes 6152 | tf_op jit(solution)/shard_map/ppermute | solution.py:25
  32.8 4.1 fusion.3
  40.6 5.7 %all-to-all-start.1 = ((f32[16,1,32]{2,1,0:T(1,128)}), f32[16,1,32]{2,1,0:T(1,128)S(1)}, u32[]{:S(2)}, u32[]{:S(2)}) async-start(f32[16,1,32]{2,1,0:T(1,128)} %broadcast_in_dim.80), calls=%async_computation.1 | async-start | bytes 16384 | tf_op jit(solution)/shard_map/all_to_all | solution.py:31
  50.6 6.0 %all-to-all-start = ((f32[16,64,512]{2,1,0:T(8,128)}), f32[16,64,512]{2,1,0:T(8,128)}, u32[]{:S(2)}, u32[]{:S(2)}) async-start(f32[16,64,512]{2,1,0:T(8,128)} %maximum_select_fusion), calls=%async_computation | async-start | bytes 4194304 | tf_op jit(solution)/shard_map/all_to_all | solution.py:69
  58.6 24.7 %all-to-all-done = f32[16,64,512]{2,1,0:T(8,128)} async-done(((f32[16,64,512]{2,1,0:T(8,128)}), f32[16,64,512]{2,1,0:T(8,128)}, u32[]{:S(2)}, u32[]{:S(2)}) %all-to-all-start) | async-done | bytes 2097184 | tf_op jit(solution)/shard_map/all_to_all | solution.py:69
  86.4 7.6 %collective-permute-start.5 = (f32[1,512]{1,0:T(1,128)S(1)}, f32[1,512]{1,0:T(1,128)S(1)}, u32[]{:S(2)}, u32[]{:S(2)}) collective-permute-start(f32[1,512]{1,0:T(1,128)S(1)} %get-tuple-element.98), channel_id=1, source_target_pairs={{16,0},{32,16},{48,32},{64,48},{80,64},{96,80},{112,96},{128,112},... | collective-permute-start | bytes 6152 | tf_op jit(solution)/shard_map/ppermute | solution.py:25
  109.8 8.0 %all-to-all-start.2 = ((f32[16,1,32]{2,1,0:T(1,128)}), f32[16,1,32]{2,1,0:T(1,128)S(1)}, u32[]{:S(2)}, u32[]{:S(2)}) async-start(f32[16,1,32]{2,1,0:T(1,128)} %broadcast_in_dim.81), calls=%async_computation.2 | async-start | bytes 16384 | tf_op jit(solution)/shard_map/all_to_all | solution.py:31
  118.6 3.5 all-to-all-done.2
  124.1 7.6 %collective-permute-start.9 = (f32[1,512]{1,0:T(1,128)S(1)}, f32[1,512]{1,0:T(1,128)S(1)}, u32[]{:S(2)}, u32[]{:S(2)}) collective-permute-start(f32[1,512]{1,0:T(1,128)S(1)} %get-tuple-element.90), channel_id=1, source_target_pairs={{16,0},{32,16},{48,32},{64,48},{80,64},{96,80},{112,96},{128,112},... | collective-permute-start | bytes 6152 | tf_op jit(solution)/shard_map/ppermute | solution.py:25
  144.7 7.3 %all-to-all-start.3 = ((f32[16,1,32]{2,1,0:T(1,128)}), f32[16,1,32]{2,1,0:T(1,128)S(1)}, u32[]{:S(2)}, u32[]{:S(2)}) async-start(f32[16,1,32]{2,1,0:T(1,128)} %broadcast_in_dim.82), calls=%async_computation.3 | async-start | bytes 16384 | tf_op jit(solution)/shard_map/all_to_all | solution.py:31
  158.3 7.6 %collective-permute-start.13 = (f32[1,512]{1,0:T(1,128)S(1)}, f32[1,512]{1,0:T(1,128)S(1)}, u32[]{:S(2)}, u32[]{:S(2)}) collective-permute-start(f32[1,512]{1,0:T(1,128)S(1)} %get-tuple-element.82), channel_id=1, source_target_pairs={{16,0},{32,16},{48,32},{64,48},{80,64},{96,80},{112,96},{128,112},... | collective-permute-start | bytes 6152 | tf_op jit(solution)/shard_map/ppermute | solution.py:25
  178.9 7.3 %all-to-all-start.4 = ((f32[16,1,32]{2,1,0:T(1,128)}), f32[16,1,32]{2,1,0:T(1,128)S(1)}, u32[]{:S(2)}, u32[]{:S(2)}) async-start(f32[16,1,32]{2,1,0:T(1,128)} %broadcast_in_dim.83), calls=%async_computation.4 | async-start | bytes 16384 | tf_op jit(solution)/shard_map/all_to_all | solution.py:31
  192.5 7.6 %collective-permute-start.17 = (f32[1,512]{1,0:T(1,128)S(1)}, f32[1,512]{1,0:T(1,128)S(1)}, u32[]{:S(2)}, u32[]{:S(2)}) collective-permute-start(f32[1,512]{1,0:T(1,128)S(1)} %get-tuple-element.74), channel_id=1, source_target_pairs={{16,0},{32,16},{48,32},{64,48},{80,64},{96,80},{112,96},{128,112},... | collective-permute-start | bytes 6152 | tf_op jit(solution)/shard_map/ppermute | solution.py:25
  213.1 7.3 %all-to-all-start.5 = ((f32[16,1,32]{2,1,0:T(1,128)}), f32[16,1,32]{2,1,0:T(1,128)S(1)}, u32[]{:S(2)}, u32[]{:S(2)}) async-start(f32[16,1,32]{2,1,0:T(1,128)} %broadcast_in_dim.84), calls=%async_computation.5 | async-start | bytes 16384 | tf_op jit(solution)/shard_map/all_to_all | solution.py:31
  226.6 7.6 %collective-permute-start.21 = (f32[1,512]{1,0:T(1,128)S(1)}, f32[1,512]{1,0:T(1,128)S(1)}, u32[]{:S(2)}, u32[]{:S(2)}) collective-permute-start(f32[1,512]{1,0:T(1,128)S(1)} %get-tuple-element.66), channel_id=1, source_target_pairs={{16,0},{32,16},{48,32},{64,48},{80,64},{96,80},{112,96},{128,112},... | collective-permute-start | bytes 6152 | tf_op jit(solution)/shard_map/ppermute | solution.py:25
  247.3 7.3 %all-to-all-start.6 = ((f32[16,1,32]{2,1,0:T(1,128)}), f32[16,1,32]{2,1,0:T(1,128)S(1)}, u32[]{:S(2)}, u32[]{:S(2)}) async-start(f32[16,1,32]{2,1,0:T(1,128)} %broadcast_in_dim.85), calls=%async_computation.6 | async-start | bytes 16384 | tf_op jit(solution)/shard_map/all_to_all | solution.py:31
  260.8 8.6 %all_to_all.95 = f32[16,1,128]{2,1,0:T(1,128)S(1)} all-to-all(f32[16,1,128]{2,1,0:T(1,128)S(1)} %broadcast_in_dim.86), channel_id=1, replica_groups=mesh['storey'=32,'plate'=16] {'plate'}, dimensions={0} | all-to-all | bytes 16384 | tf_op jit(solution)/shard_map/all_to_all | solution.py:31
  270.0 7.4 %all-to-all-start.8 = ((f32[32,1,128]{2,1,0:T(1,128)}), f32[32,1,128]{2,1,0:T(1,128)S(1)}, u32[]{:S(2)}, u32[]{:S(2)}) async-start(f32[32,1,128]{2,1,0:T(1,128)} %broadcast_in_dim.87), calls=%async_computation.8 | async-start | bytes 32768 | tf_op jit(solution)/shard_map/all_to_all | solution.py:31
  277.4 11.1 %all-to-all-done.8 = f32[32,1,128]{2,1,0:T(1,128)S(1)} async-done(((f32[32,1,128]{2,1,0:T(1,128)}), f32[32,1,128]{2,1,0:T(1,128)S(1)}, u32[]{:S(2)}, u32[]{:S(2)}) %all-to-all-start.8) | async-done | bytes 16416 | tf_op jit(solution)/shard_map/all_to_all | solution.py:31
  291.5 5.9 %all-to-all-start.9 = ((f32[16,1,32]{2,1,0:T(1,128)}), f32[16,1,32]{2,1,0:T(1,128)S(1)}, u32[]{:S(2)}, u32[]{:S(2)}) async-start(f32[16,1,32]{2,1,0:T(1,128)} %broadcast_in_dim.88), calls=%async_computation.9 | async-start | bytes 16384 | tf_op jit(solution)/shard_map/all_to_all | solution.py:31
  306.4 5.1 %collective-permute-start.25 = (f32[1,512]{1,0:T(1,128)S(1)}, f32[1,512]{1,0:T(1,128)S(1)}, u32[]{:S(2)}, u32[]{:S(2)}) collective-permute-start(f32[1,512]{1,0:T(1,128)S(1)} %get-tuple-element.58), channel_id=1, source_target_pairs={{16,0},{32,16},{48,32},{64,48},{80,64},{96,80},{112,96},{128,112},... | collective-permute-start | bytes 6152 | tf_op jit(solution)/shard_map/ppermute | solution.py:25
  321.9 7.3 %all-to-all-start.10 = ((f32[16,1,32]{2,1,0:T(1,128)}), f32[16,1,32]{2,1,0:T(1,128)S(1)}, u32[]{:S(2)}, u32[]{:S(2)}) async-start(f32[16,1,32]{2,1,0:T(1,128)} %broadcast_in_dim.89), calls=%async_computation.10 | async-start | bytes 16384 | tf_op jit(solution)/shard_map/all_to_all | solution.py:31
  338.2 7.6 %collective-permute-start.29 = (f32[1,512]{1,0:T(1,128)S(1)}, f32[1,512]{1,0:T(1,128)S(1)}, u32[]{:S(2)}, u32[]{:S(2)}) collective-permute-start(f32[1,512]{1,0:T(1,128)S(1)} %get-tuple-element.50), channel_id=1, source_target_pairs={{16,0},{32,16},{48,32},{64,48},{80,64},{96,80},{112,96},{128,112},... | collective-permute-start | bytes 6152 | tf_op jit(solution)/shard_map/ppermute | solution.py:25
  356.2 7.3 %all-to-all-start.11 = ((f32[16,1,32]{2,1,0:T(1,128)}), f32[16,1,32]{2,1,0:T(1,128)S(1)}, u32[]{:S(2)}, u32[]{:S(2)}) async-start(f32[16,1,32]{2,1,0:T(1,128)} %broadcast_in_dim.90), calls=%async_computation.11 | async-start | bytes 16384 | tf_op jit(solution)/shard_map/all_to_all | solution.py:31
  372.4 7.6 %collective-permute-start.33 = (f32[1,512]{1,0:T(1,128)S(1)}, f32[1,512]{1,0:T(1,128)S(1)}, u32[]{:S(2)}, u32[]{:S(2)}) collective-permute-start(f32[1,512]{1,0:T(1,128)S(1)} %get-tuple-element.42), channel_id=1, source_target_pairs={{16,0},{32,16},{48,32},{64,48},{80,64},{96,80},{112,96},{128,112},... | collective-permute-start | bytes 6152 | tf_op jit(solution)/shard_map/ppermute | solution.py:25
  390.4 7.3 %all-to-all-start.12 = ((f32[16,1,32]{2,1,0:T(1,128)}), f32[16,1,32]{2,1,0:T(1,128)S(1)}, u32[]{:S(2)}, u32[]{:S(2)}) async-start(f32[16,1,32]{2,1,0:T(1,128)} %broadcast_in_dim.91), calls=%async_computation.12 | async-start | bytes 16384 | tf_op jit(solution)/shard_map/all_to_all | solution.py:31
  406.7 7.6 %collective-permute-start.37 = (f32[1,512]{1,0:T(1,128)S(1)}, f32[1,512]{1,0:T(1,128)S(1)}, u32[]{:S(2)}, u32[]{:S(2)}) collective-permute-start(f32[1,512]{1,0:T(1,128)S(1)} %get-tuple-element.34), channel_id=1, source_target_pairs={{16,0},{32,16},{48,32},{64,48},{80,64},{96,80},{112,96},{128,112},... | collective-permute-start | bytes 6152 | tf_op jit(solution)/shard_map/ppermute | solution.py:25
  424.7 7.3 %all-to-all-start.13 = ((f32[16,1,32]{2,1,0:T(1,128)}), f32[16,1,32]{2,1,0:T(1,128)S(1)}, u32[]{:S(2)}, u32[]{:S(2)}) async-start(f32[16,1,32]{2,1,0:T(1,128)} %broadcast_in_dim.92), calls=%async_computation.13 | async-start | bytes 16384 | tf_op jit(solution)/shard_map/all_to_all | solution.py:31
  440.9 7.6 %collective-permute-start.41 = (f32[1,512]{1,0:T(1,128)S(1)}, f32[1,512]{1,0:T(1,128)S(1)}, u32[]{:S(2)}, u32[]{:S(2)}) collective-permute-start(f32[1,512]{1,0:T(1,128)S(1)} %get-tuple-element.26), channel_id=1, source_target_pairs={{16,0},{32,16},{48,32},{64,48},{80,64},{96,80},{112,96},{128,112},... | collective-permute-start | bytes 6152 | tf_op jit(solution)/shard_map/ppermute | solution.py:25
  458.9 7.3 %all-to-all-start.14 = ((f32[16,1,32]{2,1,0:T(1,128)}), f32[16,1,32]{2,1,0:T(1,128)S(1)}, u32[]{:S(2)}, u32[]{:S(2)}) async-start(f32[16,1,32]{2,1,0:T(1,128)} %broadcast_in_dim.93), calls=%async_computation.14 | async-start | bytes 16384 | tf_op jit(solution)/shard_map/all_to_all | solution.py:31
  476.0 5.0 %all-to-all-start.15 = ((f32[16,1,64]{2,1,0:T(1,128)}), f32[16,1,64]{2,1,0:T(1,128)S(1)}, u32[]{:S(2)}, u32[]{:S(2)}) async-start(f32[16,1,64]{2,1,0:T(1,128)} %broadcast_in_dim.95), calls=%async_computation.15 | async-start | bytes 16384 | tf_op jit(solution)/shard_map/all_to_all | solution.py:31
  481.6 3.8 all-to-all-done.15
  (333 shorter events, 238.5 us)
Async XLA Ops:
  2.2 30.5 %collective-permute-start.1 = (f32[1,512]{1,0:T(1,128)}, f32[1,512]{1,0:T(1,128)S(1)}, u32[]{:S(2)}, u32[]{:S(2)}) collective-permute-start(f32[1,512]{1,0:T(1,128)} %get-tuple-element.106), channel_id=1, source_target_pairs={{16,0},{32,16},{48,32},{64,48},{80,64},{96,80},{112,96},{128,112},... | collective-permute-start | bytes 6152 | tf_op jit(solution)/shard_map/ppermute | solution.py:25
  14.1 18.6 %collective-permute-start = (f32[1,512]{1,0:T(1,128)}, f32[1,512]{1,0:T(1,128)S(1)}, u32[]{:S(2)}, u32[]{:S(2)}) collective-permute-start(f32[1,512]{1,0:T(1,128)} %get-tuple-element.107), channel_id=1, source_target_pairs={{0,16},{16,32},{32,48},{48,64},{64,80},{80,96},{96,112},{112,128},... | collective-permute-start | bytes 6152 | tf_op jit(solution)/shard_map/ppermute | solution.py:25
  17.6 15.1 %collective-permute-start.3 = (f32[128,1]{1,0:T(8,128)}, f32[128,1]{1,0:T(8,128)S(1)}, u32[]{:S(2)}, u32[]{:S(2)}) collective-permute-start(f32[128,1]{1,0:T(8,128)} %get-tuple-element.102), channel_id=1, source_target_pairs={{1,0},{2,1},{3,2},{4,3},{5,4},{6,5},{7,6},{8,7},{9,8},{10,9},{11,1... | collective-permute-start | bytes 1544 | tf_op jit(solution)/shard_map/ppermute | solution.py:25
  20.5 12.2 %collective-permute-start.2 = (f32[128,1]{1,0:T(8,128)}, f32[128,1]{1,0:T(8,128)S(1)}, u32[]{:S(2)}, u32[]{:S(2)}) collective-permute-start(f32[128,1]{1,0:T(8,128)} %get-tuple-element.103), channel_id=1, source_target_pairs={{0,1},{1,2},{2,3},{3,4},{4,5},{5,6},{6,7},{7,8},{8,9},{9,10},{10,1... | collective-permute-start | bytes 1544 | tf_op jit(solution)/shard_map/ppermute | solution.py:25
  40.6 10.0 %all-to-all-start.1 = ((f32[16,1,32]{2,1,0:T(1,128)}), f32[16,1,32]{2,1,0:T(1,128)S(1)}, u32[]{:S(2)}, u32[]{:S(2)}) async-start(f32[16,1,32]{2,1,0:T(1,128)} %broadcast_in_dim.80), calls=%async_computation.1 | async-start | bytes 16384 | tf_op jit(solution)/shard_map/all_to_all | solution.py:31
  50.6 32.7 %all-to-all-start = ((f32[16,64,512]{2,1,0:T(8,128)}), f32[16,64,512]{2,1,0:T(8,128)}, u32[]{:S(2)}, u32[]{:S(2)}) async-start(f32[16,64,512]{2,1,0:T(8,128)} %maximum_select_fusion), calls=%async_computation | async-start | bytes 4194304 | tf_op jit(solution)/shard_map/all_to_all | solution.py:69
  86.4 19.2 %collective-permute-start.5 = (f32[1,512]{1,0:T(1,128)S(1)}, f32[1,512]{1,0:T(1,128)S(1)}, u32[]{:S(2)}, u32[]{:S(2)}) collective-permute-start(f32[1,512]{1,0:T(1,128)S(1)} %get-tuple-element.98), channel_id=1, source_target_pairs={{16,0},{32,16},{48,32},{64,48},{80,64},{96,80},{112,96},{128,112},... | collective-permute-start | bytes 6152 | tf_op jit(solution)/shard_map/ppermute | solution.py:25
  94.0 11.6 %collective-permute-start.4 = (f32[1,512]{1,0:T(1,128)S(1)}, f32[1,512]{1,0:T(1,128)S(1)}, u32[]{:S(2)}, u32[]{:S(2)}) collective-permute-start(f32[1,512]{1,0:T(1,128)S(1)} %get-tuple-element.99), channel_id=1, source_target_pairs={{0,16},{16,32},{32,48},{48,64},{64,80},{80,96},{96,112},{112,128},... | collective-permute-start | bytes 6152 | tf_op jit(solution)/shard_map/ppermute | solution.py:25
  109.8 12.3 %all-to-all-start.2 = ((f32[16,1,32]{2,1,0:T(1,128)}), f32[16,1,32]{2,1,0:T(1,128)S(1)}, u32[]{:S(2)}, u32[]{:S(2)}) async-start(f32[16,1,32]{2,1,0:T(1,128)} %broadcast_in_dim.81), calls=%async_computation.2 | async-start | bytes 16384 | tf_op jit(solution)/shard_map/all_to_all | solution.py:31
  124.1 16.4 %collective-permute-start.9 = (f32[1,512]{1,0:T(1,128)S(1)}, f32[1,512]{1,0:T(1,128)S(1)}, u32[]{:S(2)}, u32[]{:S(2)}) collective-permute-start(f32[1,512]{1,0:T(1,128)S(1)} %get-tuple-element.90), channel_id=1, source_target_pairs={{16,0},{32,16},{48,32},{64,48},{80,64},{96,80},{112,96},{128,112},... | collective-permute-start | bytes 6152 | tf_op jit(solution)/shard_map/ppermute | solution.py:25
  131.7 8.8 %collective-permute-start.8 = (f32[1,512]{1,0:T(1,128)S(1)}, f32[1,512]{1,0:T(1,128)S(1)}, u32[]{:S(2)}, u32[]{:S(2)}) collective-permute-start(f32[1,512]{1,0:T(1,128)S(1)} %get-tuple-element.91), channel_id=1, source_target_pairs={{0,16},{16,32},{32,48},{48,64},{64,80},{80,96},{96,112},{112,128},... | collective-permute-start | bytes 6152 | tf_op jit(solution)/shard_map/ppermute | solution.py:25
  144.7 11.6 %all-to-all-start.3 = ((f32[16,1,32]{2,1,0:T(1,128)}), f32[16,1,32]{2,1,0:T(1,128)S(1)}, u32[]{:S(2)}, u32[]{:S(2)}) async-start(f32[16,1,32]{2,1,0:T(1,128)} %broadcast_in_dim.82), calls=%async_computation.3 | async-start | bytes 16384 | tf_op jit(solution)/shard_map/all_to_all | solution.py:31
  158.3 16.4 %collective-permute-start.13 = (f32[1,512]{1,0:T(1,128)S(1)}, f32[1,512]{1,0:T(1,128)S(1)}, u32[]{:S(2)}, u32[]{:S(2)}) collective-permute-start(f32[1,512]{1,0:T(1,128)S(1)} %get-tuple-element.82), channel_id=1, source_target_pairs={{16,0},{32,16},{48,32},{64,48},{80,64},{96,80},{112,96},{128,112},... | collective-permute-start | bytes 6152 | tf_op jit(solution)/shard_map/ppermute | solution.py:25
  165.9 8.8 %collective-permute-start.12 = (f32[1,512]{1,0:T(1,128)S(1)}, f32[1,512]{1,0:T(1,128)S(1)}, u32[]{:S(2)}, u32[]{:S(2)}) collective-permute-start(f32[1,512]{1,0:T(1,128)S(1)} %get-tuple-element.83), channel_id=1, source_target_pairs={{0,16},{16,32},{32,48},{48,64},{64,80},{80,96},{96,112},{112,128},... | collective-permute-start | bytes 6152 | tf_op jit(solution)/shard_map/ppermute | solution.py:25
  178.9 11.6 %all-to-all-start.4 = ((f32[16,1,32]{2,1,0:T(1,128)}), f32[16,1,32]{2,1,0:T(1,128)S(1)}, u32[]{:S(2)}, u32[]{:S(2)}) async-start(f32[16,1,32]{2,1,0:T(1,128)} %broadcast_in_dim.83), calls=%async_computation.4 | async-start | bytes 16384 | tf_op jit(solution)/shard_map/all_to_all | solution.py:31
  192.5 16.4 %collective-permute-start.17 = (f32[1,512]{1,0:T(1,128)S(1)}, f32[1,512]{1,0:T(1,128)S(1)}, u32[]{:S(2)}, u32[]{:S(2)}) collective-permute-start(f32[1,512]{1,0:T(1,128)S(1)} %get-tuple-element.74), channel_id=1, source_target_pairs={{16,0},{32,16},{48,32},{64,48},{80,64},{96,80},{112,96},{128,112},... | collective-permute-start | bytes 6152 | tf_op jit(solution)/shard_map/ppermute | solution.py:25
  213.1 11.6 %all-to-all-start.5 = ((f32[16,1,32]{2,1,0:T(1,128)}), f32[16,1,32]{2,1,0:T(1,128)S(1)}, u32[]{:S(2)}, u32[]{:S(2)}) async-start(f32[16,1,32]{2,1,0:T(1,128)} %broadcast_in_dim.84), calls=%async_computation.5 | async-start | bytes 16384 | tf_op jit(solution)/shard_map/all_to_all | solution.py:31
  226.6 16.4 %collective-permute-start.21 = (f32[1,512]{1,0:T(1,128)S(1)}, f32[1,512]{1,0:T(1,128)S(1)}, u32[]{:S(2)}, u32[]{:S(2)}) collective-permute-start(f32[1,512]{1,0:T(1,128)S(1)} %get-tuple-element.66), channel_id=1, source_target_pairs={{16,0},{32,16},{48,32},{64,48},{80,64},{96,80},{112,96},{128,112},... | collective-permute-start | bytes 6152 | tf_op jit(solution)/shard_map/ppermute | solution.py:25
  247.3 11.6 %all-to-all-start.6 = ((f32[16,1,32]{2,1,0:T(1,128)}), f32[16,1,32]{2,1,0:T(1,128)S(1)}, u32[]{:S(2)}, u32[]{:S(2)}) async-start(f32[16,1,32]{2,1,0:T(1,128)} %broadcast_in_dim.85), calls=%async_computation.6 | async-start | bytes 16384 | tf_op jit(solution)/shard_map/all_to_all | solution.py:31
  270.0 18.5 %all-to-all-start.8 = ((f32[32,1,128]{2,1,0:T(1,128)}), f32[32,1,128]{2,1,0:T(1,128)S(1)}, u32[]{:S(2)}, u32[]{:S(2)}) async-start(f32[32,1,128]{2,1,0:T(1,128)} %broadcast_in_dim.87), calls=%async_computation.8 | async-start | bytes 32768 | tf_op jit(solution)/shard_map/all_to_all | solution.py:31
  291.5 10.2 %all-to-all-start.9 = ((f32[16,1,32]{2,1,0:T(1,128)}), f32[16,1,32]{2,1,0:T(1,128)S(1)}, u32[]{:S(2)}, u32[]{:S(2)}) async-start(f32[16,1,32]{2,1,0:T(1,128)} %broadcast_in_dim.88), calls=%async_computation.9 | async-start | bytes 16384 | tf_op jit(solution)/shard_map/all_to_all | solution.py:31
  306.4 14.0 %collective-permute-start.25 = (f32[1,512]{1,0:T(1,128)S(1)}, f32[1,512]{1,0:T(1,128)S(1)}, u32[]{:S(2)}, u32[]{:S(2)}) collective-permute-start(f32[1,512]{1,0:T(1,128)S(1)} %get-tuple-element.58), channel_id=1, source_target_pairs={{16,0},{32,16},{48,32},{64,48},{80,64},{96,80},{112,96},{128,112},... | collective-permute-start | bytes 6152 | tf_op jit(solution)/shard_map/ppermute | solution.py:25
  321.9 11.6 %all-to-all-start.10 = ((f32[16,1,32]{2,1,0:T(1,128)}), f32[16,1,32]{2,1,0:T(1,128)S(1)}, u32[]{:S(2)}, u32[]{:S(2)}) async-start(f32[16,1,32]{2,1,0:T(1,128)} %broadcast_in_dim.89), calls=%async_computation.10 | async-start | bytes 16384 | tf_op jit(solution)/shard_map/all_to_all | solution.py:31
  338.2 16.4 %collective-permute-start.29 = (f32[1,512]{1,0:T(1,128)S(1)}, f32[1,512]{1,0:T(1,128)S(1)}, u32[]{:S(2)}, u32[]{:S(2)}) collective-permute-start(f32[1,512]{1,0:T(1,128)S(1)} %get-tuple-element.50), channel_id=1, source_target_pairs={{16,0},{32,16},{48,32},{64,48},{80,64},{96,80},{112,96},{128,112},... | collective-permute-start | bytes 6152 | tf_op jit(solution)/shard_map/ppermute | solution.py:25
  356.2 11.6 %all-to-all-start.11 = ((f32[16,1,32]{2,1,0:T(1,128)}), f32[16,1,32]{2,1,0:T(1,128)S(1)}, u32[]{:S(2)}, u32[]{:S(2)}) async-start(f32[16,1,32]{2,1,0:T(1,128)} %broadcast_in_dim.90), calls=%async_computation.11 | async-start | bytes 16384 | tf_op jit(solution)/shard_map/all_to_all | solution.py:31
  372.4 16.4 %collective-permute-start.33 = (f32[1,512]{1,0:T(1,128)S(1)}, f32[1,512]{1,0:T(1,128)S(1)}, u32[]{:S(2)}, u32[]{:S(2)}) collective-permute-start(f32[1,512]{1,0:T(1,128)S(1)} %get-tuple-element.42), channel_id=1, source_target_pairs={{16,0},{32,16},{48,32},{64,48},{80,64},{96,80},{112,96},{128,112},... | collective-permute-start | bytes 6152 | tf_op jit(solution)/shard_map/ppermute | solution.py:25
  390.4 11.6 %all-to-all-start.12 = ((f32[16,1,32]{2,1,0:T(1,128)}), f32[16,1,32]{2,1,0:T(1,128)S(1)}, u32[]{:S(2)}, u32[]{:S(2)}) async-start(f32[16,1,32]{2,1,0:T(1,128)} %broadcast_in_dim.91), calls=%async_computation.12 | async-start | bytes 16384 | tf_op jit(solution)/shard_map/all_to_all | solution.py:31
  406.7 16.4 %collective-permute-start.37 = (f32[1,512]{1,0:T(1,128)S(1)}, f32[1,512]{1,0:T(1,128)S(1)}, u32[]{:S(2)}, u32[]{:S(2)}) collective-permute-start(f32[1,512]{1,0:T(1,128)S(1)} %get-tuple-element.34), channel_id=1, source_target_pairs={{16,0},{32,16},{48,32},{64,48},{80,64},{96,80},{112,96},{128,112},... | collective-permute-start | bytes 6152 | tf_op jit(solution)/shard_map/ppermute | solution.py:25
  424.7 11.6 %all-to-all-start.13 = ((f32[16,1,32]{2,1,0:T(1,128)}), f32[16,1,32]{2,1,0:T(1,128)S(1)}, u32[]{:S(2)}, u32[]{:S(2)}) async-start(f32[16,1,32]{2,1,0:T(1,128)} %broadcast_in_dim.92), calls=%async_computation.13 | async-start | bytes 16384 | tf_op jit(solution)/shard_map/all_to_all | solution.py:31
  440.9 16.4 %collective-permute-start.41 = (f32[1,512]{1,0:T(1,128)S(1)}, f32[1,512]{1,0:T(1,128)S(1)}, u32[]{:S(2)}, u32[]{:S(2)}) collective-permute-start(f32[1,512]{1,0:T(1,128)S(1)} %get-tuple-element.26), channel_id=1, source_target_pairs={{16,0},{32,16},{48,32},{64,48},{80,64},{96,80},{112,96},{128,112},... | collective-permute-start | bytes 6152 | tf_op jit(solution)/shard_map/ppermute | solution.py:25
  458.9 11.6 %all-to-all-start.14 = ((f32[16,1,32]{2,1,0:T(1,128)}), f32[16,1,32]{2,1,0:T(1,128)S(1)}, u32[]{:S(2)}, u32[]{:S(2)}) async-start(f32[16,1,32]{2,1,0:T(1,128)} %broadcast_in_dim.93), calls=%async_computation.14 | async-start | bytes 16384 | tf_op jit(solution)/shard_map/all_to_all | solution.py:31
  476.0 9.4 %all-to-all-start.15 = ((f32[16,1,64]{2,1,0:T(1,128)}), f32[16,1,64]{2,1,0:T(1,128)S(1)}, u32[]{:S(2)}, u32[]{:S(2)}) async-start(f32[16,1,64]{2,1,0:T(1,128)} %broadcast_in_dim.95), calls=%async_computation.15 | async-start | bytes 16384 | tf_op jit(solution)/shard_map/all_to_all | solution.py:31
  (41 other events, 613.6 us)

commit v5 on v4

--- a/solution.py
+++ b/solution.py
@@ -107,7 +107,7 @@
             result = jnp.dot(scaled, band_tile, precision=HIGH)
         picked = resid.reshape(-1)[places]
         if first:
-            picked, _ = lax.optimization_barrier((picked, row_slab))
+            picked = picked + 0.0 * row_slab[0, 0]
         values = gather_all(picked, "plate").reshape(-1)
         slab = col_slab if transpose else row_slab
         mine = jnp.dot(slab, values, precision=HIGH)

time: 489 us -> 452 us (0.924)
  waiting for transfers between devices: 90.9 us -> 63.5 us
  local copies, waits for them, and re-layouts: 35.6 us -> 29.3 us
    all_to_all x1, waiting for transfers between devices: 24.7 us -> 0.01 us  [panel_slabs(): got = jnp.sum(lax.all_to_all(sent, 'plate', 0, 0, tiled=False), axis=0)]
  transfers between devices with their start and end apart: 59 -> 59, of which waited for: 34 -> 25; matrix products, arithmetic and copies ran while one was open for 6% -> 4% of each run, Pallas kernels for 0% -> 0%
where the time goes in v5:
time: 452 us; the launch traced here: 448 us
  starting transfers between devices  270 us (60%)
  waiting for transfers between devices  63.5 us (14%)
  other arithmetic  60.3 us (13%)
  local copies, waits for them, and re-layouts  29.3 us (6%)
  matrix products  13 us (3%)
  blocking collectives  8.6 us (2%)
    ppermute x44, starting transfers between devices, shifted(): return lax.ppermute(edge, axis, pairs)  164 us
    all_to_all x14, starting transfers between devices, gather_all(): return lax.all_to_all(spread, axis, 0, 0, tiled=False)  99.1 us
    all_to_all x14, waiting for transfers between devices, gather_all(): return lax.all_to_all(spread, axis, 0, 0, tiled=False)  53.7 us
    sub x6, other arithmetic, on_device(): resid = load - (diag * new_disp - stiff * neighbours(new_disp))  15.9 us
    mul x5, other arithmetic, on_device(): resid = target - (diag * adjoint - neighbours(stiff * adjoint))  12.6 us
    scatter-add x12, other arithmetic, correct(): return result.reshape(-1).at[places].add(mine).reshape(rows, cols)  10.7 us
    ppermute x44, waiting for transfers between devices, shifted(): return lax.ppermute(edge, axis, pairs)  9.76 us
  transfers between devices with their start and end apart: 59, of which 25 were waited for; matrix products, arithmetic and copies ran while one was open for 4% of the time, Pallas kernels for 0%

profile of v5, /device:TPU:7, one launch (start us, length us, event | category | flops | bytes accessed | tf_op | source)
XLA Modules:
  0.0 448.3 jit_solution(8694226998494335026)
XLA Ops:
  6.9 6.4 %all-to-all-start = ((f32[16,64,512]{2,1,0:T(8,128)}), f32[16,64,512]{2,1,0:T(8,128)}, u32[]{:S(2)}, u32[]{:S(2)}) async-start(f32[16,64,512]{2,1,0:T(8,128)} %maximum_select_fusion), calls=%async_computation | async-start | bytes 4194304 | tf_op jit(solution)/shard_map/all_to_all | solution.py:69
  18.9 3.5 collective-permute-start
  22.4 10.3 %collective-permute-start.1 = (f32[1,512]{1,0:T(1,128)S(1)}, f32[1,512]{1,0:T(1,128)S(1)}, u32[]{:S(2)}, u32[]{:S(2)}) collective-permute-start(f32[1,512]{1,0:T(1,128)S(1)} %get-tuple-element.104), channel_id=1, source_target_pairs={{16,0},{32,16},{48,32},{64,48},{80,64},{96,80},{112,96},{128,112},... | collective-permute-start | bytes 6152 | tf_op jit(solution)/shard_map/ppermute | solution.py:25
  45.8 5.7 %all-to-all-start.1 = ((f32[16,1,32]{2,1,0:T(1,128)}), f32[16,1,32]{2,1,0:T(1,128)S(1)}, u32[]{:S(2)}, u32[]{:S(2)}) async-start(f32[16,1,32]{2,1,0:T(1,128)} %broadcast_in_dim.80), calls=%async_computation.1 | async-start | bytes 16384 | tf_op jit(solution)/shard_map/all_to_all | solution.py:31
  63.3 3.5 collective-permute-start.4
  66.9 10.3 %collective-permute-start.5 = (f32[1,512]{1,0:T(1,128)S(1)}, f32[1,512]{1,0:T(1,128)S(1)}, u32[]{:S(2)}, u32[]{:S(2)}) collective-permute-start(f32[1,512]{1,0:T(1,128)S(1)} %get-tuple-element.96), channel_id=1, source_target_pairs={{16,0},{32,16},{48,32},{64,48},{80,64},{96,80},{112,96},{128,112},... | collective-permute-start | bytes 6152 | tf_op jit(solution)/shard_map/ppermute | solution.py:25
  81.9 7.5 %all-to-all-start.2 = ((f32[16,1,32]{2,1,0:T(1,128)}), f32[16,1,32]{2,1,0:T(1,128)S(1)}, u32[]{:S(2)}, u32[]{:S(2)}) async-start(f32[16,1,32]{2,1,0:T(1,128)} %broadcast_in_dim.81), calls=%async_computation.2 | async-start | bytes 16384 | tf_op jit(solution)/shard_map/all_to_all | solution.py:31
  102.5 7.5 %collective-permute-start.9 = (f32[1,512]{1,0:T(1,128)S(1)}, f32[1,512]{1,0:T(1,128)S(1)}, u32[]{:S(2)}, u32[]{:S(2)}) collective-permute-start(f32[1,512]{1,0:T(1,128)S(1)} %get-tuple-element.88), channel_id=1, source_target_pairs={{16,0},{32,16},{48,32},{64,48},{80,64},{96,80},{112,96},{128,112},... | collective-permute-start | bytes 6152 | tf_op jit(solution)/shard_map/ppermute | solution.py:25
  114.8 7.5 %all-to-all-start.3 = ((f32[16,1,32]{2,1,0:T(1,128)}), f32[16,1,32]{2,1,0:T(1,128)S(1)}, u32[]{:S(2)}, u32[]{:S(2)}) async-start(f32[16,1,32]{2,1,0:T(1,128)} %broadcast_in_dim.82), calls=%async_computation.3 | async-start | bytes 16384 | tf_op jit(solution)/shard_map/all_to_all | solution.py:31
  123.1 3.5 all-to-all-done.3
  135.4 7.5 %collective-permute-start.13 = (f32[1,512]{1,0:T(1,128)S(1)}, f32[1,512]{1,0:T(1,128)S(1)}, u32[]{:S(2)}, u32[]{:S(2)}) collective-permute-start(f32[1,512]{1,0:T(1,128)S(1)} %get-tuple-element.80), channel_id=1, source_target_pairs={{16,0},{32,16},{48,32},{64,48},{80,64},{96,80},{112,96},{128,112},... | collective-permute-start | bytes 6152 | tf_op jit(solution)/shard_map/ppermute | solution.py:25
  147.6 7.5 %all-to-all-start.4 = ((f32[16,1,32]{2,1,0:T(1,128)}), f32[16,1,32]{2,1,0:T(1,128)S(1)}, u32[]{:S(2)}, u32[]{:S(2)}) async-start(f32[16,1,32]{2,1,0:T(1,128)} %broadcast_in_dim.83), calls=%async_computation.4 | async-start | bytes 16384 | tf_op jit(solution)/shard_map/all_to_all | solution.py:31
  155.9 3.5 all-to-all-done.4
  168.2 7.5 %collective-permute-start.17 = (f32[1,512]{1,0:T(1,128)S(1)}, f32[1,512]{1,0:T(1,128)S(1)}, u32[]{:S(2)}, u32[]{:S(2)}) collective-permute-start(f32[1,512]{1,0:T(1,128)S(1)} %get-tuple-element.72), channel_id=1, source_target_pairs={{16,0},{32,16},{48,32},{64,48},{80,64},{96,80},{112,96},{128,112},... | collective-permute-start | bytes 6152 | tf_op jit(solution)/shard_map/ppermute | solution.py:25
  180.5 7.5 %all-to-all-start.5 = ((f32[16,1,32]{2,1,0:T(1,128)}), f32[16,1,32]{2,1,0:T(1,128)S(1)}, u32[]{:S(2)}, u32[]{:S(2)}) async-start(f32[16,1,32]{2,1,0:T(1,128)} %broadcast_in_dim.84), calls=%async_computation.5 | async-start | bytes 16384 | tf_op jit(solution)/shard_map/all_to_all | solution.py:31
  201.1 7.5 %collective-permute-start.21 = (f32[1,512]{1,0:T(1,128)S(1)}, f32[1,512]{1,0:T(1,128)S(1)}, u32[]{:S(2)}, u32[]{:S(2)}) collective-permute-start(f32[1,512]{1,0:T(1,128)S(1)} %get-tuple-element.64), channel_id=1, source_target_pairs={{16,0},{32,16},{48,32},{64,48},{80,64},{96,80},{112,96},{128,112},... | collective-permute-start | bytes 6152 | tf_op jit(solution)/shard_map/ppermute | solution.py:25
  213.3 7.5 %all-to-all-start.6 = ((f32[16,1,32]{2,1,0:T(1,128)}), f32[16,1,32]{2,1,0:T(1,128)S(1)}, u32[]{:S(2)}, u32[]{:S(2)}) async-start(f32[16,1,32]{2,1,0:T(1,128)} %broadcast_in_dim.85), calls=%async_computation.6 | async-start | bytes 16384 | tf_op jit(solution)/shard_map/all_to_all | solution.py:31
  227.2 8.6 %all_to_all.95 = f32[16,1,128]{2,1,0:T(1,128)S(1)} all-to-all(f32[16,1,128]{2,1,0:T(1,128)S(1)} %broadcast_in_dim.86), channel_id=1, replica_groups=mesh['storey'=32,'plate'=16] {'plate'}, dimensions={0} | all-to-all | bytes 16384 | tf_op jit(solution)/shard_map/all_to_all | solution.py:31
  236.4 7.3 %all-to-all-start.8 = ((f32[32,1,128]{2,1,0:T(1,128)}), f32[32,1,128]{2,1,0:T(1,128)S(1)}, u32[]{:S(2)}, u32[]{:S(2)}) async-start(f32[32,1,128]{2,1,0:T(1,128)} %broadcast_in_dim.87), calls=%async_computation.8 | async-start | bytes 32768 | tf_op jit(solution)/shard_map/all_to_all | solution.py:31
  243.7 11.1 %all-to-all-done.8 = f32[32,1,128]{2,1,0:T(1,128)S(1)} async-done(((f32[32,1,128]{2,1,0:T(1,128)}), f32[32,1,128]{2,1,0:T(1,128)S(1)}, u32[]{:S(2)}, u32[]{:S(2)}) %all-to-all-start.8) | async-done | bytes 16416 | tf_op jit(solution)/shard_map/all_to_all | solution.py:31
  258.1 5.9 %all-to-all-start.9 = ((f32[16,1,32]{2,1,0:T(1,128)}), f32[16,1,32]{2,1,0:T(1,128)S(1)}, u32[]{:S(2)}, u32[]{:S(2)}) async-start(f32[16,1,32]{2,1,0:T(1,128)} %broadcast_in_dim.88), calls=%async_computation.9 | async-start | bytes 16384 | tf_op jit(solution)/shard_map/all_to_all | solution.py:31
  279.8 6.8 %collective-permute-start.25 = (f32[1,512]{1,0:T(1,128)S(1)}, f32[1,512]{1,0:T(1,128)S(1)}, u32[]{:S(2)}, u32[]{:S(2)}) collective-permute-start(f32[1,512]{1,0:T(1,128)S(1)} %get-tuple-element.56), channel_id=1, source_target_pairs={{16,0},{32,16},{48,32},{64,48},{80,64},{96,80},{112,96},{128,112},... | collective-permute-start | bytes 6152 | tf_op jit(solution)/shard_map/ppermute | solution.py:25
  289.0 7.8 %all-to-all-start.10 = ((f32[16,1,32]{2,1,0:T(1,128)}), f32[16,1,32]{2,1,0:T(1,128)S(1)}, u32[]{:S(2)}, u32[]{:S(2)}) async-start(f32[16,1,32]{2,1,0:T(1,128)} %broadcast_in_dim.89), calls=%async_computation.10 | async-start | bytes 16384 | tf_op jit(solution)/shard_map/all_to_all | solution.py:31
  312.3 7.5 %collective-permute-start.29 = (f32[1,512]{1,0:T(1,128)S(1)}, f32[1,512]{1,0:T(1,128)S(1)}, u32[]{:S(2)}, u32[]{:S(2)}) collective-permute-start(f32[1,512]{1,0:T(1,128)S(1)} %get-tuple-element.48), channel_id=1, source_target_pairs={{16,0},{32,16},{48,32},{64,48},{80,64},{96,80},{112,96},{128,112},... | collective-permute-start | bytes 6152 | tf_op jit(solution)/shard_map/ppermute | solution.py:25
  322.1 7.5 %all-to-all-start.11 = ((f32[16,1,32]{2,1,0:T(1,128)}), f32[16,1,32]{2,1,0:T(1,128)S(1)}, u32[]{:S(2)}, u32[]{:S(2)}) async-start(f32[16,1,32]{2,1,0:T(1,128)} %broadcast_in_dim.90), calls=%async_computation.11 | async-start | bytes 16384 | tf_op jit(solution)/shard_map/all_to_all | solution.py:31
  345.2 7.5 %collective-permute-start.33 = (f32[1,512]{1,0:T(1,128)S(1)}, f32[1,512]{1,0:T(1,128)S(1)}, u32[]{:S(2)}, u32[]{:S(2)}) collective-permute-start(f32[1,512]{1,0:T(1,128)S(1)} %get-tuple-element.40), channel_id=1, source_target_pairs={{16,0},{32,16},{48,32},{64,48},{80,64},{96,80},{112,96},{128,112},... | collective-permute-start | bytes 6152 | tf_op jit(solution)/shard_map/ppermute | solution.py:25
  355.1 7.5 %all-to-all-start.12 = ((f32[16,1,32]{2,1,0:T(1,128)}), f32[16,1,32]{2,1,0:T(1,128)S(1)}, u32[]{:S(2)}, u32[]{:S(2)}) async-start(f32[16,1,32]{2,1,0:T(1,128)} %broadcast_in_dim.91), calls=%async_computation.12 | async-start | bytes 16384 | tf_op jit(solution)/shard_map/all_to_all | solution.py:31
  378.1 7.5 %collective-permute-start.37 = (f32[1,512]{1,0:T(1,128)S(1)}, f32[1,512]{1,0:T(1,128)S(1)}, u32[]{:S(2)}, u32[]{:S(2)}) collective-permute-start(f32[1,512]{1,0:T(1,128)S(1)} %get-tuple-element.32), channel_id=1, source_target_pairs={{16,0},{32,16},{48,32},{64,48},{80,64},{96,80},{112,96},{128,112},... | collective-permute-start | bytes 6152 | tf_op jit(solution)/shard_map/ppermute | solution.py:25
  388.0 7.5 %all-to-all-start.13 = ((f32[16,1,32]{2,1,0:T(1,128)}), f32[16,1,32]{2,1,0:T(1,128)S(1)}, u32[]{:S(2)}, u32[]{:S(2)}) async-start(f32[16,1,32]{2,1,0:T(1,128)} %broadcast_in_dim.92), calls=%async_computation.13 | async-start | bytes 16384 | tf_op jit(solution)/shard_map/all_to_all | solution.py:31
  411.0 7.5 %collective-permute-start.41 = (f32[1,512]{1,0:T(1,128)S(1)}, f32[1,512]{1,0:T(1,128)S(1)}, u32[]{:S(2)}, u32[]{:S(2)}) collective-permute-start(f32[1,512]{1,0:T(1,128)S(1)} %get-tuple-element.24), channel_id=1, source_target_pairs={{16,0},{32,16},{48,32},{64,48},{80,64},{96,80},{112,96},{128,112},... | collective-permute-start | bytes 6152 | tf_op jit(solution)/shard_map/ppermute | solution.py:25
  420.9 7.5 %all-to-all-start.14 = ((f32[16,1,32]{2,1,0:T(1,128)}), f32[16,1,32]{2,1,0:T(1,128)S(1)}, u32[]{:S(2)}, u32[]{:S(2)}) async-start(f32[16,1,32]{2,1,0:T(1,128)} %broadcast_in_dim.93), calls=%async_computation.14 | async-start | bytes 16384 | tf_op jit(solution)/shard_map/all_to_all | solution.py:31
  438.2 5.1 %all-to-all-start.15 = ((f32[16,1,64]{2,1,0:T(1,128)}), f32[16,1,64]{2,1,0:T(1,128)S(1)}, u32[]{:S(2)}, u32[]{:S(2)}) async-start(f32[16,1,64]{2,1,0:T(1,128)} %broadcast_in_dim.95), calls=%async_computation.15 | async-start | bytes 16384 | tf_op jit(solution)/shard_map/all_to_all | solution.py:31
  (331 shorter events, 217.5 us)
Async XLA Ops:
  6.9 35.3 %all-to-all-start = ((f32[16,64,512]{2,1,0:T(8,128)}), f32[16,64,512]{2,1,0:T(8,128)}, u32[]{:S(2)}, u32[]{:S(2)}) async-start(f32[16,64,512]{2,1,0:T(8,128)} %maximum_select_fusion), calls=%async_computation | async-start | bytes 4194304 | tf_op jit(solution)/shard_map/all_to_all | solution.py:69
  13.4 25.3 %collective-permute-start.2 = (f32[128,1]{1,0:T(8,128)S(1)}, f32[128,1]{1,0:T(8,128)S(1)}, u32[]{:S(2)}, u32[]{:S(2)}) collective-permute-start(f32[128,1]{1,0:T(8,128)S(1)} %get-tuple-element.101), channel_id=1, source_target_pairs={{0,1},{1,2},{2,3},{3,4},{4,5},{5,6},{6,7},{7,8},{8,9},{9,10},{10,1... | collective-permute-start | bytes 1544 | tf_op jit(solution)/shard_map/ppermute | solution.py:25
  16.9 21.8 %collective-permute-start.3 = (f32[128,1]{1,0:T(8,128)S(1)}, f32[128,1]{1,0:T(8,128)S(1)}, u32[]{:S(2)}, u32[]{:S(2)}) collective-permute-start(f32[128,1]{1,0:T(8,128)S(1)} %get-tuple-element.100), channel_id=1, source_target_pairs={{1,0},{2,1},{3,2},{4,3},{5,4},{6,5},{7,6},{8,7},{9,8},{10,9},{11,1... | collective-permute-start | bytes 1544 | tf_op jit(solution)/shard_map/ppermute | solution.py:25
  18.9 19.9 %collective-permute-start = (f32[1,512]{1,0:T(1,128)S(1)}, f32[1,512]{1,0:T(1,128)S(1)}, u32[]{:S(2)}, u32[]{:S(2)}) collective-permute-start(f32[1,512]{1,0:T(1,128)S(1)} %get-tuple-element.105), channel_id=1, source_target_pairs={{0,16},{16,32},{32,48},{48,64},{64,80},{80,96},{96,112},{112,128},... | collective-permute-start | bytes 6152 | tf_op jit(solution)/shard_map/ppermute | solution.py:25
  22.4 16.3 %collective-permute-start.1 = (f32[1,512]{1,0:T(1,128)S(1)}, f32[1,512]{1,0:T(1,128)S(1)}, u32[]{:S(2)}, u32[]{:S(2)}) collective-permute-start(f32[1,512]{1,0:T(1,128)S(1)} %get-tuple-element.104), channel_id=1, source_target_pairs={{16,0},{32,16},{48,32},{64,48},{80,64},{96,80},{112,96},{128,112},... | collective-permute-start | bytes 6152 | tf_op jit(solution)/shard_map/ppermute | solution.py:25
  58.6 18.6 %collective-permute-start.6 = (f32[128,1]{1,0:T(8,128)S(1)}, f32[128,1]{1,0:T(8,128)S(1)}, u32[]{:S(2)}, u32[]{:S(2)}) collective-permute-start(f32[128,1]{1,0:T(8,128)S(1)} %get-tuple-element.93), channel_id=1, source_target_pairs={{0,1},{1,2},{2,3},{3,4},{4,5},{5,6},{6,7},{7,8},{8,9},{9,10},{10,1... | collective-permute-start | bytes 1544 | tf_op jit(solution)/shard_map/ppermute | solution.py:25
  61.4 15.9 %collective-permute-start.7 = (f32[128,1]{1,0:T(8,128)S(1)}, f32[128,1]{1,0:T(8,128)S(1)}, u32[]{:S(2)}, u32[]{:S(2)}) collective-permute-start(f32[128,1]{1,0:T(8,128)S(1)} %get-tuple-element.92), channel_id=1, source_target_pairs={{1,0},{2,1},{3,2},{4,3},{5,4},{6,5},{7,6},{8,7},{9,8},{10,9},{11,1... | collective-permute-start | bytes 1544 | tf_op jit(solution)/shard_map/ppermute | solution.py:25
  63.3 14.0 %collective-permute-start.4 = (f32[1,512]{1,0:T(1,128)S(1)}, f32[1,512]{1,0:T(1,128)S(1)}, u32[]{:S(2)}, u32[]{:S(2)}) collective-permute-start(f32[1,512]{1,0:T(1,128)S(1)} %get-tuple-element.97), channel_id=1, source_target_pairs={{0,16},{16,32},{32,48},{48,64},{64,80},{80,96},{96,112},{112,128},... | collective-permute-start | bytes 6152 | tf_op jit(solution)/shard_map/ppermute | solution.py:25
  81.9 11.8 %all-to-all-start.2 = ((f32[16,1,32]{2,1,0:T(1,128)}), f32[16,1,32]{2,1,0:T(1,128)S(1)}, u32[]{:S(2)}, u32[]{:S(2)}) async-start(f32[16,1,32]{2,1,0:T(1,128)} %broadcast_in_dim.81), calls=%async_computation.2 | async-start | bytes 16384 | tf_op jit(solution)/shard_map/all_to_all | solution.py:31
  95.9 14.2 %collective-permute-start.10 = (f32[128,1]{1,0:T(8,128)S(1)}, f32[128,1]{1,0:T(8,128)S(1)}, u32[]{:S(2)}, u32[]{:S(2)}) collective-permute-start(f32[128,1]{1,0:T(8,128)S(1)} %get-tuple-element.85), channel_id=1, source_target_pairs={{0,1},{1,2},{2,3},{3,4},{4,5},{5,6},{6,7},{7,8},{8,9},{9,10},{10,1... | collective-permute-start | bytes 1544 | tf_op jit(solution)/shard_map/ppermute | solution.py:25
  98.7 11.4 %collective-permute-start.11 = (f32[128,1]{1,0:T(8,128)S(1)}, f32[128,1]{1,0:T(8,128)S(1)}, u32[]{:S(2)}, u32[]{:S(2)}) collective-permute-start(f32[128,1]{1,0:T(8,128)S(1)} %get-tuple-element.84), channel_id=1, source_target_pairs={{1,0},{2,1},{3,2},{4,3},{5,4},{6,5},{7,6},{8,7},{9,8},{10,9},{11,1... | collective-permute-start | bytes 1544 | tf_op jit(solution)/shard_map/ppermute | solution.py:25
  114.8 11.8 %all-to-all-start.3 = ((f32[16,1,32]{2,1,0:T(1,128)}), f32[16,1,32]{2,1,0:T(1,128)S(1)}, u32[]{:S(2)}, u32[]{:S(2)}) async-start(f32[16,1,32]{2,1,0:T(1,128)} %broadcast_in_dim.82), calls=%async_computation.3 | async-start | bytes 16384 | tf_op jit(solution)/shard_map/all_to_all | solution.py:31
  128.8 14.2 %collective-permute-start.14 = (f32[128,1]{1,0:T(8,128)S(1)}, f32[128,1]{1,0:T(8,128)S(1)}, u32[]{:S(2)}, u32[]{:S(2)}) collective-permute-start(f32[128,1]{1,0:T(8,128)S(1)} %get-tuple-element.77), channel_id=1, source_target_pairs={{0,1},{1,2},{2,3},{3,4},{4,5},{5,6},{6,7},{7,8},{8,9},{9,10},{10,1... | collective-permute-start | bytes 1544 | tf_op jit(solution)/shard_map/ppermute | solution.py:25
  131.5 11.4 %collective-permute-start.15 = (f32[128,1]{1,0:T(8,128)S(1)}, f32[128,1]{1,0:T(8,128)S(1)}, u32[]{:S(2)}, u32[]{:S(2)}) collective-permute-start(f32[128,1]{1,0:T(8,128)S(1)} %get-tuple-element.76), channel_id=1, source_target_pairs={{1,0},{2,1},{3,2},{4,3},{5,4},{6,5},{7,6},{8,7},{9,8},{10,9},{11,1... | collective-permute-start | bytes 1544 | tf_op jit(solution)/shard_map/ppermute | solution.py:25
  147.6 11.8 %all-to-all-start.4 = ((f32[16,1,32]{2,1,0:T(1,128)}), f32[16,1,32]{2,1,0:T(1,128)S(1)}, u32[]{:S(2)}, u32[]{:S(2)}) async-start(f32[16,1,32]{2,1,0:T(1,128)} %broadcast_in_dim.83), calls=%async_computation.4 | async-start | bytes 16384 | tf_op jit(solution)/shard_map/all_to_all | solution.py:31
  161.6 14.2 %collective-permute-start.18 = (f32[128,1]{1,0:T(8,128)S(1)}, f32[128,1]{1,0:T(8,128)S(1)}, u32[]{:S(2)}, u32[]{:S(2)}) collective-permute-start(f32[128,1]{1,0:T(8,128)S(1)} %get-tuple-element.69), channel_id=1, source_target_pairs={{0,1},{1,2},{2,3},{3,4},{4,5},{5,6},{6,7},{7,8},{8,9},{9,10},{10,1... | collective-permute-start | bytes 1544 | tf_op jit(solution)/shard_map/ppermute | solution.py:25
  164.4 11.4 %collective-permute-start.19 = (f32[128,1]{1,0:T(8,128)S(1)}, f32[128,1]{1,0:T(8,128)S(1)}, u32[]{:S(2)}, u32[]{:S(2)}) collective-permute-start(f32[128,1]{1,0:T(8,128)S(1)} %get-tuple-element.68), channel_id=1, source_target_pairs={{1,0},{2,1},{3,2},{4,3},{5,4},{6,5},{7,6},{8,7},{9,8},{10,9},{11,1... | collective-permute-start | bytes 1544 | tf_op jit(solution)/shard_map/ppermute | solution.py:25
  180.5 11.8 %all-to-all-start.5 = ((f32[16,1,32]{2,1,0:T(1,128)}), f32[16,1,32]{2,1,0:T(1,128)S(1)}, u32[]{:S(2)}, u32[]{:S(2)}) async-start(f32[16,1,32]{2,1,0:T(1,128)} %broadcast_in_dim.84), calls=%async_computation.5 | async-start | bytes 16384 | tf_op jit(solution)/shard_map/all_to_all | solution.py:31
  194.4 14.2 %collective-permute-start.22 = (f32[128,1]{1,0:T(8,128)S(1)}, f32[128,1]{1,0:T(8,128)S(1)}, u32[]{:S(2)}, u32[]{:S(2)}) collective-permute-start(f32[128,1]{1,0:T(8,128)S(1)} %get-tuple-element.61), channel_id=1, source_target_pairs={{0,1},{1,2},{2,3},{3,4},{4,5},{5,6},{6,7},{7,8},{8,9},{9,10},{10,1... | collective-permute-start | bytes 1544 | tf_op jit(solution)/shard_map/ppermute | solution.py:25
  197.2 11.4 %collective-permute-start.23 = (f32[128,1]{1,0:T(8,128)S(1)}, f32[128,1]{1,0:T(8,128)S(1)}, u32[]{:S(2)}, u32[]{:S(2)}) collective-permute-start(f32[128,1]{1,0:T(8,128)S(1)} %get-tuple-element.60), channel_id=1, source_target_pairs={{1,0},{2,1},{3,2},{4,3},{5,4},{6,5},{7,6},{8,7},{9,8},{10,9},{11,1... | collective-permute-start | bytes 1544 | tf_op jit(solution)/shard_map/ppermute | solution.py:25
  213.3 11.8 %all-to-all-start.6 = ((f32[16,1,32]{2,1,0:T(1,128)}), f32[16,1,32]{2,1,0:T(1,128)S(1)}, u32[]{:S(2)}, u32[]{:S(2)}) async-start(f32[16,1,32]{2,1,0:T(1,128)} %broadcast_in_dim.85), calls=%async_computation.6 | async-start | bytes 16384 | tf_op jit(solution)/shard_map/all_to_all | solution.py:31
  236.4 18.5 %all-to-all-start.8 = ((f32[32,1,128]{2,1,0:T(1,128)}), f32[32,1,128]{2,1,0:T(1,128)S(1)}, u32[]{:S(2)}, u32[]{:S(2)}) async-start(f32[32,1,128]{2,1,0:T(1,128)} %broadcast_in_dim.87), calls=%async_computation.8 | async-start | bytes 32768 | tf_op jit(solution)/shard_map/all_to_all | solution.py:31
  273.0 13.7 %collective-permute-start.26 = (f32[128,1]{1,0:T(8,128)S(1)}, f32[128,1]{1,0:T(8,128)S(1)}, u32[]{:S(2)}, u32[]{:S(2)}) collective-permute-start(f32[128,1]{1,0:T(8,128)S(1)} %get-tuple-element.53), channel_id=1, source_target_pairs={{0,1},{1,2},{2,3},{3,4},{4,5},{5,6},{6,7},{7,8},{8,9},{9,10},{10,1... | collective-permute-start | bytes 1544 | tf_op jit(solution)/shard_map/ppermute | solution.py:25
  289.0 12.1 %all-to-all-start.10 = ((f32[16,1,32]{2,1,0:T(1,128)}), f32[16,1,32]{2,1,0:T(1,128)S(1)}, u32[]{:S(2)}, u32[]{:S(2)}) async-start(f32[16,1,32]{2,1,0:T(1,128)} %broadcast_in_dim.89), calls=%async_computation.10 | async-start | bytes 16384 | tf_op jit(solution)/shard_map/all_to_all | solution.py:31
  305.7 14.2 %collective-permute-start.30 = (f32[128,1]{1,0:T(8,128)S(1)}, f32[128,1]{1,0:T(8,128)S(1)}, u32[]{:S(2)}, u32[]{:S(2)}) collective-permute-start(f32[128,1]{1,0:T(8,128)S(1)} %get-tuple-element.45), channel_id=1, source_target_pairs={{0,1},{1,2},{2,3},{3,4},{4,5},{5,6},{6,7},{7,8},{8,9},{9,10},{10,1... | collective-permute-start | bytes 1544 | tf_op jit(solution)/shard_map/ppermute | solution.py:25
  322.1 11.8 %all-to-all-start.11 = ((f32[16,1,32]{2,1,0:T(1,128)}), f32[16,1,32]{2,1,0:T(1,128)S(1)}, u32[]{:S(2)}, u32[]{:S(2)}) async-start(f32[16,1,32]{2,1,0:T(1,128)} %broadcast_in_dim.90), calls=%async_computation.11 | async-start | bytes 16384 | tf_op jit(solution)/shard_map/all_to_all | solution.py:31
  338.6 14.2 %collective-permute-start.34 = (f32[128,1]{1,0:T(8,128)S(1)}, f32[128,1]{1,0:T(8,128)S(1)}, u32[]{:S(2)}, u32[]{:S(2)}) collective-permute-start(f32[128,1]{1,0:T(8,128)S(1)} %get-tuple-element.37), channel_id=1, source_target_pairs={{0,1},{1,2},{2,3},{3,4},{4,5},{5,6},{6,7},{7,8},{8,9},{9,10},{10,1... | collective-permute-start | bytes 1544 | tf_op jit(solution)/shard_map/ppermute | solution.py:25
  355.1 11.8 %all-to-all-start.12 = ((f32[16,1,32]{2,1,0:T(1,128)}), f32[16,1,32]{2,1,0:T(1,128)S(1)}, u32[]{:S(2)}, u32[]{:S(2)}) async-start(f32[16,1,32]{2,1,0:T(1,128)} %broadcast_in_dim.91), calls=%async_computation.12 | async-start | bytes 16384 | tf_op jit(solution)/shard_map/all_to_all | solution.py:31
  371.5 14.2 %collective-permute-start.38 = (f32[128,1]{1,0:T(8,128)S(1)}, f32[128,1]{1,0:T(8,128)S(1)}, u32[]{:S(2)}, u32[]{:S(2)}) collective-permute-start(f32[128,1]{1,0:T(8,128)S(1)} %get-tuple-element.29), channel_id=1, source_target_pairs={{0,1},{1,2},{2,3},{3,4},{4,5},{5,6},{6,7},{7,8},{8,9},{9,10},{10,1... | collective-permute-start | bytes 1544 | tf_op jit(solution)/shard_map/ppermute | solution.py:25
  388.0 11.8 %all-to-all-start.13 = ((f32[16,1,32]{2,1,0:T(1,128)}), f32[16,1,32]{2,1,0:T(1,128)S(1)}, u32[]{:S(2)}, u32[]{:S(2)}) async-start(f32[16,1,32]{2,1,0:T(1,128)} %broadcast_in_dim.92), calls=%async_computation.13 | async-start | bytes 16384 | tf_op jit(solution)/shard_map/all_to_all | solution.py:31
  404.4 14.2 %collective-permute-start.42 = (f32[128,1]{1,0:T(8,128)S(1)}, f32[128,1]{1,0:T(8,128)S(1)}, u32[]{:S(2)}, u32[]{:S(2)}) collective-permute-start(f32[128,1]{1,0:T(8,128)S(1)} %get-tuple-element.21), channel_id=1, source_target_pairs={{0,1},{1,2},{2,3},{3,4},{4,5},{5,6},{6,7},{7,8},{8,9},{9,10},{10,1... | collective-permute-start | bytes 1544 | tf_op jit(solution)/shard_map/ppermute | solution.py:25
  420.9 11.8 %all-to-all-start.14 = ((f32[16,1,32]{2,1,0:T(1,128)}), f32[16,1,32]{2,1,0:T(1,128)S(1)}, u32[]{:S(2)}, u32[]{:S(2)}) async-start(f32[16,1,32]{2,1,0:T(1,128)} %broadcast_in_dim.93), calls=%async_computation.14 | async-start | bytes 16384 | tf_op jit(solution)/shard_map/all_to_all | solution.py:31
  (39 other events, 694.0 us)

commit v6 on v5

--- a/solution.py
+++ b/solution.py
@@ -59,15 +59,13 @@
 
 def panel_slabs(panel_store, owner, nodes):
     n_plate = lax.axis_size("plate")
-    mine = lax.axis_index("plate") == owner
     rows_of = panel_store.reshape(n_plate, nodes, -1)
-    cols_of = jnp.swapaxes(panel_store.reshape(-1, n_plate, nodes), 0, 1)
-    cols_of = jnp.swapaxes(cols_of, 1, 2)
-
-    both = jnp.concatenate([rows_of, cols_of], axis=1)
-    sent = jnp.where(mine, both, 0.0)
-    got = jnp.sum(lax.all_to_all(sent, "plate", 0, 0, tiled=False), axis=0)
-    return got[:nodes], got[nodes:]
+    got_rows = lax.all_to_all(rows_of, "plate", 0, 0, tiled=False)
+    cols_of = panel_store.reshape(-1, n_plate, nodes)
+    got_cols = lax.all_to_all(cols_of, "plate", 1, 1, tiled=False)
+    row_slab = lax.dynamic_index_in_dim(got_rows, owner, 0, keepdims=False)
+    col_slab = lax.dynamic_index_in_dim(got_cols, owner, 1, keepdims=False).T
+    return row_slab, col_slab
 
 
 def on_device(

time: 452 us -> 476 us (1.053)
  waiting for transfers between devices: 63.5 us -> 79.1 us
  starting transfers between devices: 270 us -> 277 us
    all_to_all x1 -> x2, waiting for transfers between devices: 0.01 us -> 12.8 us  [the longest x1 12.8 us: panel_slabs(): got_cols = lax.all_to_all(cols_of, 'plate', 1, 1, tiled=False)]
    all_to_all x1 -> x2, starting transfers between devices: 6.39 us -> 11.7 us  [the longest x1 6.41 us: panel_slabs(): got_rows = lax.all_to_all(rows_of, 'plate', 0, 0, tiled=False)]
  transfers between devices with their start and end apart: 59 -> 60, of which waited for: 25 -> 35; matrix products, arithmetic and copies ran while one was open for 4% -> 5% of each run, Pallas kernels for 0% -> 0%
where the time goes in v6:
time: 476 us; the launch traced here: 473 us
  starting transfers between devices  277 us (58%)
  waiting for transfers between devices  79.1 us (17%)
  other arithmetic  57.1 us (12%)
  local copies, waits for them, and re-layouts  30.2 us (6%)
  matrix products  17.2 us (4%)
  blocking collectives  8.73 us (2%)
    ppermute x44, starting transfers between devices, shifted(): return lax.ppermute(edge, axis, pairs)  168 us
    all_to_all x14, starting transfers between devices, gather_all(): return lax.all_to_all(spread, axis, 0, 0, tiled=False)  97.7 us
    all_to_all x14, waiting for transfers between devices, gather_all(): return lax.all_to_all(spread, axis, 0, 0, tiled=False)  54.3 us
    sub x6, other arithmetic, on_device(): resid = load - (diag * new_disp - stiff * neighbours(new_disp))  17.7 us
    mul x5, other arithmetic, on_device(): resid = target - (diag * adjoint - neighbours(stiff * adjoint))  13.2 us
    all_to_all x1, waiting for transfers between devices, panel_slabs(): got_cols = lax.all_to_all(cols_of, 'plate', 1, 1, tiled=False)  12.8 us
    ppermute x44, waiting for transfers between devices, shifted(): return lax.ppermute(edge, axis, pairs)  12 us
    scatter-add x12, other arithmetic, correct(): return result.reshape(-1).at[places].add(mine).reshape(rows, cols)  10.9 us
  transfers between devices with their start and end apart: 60, of which 35 were waited for; matrix products, arithmetic and copies ran while one was open for 5% of the time, Pallas kernels for 0%

profile of v6, /device:TPU:7, one launch (start us, length us, event | category | flops | bytes accessed | tf_op | source)
XLA Modules:
  0.0 472.9 jit_solution(9747773621489629631)
XLA Ops:
  0.7 6.4 %all-to-all-start = ((f32[16,32,512]{2,1,0:T(8,128)}), f32[16,32,512]{2,1,0:T(8,128)}, u32[]{:S(2)}, u32[]{:S(2)}) async-start(f32[16,32,512]{2,1,0:T(8,128)} %bitcast.168), calls=%async_computation | async-start | bytes 2097152 | tf_op jit(solution)/shard_map/all_to_all | solution.py:63
  7.1 12.0 %collective-permute-start.1 = (f32[1,512]{1,0:T(1,128)S(1)}, f32[1,512]{1,0:T(1,128)S(1)}, u32[]{:S(2)}, u32[]{:S(2)}) collective-permute-start(f32[1,512]{1,0:T(1,128)S(1)} %get-tuple-element.104), channel_id=1, source_target_pairs={{16,0},{32,16},{48,32},{64,48},{80,64},{96,80},{112,96},{128,112},... | collective-permute-start | bytes 6152 | tf_op jit(solution)/shard_map/ppermute | solution.py:25
  31.7 3.9 fusion.3
  39.0 5.8 %all-to-all-start.1 = ((f32[16,1,32]{2,1,0:T(1,128)}), f32[16,1,32]{2,1,0:T(1,128)S(1)}, u32[]{:S(2)}, u32[]{:S(2)}) async-start(f32[16,1,32]{2,1,0:T(1,128)} %broadcast_in_dim.75), calls=%async_computation.1 | async-start | bytes 16384 | tf_op jit(solution)/shard_map/all_to_all | solution.py:31
  51.5 7.6 %collective-permute-start.5 = (f32[1,512]{1,0:T(1,128)S(1)}, f32[1,512]{1,0:T(1,128)S(1)}, u32[]{:S(2)}, u32[]{:S(2)}) collective-permute-start(f32[1,512]{1,0:T(1,128)S(1)} %get-tuple-element.96), channel_id=1, source_target_pairs={{16,0},{32,16},{48,32},{64,48},{80,64},{96,80},{112,96},{128,112},... | collective-permute-start | bytes 6152 | tf_op jit(solution)/shard_map/ppermute | solution.py:25
  72.1 7.3 %all-to-all-start.2 = ((f32[16,1,32]{2,1,0:T(1,128)}), f32[16,1,32]{2,1,0:T(1,128)S(1)}, u32[]{:S(2)}, u32[]{:S(2)}) async-start(f32[16,1,32]{2,1,0:T(1,128)} %broadcast_in_dim.76), calls=%async_computation.2 | async-start | bytes 16384 | tf_op jit(solution)/shard_map/all_to_all | solution.py:31
  85.6 7.6 %collective-permute-start.9 = (f32[1,512]{1,0:T(1,128)S(1)}, f32[1,512]{1,0:T(1,128)S(1)}, u32[]{:S(2)}, u32[]{:S(2)}) collective-permute-start(f32[1,512]{1,0:T(1,128)S(1)} %get-tuple-element.88), channel_id=1, source_target_pairs={{16,0},{32,16},{48,32},{64,48},{80,64},{96,80},{112,96},{128,112},... | collective-permute-start | bytes 6152 | tf_op jit(solution)/shard_map/ppermute | solution.py:25
  106.1 7.3 %all-to-all-start.3 = ((f32[16,1,32]{2,1,0:T(1,128)}), f32[16,1,32]{2,1,0:T(1,128)S(1)}, u32[]{:S(2)}, u32[]{:S(2)}) async-start(f32[16,1,32]{2,1,0:T(1,128)} %broadcast_in_dim.77), calls=%async_computation.3 | async-start | bytes 16384 | tf_op jit(solution)/shard_map/all_to_all | solution.py:31
  119.7 7.6 %collective-permute-start.13 = (f32[1,512]{1,0:T(1,128)S(1)}, f32[1,512]{1,0:T(1,128)S(1)}, u32[]{:S(2)}, u32[]{:S(2)}) collective-permute-start(f32[1,512]{1,0:T(1,128)S(1)} %get-tuple-element.80), channel_id=1, source_target_pairs={{16,0},{32,16},{48,32},{64,48},{80,64},{96,80},{112,96},{128,112},... | collective-permute-start | bytes 6152 | tf_op jit(solution)/shard_map/ppermute | solution.py:25
  140.2 7.3 %all-to-all-start.4 = ((f32[16,1,32]{2,1,0:T(1,128)}), f32[16,1,32]{2,1,0:T(1,128)S(1)}, u32[]{:S(2)}, u32[]{:S(2)}) async-start(f32[16,1,32]{2,1,0:T(1,128)} %broadcast_in_dim.78), calls=%async_computation.4 | async-start | bytes 16384 | tf_op jit(solution)/shard_map/all_to_all | solution.py:31
  153.9 7.6 %collective-permute-start.17 = (f32[1,512]{1,0:T(1,128)S(1)}, f32[1,512]{1,0:T(1,128)S(1)}, u32[]{:S(2)}, u32[]{:S(2)}) collective-permute-start(f32[1,512]{1,0:T(1,128)S(1)} %get-tuple-element.72), channel_id=1, source_target_pairs={{16,0},{32,16},{48,32},{64,48},{80,64},{96,80},{112,96},{128,112},... | collective-permute-start | bytes 6152 | tf_op jit(solution)/shard_map/ppermute | solution.py:25
  174.5 7.3 %all-to-all-start.5 = ((f32[16,1,32]{2,1,0:T(1,128)}), f32[16,1,32]{2,1,0:T(1,128)S(1)}, u32[]{:S(2)}, u32[]{:S(2)}) async-start(f32[16,1,32]{2,1,0:T(1,128)} %broadcast_in_dim.79), calls=%async_computation.5 | async-start | bytes 16384 | tf_op jit(solution)/shard_map/all_to_all | solution.py:31
  188.0 7.6 %collective-permute-start.21 = (f32[1,512]{1,0:T(1,128)S(1)}, f32[1,512]{1,0:T(1,128)S(1)}, u32[]{:S(2)}, u32[]{:S(2)}) collective-permute-start(f32[1,512]{1,0:T(1,128)S(1)} %get-tuple-element.64), channel_id=1, source_target_pairs={{16,0},{32,16},{48,32},{64,48},{80,64},{96,80},{112,96},{128,112},... | collective-permute-start | bytes 6152 | tf_op jit(solution)/shard_map/ppermute | solution.py:25
  208.6 7.3 %all-to-all-start.6 = ((f32[16,1,32]{2,1,0:T(1,128)}), f32[16,1,32]{2,1,0:T(1,128)S(1)}, u32[]{:S(2)}, u32[]{:S(2)}) async-start(f32[16,1,32]{2,1,0:T(1,128)} %broadcast_in_dim.80), calls=%async_computation.6 | async-start | bytes 16384 | tf_op jit(solution)/shard_map/all_to_all | solution.py:31
  222.7 8.7 %all_to_all.100 = f32[16,1,128]{2,1,0:T(1,128)S(1)} all-to-all(f32[16,1,128]{2,1,0:T(1,128)S(1)} %broadcast_in_dim.81), channel_id=1, replica_groups=mesh['storey'=32,'plate'=16] {'plate'}, dimensions={0} | all-to-all | bytes 16384 | tf_op jit(solution)/shard_map/all_to_all | solution.py:31
  232.0 7.4 %all-to-all-start.8 = ((f32[32,1,128]{2,1,0:T(1,128)}), f32[32,1,128]{2,1,0:T(1,128)S(1)}, u32[]{:S(2)}, u32[]{:S(2)}) async-start(f32[32,1,128]{2,1,0:T(1,128)} %broadcast_in_dim.82), calls=%async_computation.8 | async-start | bytes 32768 | tf_op jit(solution)/shard_map/all_to_all | solution.py:31
  239.4 11.1 %all-to-all-done.8 = f32[32,1,128]{2,1,0:T(1,128)S(1)} async-done(((f32[32,1,128]{2,1,0:T(1,128)}), f32[32,1,128]{2,1,0:T(1,128)S(1)}, u32[]{:S(2)}, u32[]{:S(2)}) %all-to-all-start.8) | async-done | bytes 16416 | tf_op jit(solution)/shard_map/all_to_all | solution.py:31
  253.5 5.9 %all-to-all-start.10 = ((f32[16,1,32]{2,1,0:T(1,128)}), f32[16,1,32]{2,1,0:T(1,128)S(1)}, u32[]{:S(2)}, u32[]{:S(2)}) async-start(f32[16,1,32]{2,1,0:T(1,128)} %broadcast_in_dim.83), calls=%async_computation.10 | async-start | bytes 16384 | tf_op jit(solution)/shard_map/all_to_all | solution.py:31
  263.8 5.3 %all-to-all-start.9 = ((f32[512,16,32]{0,2,1:T(8,128)}), f32[512,16,32]{0,2,1:T(8,128)S(1)}, u32[]{:S(2)}, u32[]{:S(2)}) async-start(f32[512,16,32]{0,2,1:T(8,128)} %bitcast.169), calls=%async_computation.9 | async-start | bytes 2097152 | tf_op jit(solution)/shard_map/all_to_all | solution.py:65
  271.0 12.8 %all-to-all-done.9 = f32[512,16,32]{0,2,1:T(8,128)S(1)} async-done(((f32[512,16,32]{0,2,1:T(8,128)}), f32[512,16,32]{0,2,1:T(8,128)S(1)}, u32[]{:S(2)}, u32[]{:S(2)}) %all-to-all-start.9) | async-done | bytes 1048608 | tf_op jit(solution)/shard_map/all_to_all | solution.py:65
  288.4 5.1 %collective-permute-start.25 = (f32[1,512]{1,0:T(1,128)S(1)}, f32[1,512]{1,0:T(1,128)S(1)}, u32[]{:S(2)}, u32[]{:S(2)}) collective-permute-start(f32[1,512]{1,0:T(1,128)S(1)} %get-tuple-element.56), channel_id=1, source_target_pairs={{16,0},{32,16},{48,32},{64,48},{80,64},{96,80},{112,96},{128,112},... | collective-permute-start | bytes 6152 | tf_op jit(solution)/shard_map/ppermute | solution.py:25
  304.2 8.0 %all-to-all-start.11 = ((f32[16,1,32]{2,1,0:T(1,128)}), f32[16,1,32]{2,1,0:T(1,128)S(1)}, u32[]{:S(2)}, u32[]{:S(2)}) async-start(f32[16,1,32]{2,1,0:T(1,128)} %broadcast_in_dim.84), calls=%async_computation.11 | async-start | bytes 16384 | tf_op jit(solution)/shard_map/all_to_all | solution.py:31
  321.9 7.6 %collective-permute-start.29 = (f32[1,512]{1,0:T(1,128)S(1)}, f32[1,512]{1,0:T(1,128)S(1)}, u32[]{:S(2)}, u32[]{:S(2)}) collective-permute-start(f32[1,512]{1,0:T(1,128)S(1)} %get-tuple-element.48), channel_id=1, source_target_pairs={{16,0},{32,16},{48,32},{64,48},{80,64},{96,80},{112,96},{128,112},... | collective-permute-start | bytes 6152 | tf_op jit(solution)/shard_map/ppermute | solution.py:25
  339.9 7.5 %all-to-all-start.12 = ((f32[16,1,32]{2,1,0:T(1,128)}), f32[16,1,32]{2,1,0:T(1,128)S(1)}, u32[]{:S(2)}, u32[]{:S(2)}) async-start(f32[16,1,32]{2,1,0:T(1,128)} %broadcast_in_dim.85), calls=%async_computation.12 | async-start | bytes 16384 | tf_op jit(solution)/shard_map/all_to_all | solution.py:31
  357.1 7.6 %collective-permute-start.33 = (f32[1,512]{1,0:T(1,128)S(1)}, f32[1,512]{1,0:T(1,128)S(1)}, u32[]{:S(2)}, u32[]{:S(2)}) collective-permute-start(f32[1,512]{1,0:T(1,128)S(1)} %get-tuple-element.40), channel_id=1, source_target_pairs={{16,0},{32,16},{48,32},{64,48},{80,64},{96,80},{112,96},{128,112},... | collective-permute-start | bytes 6152 | tf_op jit(solution)/shard_map/ppermute | solution.py:25
  375.1 7.3 %all-to-all-start.13 = ((f32[16,1,32]{2,1,0:T(1,128)}), f32[16,1,32]{2,1,0:T(1,128)S(1)}, u32[]{:S(2)}, u32[]{:S(2)}) async-start(f32[16,1,32]{2,1,0:T(1,128)} %broadcast_in_dim.86), calls=%async_computation.13 | async-start | bytes 16384 | tf_op jit(solution)/shard_map/all_to_all | solution.py:31
  392.1 7.6 %collective-permute-start.37 = (f32[1,512]{1,0:T(1,128)S(1)}, f32[1,512]{1,0:T(1,128)S(1)}, u32[]{:S(2)}, u32[]{:S(2)}) collective-permute-start(f32[1,512]{1,0:T(1,128)S(1)} %get-tuple-element.32), channel_id=1, source_target_pairs={{16,0},{32,16},{48,32},{64,48},{80,64},{96,80},{112,96},{128,112},... | collective-permute-start | bytes 6152 | tf_op jit(solution)/shard_map/ppermute | solution.py:25
  410.1 7.3 %all-to-all-start.14 = ((f32[16,1,32]{2,1,0:T(1,128)}), f32[16,1,32]{2,1,0:T(1,128)S(1)}, u32[]{:S(2)}, u32[]{:S(2)}) async-start(f32[16,1,32]{2,1,0:T(1,128)} %broadcast_in_dim.87), calls=%async_computation.14 | async-start | bytes 16384 | tf_op jit(solution)/shard_map/all_to_all | solution.py:31
  427.1 7.6 %collective-permute-start.41 = (f32[1,512]{1,0:T(1,128)S(1)}, f32[1,512]{1,0:T(1,128)S(1)}, u32[]{:S(2)}, u32[]{:S(2)}) collective-permute-start(f32[1,512]{1,0:T(1,128)S(1)} %get-tuple-element.24), channel_id=1, source_target_pairs={{16,0},{32,16},{48,32},{64,48},{80,64},{96,80},{112,96},{128,112},... | collective-permute-start | bytes 6152 | tf_op jit(solution)/shard_map/ppermute | solution.py:25
  445.1 7.3 %all-to-all-start.15 = ((f32[16,1,32]{2,1,0:T(1,128)}), f32[16,1,32]{2,1,0:T(1,128)S(1)}, u32[]{:S(2)}, u32[]{:S(2)}) async-start(f32[16,1,32]{2,1,0:T(1,128)} %broadcast_in_dim.88), calls=%async_computation.15 | async-start | bytes 16384 | tf_op jit(solution)/shard_map/all_to_all | solution.py:31
  463.0 5.0 %all-to-all-start.16 = ((f32[16,1,64]{2,1,0:T(1,128)}), f32[16,1,64]{2,1,0:T(1,128)S(1)}, u32[]{:S(2)}, u32[]{:S(2)}) async-start(f32[16,1,64]{2,1,0:T(1,128)} %broadcast_in_dim.90), calls=%async_computation.16 | async-start | bytes 16384 | tf_op jit(solution)/shard_map/all_to_all | solution.py:31
  468.6 3.8 all-to-all-done.16
  (332 shorter events, 234.3 us)
Async XLA Ops:
  0.7 35.7 %all-to-all-start = ((f32[16,32,512]{2,1,0:T(8,128)}), f32[16,32,512]{2,1,0:T(8,128)}, u32[]{:S(2)}, u32[]{:S(2)}) async-start(f32[16,32,512]{2,1,0:T(8,128)} %bitcast.168), calls=%async_computation | async-start | bytes 2097152 | tf_op jit(solution)/shard_map/all_to_all | solution.py:63
  7.1 24.5 %collective-permute-start.1 = (f32[1,512]{1,0:T(1,128)S(1)}, f32[1,512]{1,0:T(1,128)S(1)}, u32[]{:S(2)}, u32[]{:S(2)}) collective-permute-start(f32[1,512]{1,0:T(1,128)S(1)} %get-tuple-element.104), channel_id=1, source_target_pairs={{16,0},{32,16},{48,32},{64,48},{80,64},{96,80},{112,96},{128,112},... | collective-permute-start | bytes 6152 | tf_op jit(solution)/shard_map/ppermute | solution.py:25
  19.1 12.6 %collective-permute-start = (f32[1,512]{1,0:T(1,128)S(1)}, f32[1,512]{1,0:T(1,128)S(1)}, u32[]{:S(2)}, u32[]{:S(2)}) collective-permute-start(f32[1,512]{1,0:T(1,128)S(1)} %get-tuple-element.105), channel_id=1, source_target_pairs={{0,16},{16,32},{32,48},{48,64},{64,80},{80,96},{96,112},{112,128},... | collective-permute-start | bytes 6152 | tf_op jit(solution)/shard_map/ppermute | solution.py:25
  21.1 10.5 %collective-permute-start.3 = (f32[128,1]{1,0:T(8,128)S(1)}, f32[128,1]{1,0:T(8,128)S(1)}, u32[]{:S(2)}, u32[]{:S(2)}) collective-permute-start(f32[128,1]{1,0:T(8,128)S(1)} %get-tuple-element.100), channel_id=1, source_target_pairs={{1,0},{2,1},{3,2},{4,3},{5,4},{6,5},{7,6},{8,7},{9,8},{10,9},{11,1... | collective-permute-start | bytes 1544 | tf_op jit(solution)/shard_map/ppermute | solution.py:25
  39.0 10.1 %all-to-all-start.1 = ((f32[16,1,32]{2,1,0:T(1,128)}), f32[16,1,32]{2,1,0:T(1,128)S(1)}, u32[]{:S(2)}, u32[]{:S(2)}) async-start(f32[16,1,32]{2,1,0:T(1,128)} %broadcast_in_dim.75), calls=%async_computation.1 | async-start | bytes 16384 | tf_op jit(solution)/shard_map/all_to_all | solution.py:31
  51.5 16.4 %collective-permute-start.5 = (f32[1,512]{1,0:T(1,128)S(1)}, f32[1,512]{1,0:T(1,128)S(1)}, u32[]{:S(2)}, u32[]{:S(2)}) collective-permute-start(f32[1,512]{1,0:T(1,128)S(1)} %get-tuple-element.96), channel_id=1, source_target_pairs={{16,0},{32,16},{48,32},{64,48},{80,64},{96,80},{112,96},{128,112},... | collective-permute-start | bytes 6152 | tf_op jit(solution)/shard_map/ppermute | solution.py:25
  59.1 8.8 %collective-permute-start.4 = (f32[1,512]{1,0:T(1,128)S(1)}, f32[1,512]{1,0:T(1,128)S(1)}, u32[]{:S(2)}, u32[]{:S(2)}) collective-permute-start(f32[1,512]{1,0:T(1,128)S(1)} %get-tuple-element.97), channel_id=1, source_target_pairs={{0,16},{16,32},{32,48},{48,64},{64,80},{80,96},{96,112},{112,128},... | collective-permute-start | bytes 6152 | tf_op jit(solution)/shard_map/ppermute | solution.py:25
  72.1 11.6 %all-to-all-start.2 = ((f32[16,1,32]{2,1,0:T(1,128)}), f32[16,1,32]{2,1,0:T(1,128)S(1)}, u32[]{:S(2)}, u32[]{:S(2)}) async-start(f32[16,1,32]{2,1,0:T(1,128)} %broadcast_in_dim.76), calls=%async_computation.2 | async-start | bytes 16384 | tf_op jit(solution)/shard_map/all_to_all | solution.py:31
  85.6 16.4 %collective-permute-start.9 = (f32[1,512]{1,0:T(1,128)S(1)}, f32[1,512]{1,0:T(1,128)S(1)}, u32[]{:S(2)}, u32[]{:S(2)}) collective-permute-start(f32[1,512]{1,0:T(1,128)S(1)} %get-tuple-element.88), channel_id=1, source_target_pairs={{16,0},{32,16},{48,32},{64,48},{80,64},{96,80},{112,96},{128,112},... | collective-permute-start | bytes 6152 | tf_op jit(solution)/shard_map/ppermute | solution.py:25
  93.2 8.8 %collective-permute-start.8 = (f32[1,512]{1,0:T(1,128)S(1)}, f32[1,512]{1,0:T(1,128)S(1)}, u32[]{:S(2)}, u32[]{:S(2)}) collective-permute-start(f32[1,512]{1,0:T(1,128)S(1)} %get-tuple-element.89), channel_id=1, source_target_pairs={{0,16},{16,32},{32,48},{48,64},{64,80},{80,96},{96,112},{112,128},... | collective-permute-start | bytes 6152 | tf_op jit(solution)/shard_map/ppermute | solution.py:25
  106.1 11.6 %all-to-all-start.3 = ((f32[16,1,32]{2,1,0:T(1,128)}), f32[16,1,32]{2,1,0:T(1,128)S(1)}, u32[]{:S(2)}, u32[]{:S(2)}) async-start(f32[16,1,32]{2,1,0:T(1,128)} %broadcast_in_dim.77), calls=%async_computation.3 | async-start | bytes 16384 | tf_op jit(solution)/shard_map/all_to_all | solution.py:31
  119.7 16.4 %collective-permute-start.13 = (f32[1,512]{1,0:T(1,128)S(1)}, f32[1,512]{1,0:T(1,128)S(1)}, u32[]{:S(2)}, u32[]{:S(2)}) collective-permute-start(f32[1,512]{1,0:T(1,128)S(1)} %get-tuple-element.80), channel_id=1, source_target_pairs={{16,0},{32,16},{48,32},{64,48},{80,64},{96,80},{112,96},{128,112},... | collective-permute-start | bytes 6152 | tf_op jit(solution)/shard_map/ppermute | solution.py:25
  140.2 11.6 %all-to-all-start.4 = ((f32[16,1,32]{2,1,0:T(1,128)}), f32[16,1,32]{2,1,0:T(1,128)S(1)}, u32[]{:S(2)}, u32[]{:S(2)}) async-start(f32[16,1,32]{2,1,0:T(1,128)} %broadcast_in_dim.78), calls=%async_computation.4 | async-start | bytes 16384 | tf_op jit(solution)/shard_map/all_to_all | solution.py:31
  153.9 16.4 %collective-permute-start.17 = (f32[1,512]{1,0:T(1,128)S(1)}, f32[1,512]{1,0:T(1,128)S(1)}, u32[]{:S(2)}, u32[]{:S(2)}) collective-permute-start(f32[1,512]{1,0:T(1,128)S(1)} %get-tuple-element.72), channel_id=1, source_target_pairs={{16,0},{32,16},{48,32},{64,48},{80,64},{96,80},{112,96},{128,112},... | collective-permute-start | bytes 6152 | tf_op jit(solution)/shard_map/ppermute | solution.py:25
  174.5 11.6 %all-to-all-start.5 = ((f32[16,1,32]{2,1,0:T(1,128)}), f32[16,1,32]{2,1,0:T(1,128)S(1)}, u32[]{:S(2)}, u32[]{:S(2)}) async-start(f32[16,1,32]{2,1,0:T(1,128)} %broadcast_in_dim.79), calls=%async_computation.5 | async-start | bytes 16384 | tf_op jit(solution)/shard_map/all_to_all | solution.py:31
  188.0 16.4 %collective-permute-start.21 = (f32[1,512]{1,0:T(1,128)S(1)}, f32[1,512]{1,0:T(1,128)S(1)}, u32[]{:S(2)}, u32[]{:S(2)}) collective-permute-start(f32[1,512]{1,0:T(1,128)S(1)} %get-tuple-element.64), channel_id=1, source_target_pairs={{16,0},{32,16},{48,32},{64,48},{80,64},{96,80},{112,96},{128,112},... | collective-permute-start | bytes 6152 | tf_op jit(solution)/shard_map/ppermute | solution.py:25
  208.6 11.6 %all-to-all-start.6 = ((f32[16,1,32]{2,1,0:T(1,128)}), f32[16,1,32]{2,1,0:T(1,128)S(1)}, u32[]{:S(2)}, u32[]{:S(2)}) async-start(f32[16,1,32]{2,1,0:T(1,128)} %broadcast_in_dim.80), calls=%async_computation.6 | async-start | bytes 16384 | tf_op jit(solution)/shard_map/all_to_all | solution.py:31
  232.0 18.5 %all-to-all-start.8 = ((f32[32,1,128]{2,1,0:T(1,128)}), f32[32,1,128]{2,1,0:T(1,128)S(1)}, u32[]{:S(2)}, u32[]{:S(2)}) async-start(f32[32,1,128]{2,1,0:T(1,128)} %broadcast_in_dim.82), calls=%async_computation.8 | async-start | bytes 32768 | tf_op jit(solution)/shard_map/all_to_all | solution.py:31
  253.5 10.2 %all-to-all-start.10 = ((f32[16,1,32]{2,1,0:T(1,128)}), f32[16,1,32]{2,1,0:T(1,128)S(1)}, u32[]{:S(2)}, u32[]{:S(2)}) async-start(f32[16,1,32]{2,1,0:T(1,128)} %broadcast_in_dim.83), calls=%async_computation.10 | async-start | bytes 16384 | tf_op jit(solution)/shard_map/all_to_all | solution.py:31
  263.8 20.0 %all-to-all-start.9 = ((f32[512,16,32]{0,2,1:T(8,128)}), f32[512,16,32]{0,2,1:T(8,128)S(1)}, u32[]{:S(2)}, u32[]{:S(2)}) async-start(f32[512,16,32]{0,2,1:T(8,128)} %bitcast.169), calls=%async_computation.9 | async-start | bytes 2097152 | tf_op jit(solution)/shard_map/all_to_all | solution.py:65
  288.4 14.2 %collective-permute-start.25 = (f32[1,512]{1,0:T(1,128)S(1)}, f32[1,512]{1,0:T(1,128)S(1)}, u32[]{:S(2)}, u32[]{:S(2)}) collective-permute-start(f32[1,512]{1,0:T(1,128)S(1)} %get-tuple-element.56), channel_id=1, source_target_pairs={{16,0},{32,16},{48,32},{64,48},{80,64},{96,80},{112,96},{128,112},... | collective-permute-start | bytes 6152 | tf_op jit(solution)/shard_map/ppermute | solution.py:25
  293.6 9.0 %collective-permute-start.24 = (f32[1,512]{1,0:T(1,128)S(1)}, f32[1,512]{1,0:T(1,128)S(1)}, u32[]{:S(2)}, u32[]{:S(2)}) collective-permute-start(f32[1,512]{1,0:T(1,128)S(1)} %get-tuple-element.57), channel_id=1, source_target_pairs={{0,16},{16,32},{32,48},{48,64},{64,80},{80,96},{96,112},{112,128},... | collective-permute-start | bytes 6152 | tf_op jit(solution)/shard_map/ppermute | solution.py:25
  304.2 12.3 %all-to-all-start.11 = ((f32[16,1,32]{2,1,0:T(1,128)}), f32[16,1,32]{2,1,0:T(1,128)S(1)}, u32[]{:S(2)}, u32[]{:S(2)}) async-start(f32[16,1,32]{2,1,0:T(1,128)} %broadcast_in_dim.84), calls=%async_computation.11 | async-start | bytes 16384 | tf_op jit(solution)/shard_map/all_to_all | solution.py:31
  321.9 16.4 %collective-permute-start.29 = (f32[1,512]{1,0:T(1,128)S(1)}, f32[1,512]{1,0:T(1,128)S(1)}, u32[]{:S(2)}, u32[]{:S(2)}) collective-permute-start(f32[1,512]{1,0:T(1,128)S(1)} %get-tuple-element.48), channel_id=1, source_target_pairs={{16,0},{32,16},{48,32},{64,48},{80,64},{96,80},{112,96},{128,112},... | collective-permute-start | bytes 6152 | tf_op jit(solution)/shard_map/ppermute | solution.py:25
  339.9 11.8 %all-to-all-start.12 = ((f32[16,1,32]{2,1,0:T(1,128)}), f32[16,1,32]{2,1,0:T(1,128)S(1)}, u32[]{:S(2)}, u32[]{:S(2)}) async-start(f32[16,1,32]{2,1,0:T(1,128)} %broadcast_in_dim.85), calls=%async_computation.12 | async-start | bytes 16384 | tf_op jit(solution)/shard_map/all_to_all | solution.py:31
  357.1 16.4 %collective-permute-start.33 = (f32[1,512]{1,0:T(1,128)S(1)}, f32[1,512]{1,0:T(1,128)S(1)}, u32[]{:S(2)}, u32[]{:S(2)}) collective-permute-start(f32[1,512]{1,0:T(1,128)S(1)} %get-tuple-element.40), channel_id=1, source_target_pairs={{16,0},{32,16},{48,32},{64,48},{80,64},{96,80},{112,96},{128,112},... | collective-permute-start | bytes 6152 | tf_op jit(solution)/shard_map/ppermute | solution.py:25
  375.1 11.6 %all-to-all-start.13 = ((f32[16,1,32]{2,1,0:T(1,128)}), f32[16,1,32]{2,1,0:T(1,128)S(1)}, u32[]{:S(2)}, u32[]{:S(2)}) async-start(f32[16,1,32]{2,1,0:T(1,128)} %broadcast_in_dim.86), calls=%async_computation.13 | async-start | bytes 16384 | tf_op jit(solution)/shard_map/all_to_all | solution.py:31
  392.1 16.4 %collective-permute-start.37 = (f32[1,512]{1,0:T(1,128)S(1)}, f32[1,512]{1,0:T(1,128)S(1)}, u32[]{:S(2)}, u32[]{:S(2)}) collective-permute-start(f32[1,512]{1,0:T(1,128)S(1)} %get-tuple-element.32), channel_id=1, source_target_pairs={{16,0},{32,16},{48,32},{64,48},{80,64},{96,80},{112,96},{128,112},... | collective-permute-start | bytes 6152 | tf_op jit(solution)/shard_map/ppermute | solution.py:25
  410.1 11.6 %all-to-all-start.14 = ((f32[16,1,32]{2,1,0:T(1,128)}), f32[16,1,32]{2,1,0:T(1,128)S(1)}, u32[]{:S(2)}, u32[]{:S(2)}) async-start(f32[16,1,32]{2,1,0:T(1,128)} %broadcast_in_dim.87), calls=%async_computation.14 | async-start | bytes 16384 | tf_op jit(solution)/shard_map/all_to_all | solution.py:31
  427.1 16.4 %collective-permute-start.41 = (f32[1,512]{1,0:T(1,128)S(1)}, f32[1,512]{1,0:T(1,128)S(1)}, u32[]{:S(2)}, u32[]{:S(2)}) collective-permute-start(f32[1,512]{1,0:T(1,128)S(1)} %get-tuple-element.24), channel_id=1, source_target_pairs={{16,0},{32,16},{48,32},{64,48},{80,64},{96,80},{112,96},{128,112},... | collective-permute-start | bytes 6152 | tf_op jit(solution)/shard_map/ppermute | solution.py:25
  445.1 11.6 %all-to-all-start.15 = ((f32[16,1,32]{2,1,0:T(1,128)}), f32[16,1,32]{2,1,0:T(1,128)S(1)}, u32[]{:S(2)}, u32[]{:S(2)}) async-start(f32[16,1,32]{2,1,0:T(1,128)} %broadcast_in_dim.88), calls=%async_computation.15 | async-start | bytes 16384 | tf_op jit(solution)/shard_map/all_to_all | solution.py:31
  463.0 9.4 %all-to-all-start.16 = ((f32[16,1,64]{2,1,0:T(1,128)}), f32[16,1,64]{2,1,0:T(1,128)S(1)}, u32[]{:S(2)}, u32[]{:S(2)}) async-start(f32[16,1,64]{2,1,0:T(1,128)} %broadcast_in_dim.90), calls=%async_computation.16 | async-start | bytes 16384 | tf_op jit(solution)/shard_map/all_to_all | solution.py:31
  (40 other events, 295.6 us)

commit v7 on v5

--- a/solution.py
+++ b/solution.py
@@ -128,12 +128,13 @@
     shear = lax.dynamic_slice_in_dim(every_shear, here_storey * rows, rows)
     drift = lax.dynamic_slice_in_dim(every_drift, here_storey * rows, rows)
     target = inertia * drift[:, None]
-    adjoint = jnp.zeros_like(load)
-    resid = target
-    for step in range(ITERS):
-        adjoint = adjoint + correct(resid, True)
-        if step < ITERS - 1:
-            resid = target - (diag * adjoint - neighbours(stiff * adjoint))
+    adjoint = jnp.zeros_like(load) + correct(target, True)
+
+    def adjoint_step(_, adjoint):
+        resid = target - (diag * adjoint - neighbours(stiff * adjoint))
+        return adjoint + correct(resid, True)
+
+    adjoint = lax.fori_loop(0, ITERS - 1, adjoint_step, adjoint)
     partial_sums = damper_totals(damper_map, adjoint * new_disp, damper_coef.shape[0])
     sums = sum_all(partial_sums, "plate")
     grads = -CD * 64.0 / math.sqrt(rows * total_cols / damper_coef.shape[0]) * sums

time: 452 us -> 433 us (0.958)
  other arithmetic: 60.3 us -> 40.9 us
    mul x5, other arithmetic: 12.6 us -> 0.19 us  [adjoint_step(): resid = target - (diag * adjoint - neighbours(stiff * adjoint))]
    sub x6, other arithmetic: 15.9 us -> 3.88 us  [on_device(): resid = load - (diag * new_disp - stiff * neighbours(new_disp))]
  transfers between devices with their start and end apart: 59 -> 59, of which waited for: 25 -> 25; matrix products, arithmetic and copies ran while one was open for 4% -> 5% of each run, Pallas kernels for 0% -> 0%
where the time goes in v7:
time: 433 us; the launch traced here: 430 us
  starting transfers between devices  270 us (62%)
  waiting for transfers between devices  62.6 us (14%)
  other arithmetic  40.9 us (9%)
  local copies, waits for them, and re-layouts  30.8 us (7%)
  matrix products  12.9 us (3%)
  blocking collectives  8.59 us (2%)
    ppermute x44, starting transfers between devices, shifted(): return lax.ppermute(edge, axis, pairs)  164 us
    all_to_all x14, starting transfers between devices, gather_all(): return lax.all_to_all(spread, axis, 0, 0, tiled=False)  99.1 us
    all_to_all x14, waiting for transfers between devices, gather_all(): return lax.all_to_all(spread, axis, 0, 0, tiled=False)  53.7 us
    scatter-add x12, other arithmetic, correct(): return result.reshape(-1).at[places].add(mine).reshape(rows, cols)  11 us
    ppermute x44, waiting for transfers between devices, shifted(): return lax.ppermute(edge, axis, pairs)  8.93 us
  transfers between devices with their start and end apart: 59, of which 25 were waited for; matrix products, arithmetic and copies ran while one was open for 5% of the time, Pallas kernels for 0%

profile of v7, /device:TPU:7, one launch (start us, length us, event | category | flops | bytes accessed | tf_op | source)
XLA Modules:
  0.0 429.7 jit_solution(2005962973561522231)
XLA Ops:
  4.6 6.4 %all-to-all-start.1 = ((f32[16,64,512]{2,1,0:T(8,128)}), f32[16,64,512]{2,1,0:T(8,128)}, u32[]{:S(2)}, u32[]{:S(2)}) async-start(f32[16,64,512]{2,1,0:T(8,128)} %maximum_select_fusion), calls=%async_computation.1 | async-start | bytes 4194304 | tf_op jit(solution)/shard_map/all_to_all | solution.py:69
  16.6 3.5 collective-permute-start.4
  20.1 10.3 %collective-permute-start.5 = (f32[1,512]{1,0:T(1,128)S(1)}, f32[1,512]{1,0:T(1,128)S(1)}, u32[]{:S(2)}, u32[]{:S(2)}) collective-permute-start(f32[1,512]{1,0:T(1,128)S(1)} %get-tuple-element.122), channel_id=1, source_target_pairs={{16,0},{32,16},{48,32},{64,48},{80,64},{96,80},{112,96},{128,112},... | collective-permute-start | bytes 6152 | tf_op jit(solution)/shard_map/ppermute | solution.py:25
  43.7 5.7 %all-to-all-start.2 = ((f32[16,1,32]{2,1,0:T(1,128)}), f32[16,1,32]{2,1,0:T(1,128)S(1)}, u32[]{:S(2)}, u32[]{:S(2)}) async-start(f32[16,1,32]{2,1,0:T(1,128)} %broadcast_in_dim.72), calls=%async_computation.2 | async-start | bytes 16384 | tf_op jit(solution)/shard_map/all_to_all | solution.py:31
  61.1 3.5 collective-permute-start.8
  64.7 10.3 %collective-permute-start.9 = (f32[1,512]{1,0:T(1,128)S(1)}, f32[1,512]{1,0:T(1,128)S(1)}, u32[]{:S(2)}, u32[]{:S(2)}) collective-permute-start(f32[1,512]{1,0:T(1,128)S(1)} %get-tuple-element.114), channel_id=1, source_target_pairs={{16,0},{32,16},{48,32},{64,48},{80,64},{96,80},{112,96},{128,112},... | collective-permute-start | bytes 6152 | tf_op jit(solution)/shard_map/ppermute | solution.py:25
  77.3 7.5 %all-to-all-start.3 = ((f32[16,1,32]{2,1,0:T(1,128)}), f32[16,1,32]{2,1,0:T(1,128)S(1)}, u32[]{:S(2)}, u32[]{:S(2)}) async-start(f32[16,1,32]{2,1,0:T(1,128)} %broadcast_in_dim.73), calls=%async_computation.3 | async-start | bytes 16384 | tf_op jit(solution)/shard_map/all_to_all | solution.py:31
  85.6 3.5 all-to-all-done.3
  97.9 7.5 %collective-permute-start.13 = (f32[1,512]{1,0:T(1,128)S(1)}, f32[1,512]{1,0:T(1,128)S(1)}, u32[]{:S(2)}, u32[]{:S(2)}) collective-permute-start(f32[1,512]{1,0:T(1,128)S(1)} %get-tuple-element.106), channel_id=1, source_target_pairs={{16,0},{32,16},{48,32},{64,48},{80,64},{96,80},{112,96},{128,112},... | collective-permute-start | bytes 6152 | tf_op jit(solution)/shard_map/ppermute | solution.py:25
  107.7 7.5 %all-to-all-start.4 = ((f32[16,1,32]{2,1,0:T(1,128)}), f32[16,1,32]{2,1,0:T(1,128)S(1)}, u32[]{:S(2)}, u32[]{:S(2)}) async-start(f32[16,1,32]{2,1,0:T(1,128)} %broadcast_in_dim.80), calls=%async_computation.4 | async-start | bytes 16384 | tf_op jit(solution)/shard_map/all_to_all | solution.py:31
  128.3 7.5 %collective-permute-start.17 = (f32[1,512]{1,0:T(1,128)S(1)}, f32[1,512]{1,0:T(1,128)S(1)}, u32[]{:S(2)}, u32[]{:S(2)}) collective-permute-start(f32[1,512]{1,0:T(1,128)S(1)} %get-tuple-element.98), channel_id=1, source_target_pairs={{16,0},{32,16},{48,32},{64,48},{80,64},{96,80},{112,96},{128,112},... | collective-permute-start | bytes 6152 | tf_op jit(solution)/shard_map/ppermute | solution.py:25
  138.1 7.5 %all-to-all-start.5 = ((f32[16,1,32]{2,1,0:T(1,128)}), f32[16,1,32]{2,1,0:T(1,128)S(1)}, u32[]{:S(2)}, u32[]{:S(2)}) async-start(f32[16,1,32]{2,1,0:T(1,128)} %broadcast_in_dim.81), calls=%async_computation.5 | async-start | bytes 16384 | tf_op jit(solution)/shard_map/all_to_all | solution.py:31
  158.7 7.5 %collective-permute-start.21 = (f32[1,512]{1,0:T(1,128)S(1)}, f32[1,512]{1,0:T(1,128)S(1)}, u32[]{:S(2)}, u32[]{:S(2)}) collective-permute-start(f32[1,512]{1,0:T(1,128)S(1)} %get-tuple-element.90), channel_id=1, source_target_pairs={{16,0},{32,16},{48,32},{64,48},{80,64},{96,80},{112,96},{128,112},... | collective-permute-start | bytes 6152 | tf_op jit(solution)/shard_map/ppermute | solution.py:25
  168.5 7.5 %all-to-all-start.6 = ((f32[16,1,32]{2,1,0:T(1,128)}), f32[16,1,32]{2,1,0:T(1,128)S(1)}, u32[]{:S(2)}, u32[]{:S(2)}) async-start(f32[16,1,32]{2,1,0:T(1,128)} %broadcast_in_dim.82), calls=%async_computation.6 | async-start | bytes 16384 | tf_op jit(solution)/shard_map/all_to_all | solution.py:31
  189.1 7.5 %collective-permute-start.25 = (f32[1,512]{1,0:T(1,128)S(1)}, f32[1,512]{1,0:T(1,128)S(1)}, u32[]{:S(2)}, u32[]{:S(2)}) collective-permute-start(f32[1,512]{1,0:T(1,128)S(1)} %get-tuple-element.82), channel_id=1, source_target_pairs={{16,0},{32,16},{48,32},{64,48},{80,64},{96,80},{112,96},{128,112},... | collective-permute-start | bytes 6152 | tf_op jit(solution)/shard_map/ppermute | solution.py:25
  198.9 7.5 %all-to-all-start.7 = ((f32[16,1,32]{2,1,0:T(1,128)}), f32[16,1,32]{2,1,0:T(1,128)S(1)}, u32[]{:S(2)}, u32[]{:S(2)}) async-start(f32[16,1,32]{2,1,0:T(1,128)} %broadcast_in_dim.83), calls=%async_computation.7 | async-start | bytes 16384 | tf_op jit(solution)/shard_map/all_to_all | solution.py:31
  213.3 8.6 %all_to_all.72 = f32[16,1,128]{2,1,0:T(1,128)S(1)} all-to-all(f32[16,1,128]{2,1,0:T(1,128)S(1)} %broadcast_in_dim.84), channel_id=1, replica_groups=mesh['storey'=32,'plate'=16] {'plate'}, dimensions={0} | all-to-all | bytes 16384 | tf_op jit(solution)/shard_map/all_to_all | solution.py:31
  222.6 7.3 %all-to-all-start.9 = ((f32[32,1,128]{2,1,0:T(1,128)}), f32[32,1,128]{2,1,0:T(1,128)S(1)}, u32[]{:S(2)}, u32[]{:S(2)}) async-start(f32[32,1,128]{2,1,0:T(1,128)} %broadcast_in_dim.85), calls=%async_computation.9 | async-start | bytes 32768 | tf_op jit(solution)/shard_map/all_to_all | solution.py:31
  229.9 11.1 %all-to-all-done.9 = f32[32,1,128]{2,1,0:T(1,128)S(1)} async-done(((f32[32,1,128]{2,1,0:T(1,128)}), f32[32,1,128]{2,1,0:T(1,128)S(1)}, u32[]{:S(2)}, u32[]{:S(2)}) %all-to-all-start.9) | async-done | bytes 16416 | tf_op jit(solution)/shard_map/all_to_all | solution.py:31
  244.4 5.9 %all-to-all-start.10 = ((f32[16,1,32]{2,1,0:T(1,128)}), f32[16,1,32]{2,1,0:T(1,128)S(1)}, u32[]{:S(2)}, u32[]{:S(2)}) async-start(f32[16,1,32]{2,1,0:T(1,128)} %broadcast_in_dim.86), calls=%async_computation.10 | async-start | bytes 16384 | tf_op jit(solution)/shard_map/all_to_all | solution.py:31
  256.7 158.1 %while.10 = (s32[]{:T(128)}, f32[128,512]{1,0:T(8,128)S(1)}, f32[128,512]{1,0:T(8,128)S(1)}, f32[128,512]{1,0:T(8,128)S(1)}, f32[128,512]{1,0:T(8,128)S(1)}, /*i...) while((s32[]{:T(128)}, f32[128,512]{1,0:T(8,128)S(1)}, ...), condition=%wide.region_17.18_spmd, body=%wide.region_15.17_spmd.sunk | while | flops 403702912 | bytes 9298261 | solution.py:137
  263.6 6.8 %collective-permute-start.1 = (f32[1,512]{1,0:T(1,128)S(1)}, f32[1,512]{1,0:T(1,128)S(1)}, u32[]{:S(2)}, u32[]{:S(2)}) collective-permute-start(f32[1,512]{1,0:T(1,128)S(1)} %get-tuple-element.187), channel_id=1, source_target_pairs={{16,0},{32,16},{48,32},{64,48},{80,64},{96,80},{112,96},{128,112},... | collective-permute-start | bytes 6152 | tf_op jit(solution)/shard_map/while/body/eval_jaxpr/ppermute | solution.py:25
  273.6 7.8 %all-to-all-start = ((f32[16,1,32]{2,1,0:T(1,128)}), f32[16,1,32]{2,1,0:T(1,128)S(1)}, u32[]{:S(2)}, u32[]{:S(2)}) async-start(f32[16,1,32]{2,1,0:T(1,128)} %broadcast_in_dim.195), calls=%async_computation | async-start | bytes 16384 | tf_op jit(solution)/shard_map/while/body/eval_jaxpr/all_to_all | solution.py:31
  294.9 7.5 %collective-permute-start.1 = (f32[1,512]{1,0:T(1,128)S(1)}, f32[1,512]{1,0:T(1,128)S(1)}, u32[]{:S(2)}, u32[]{:S(2)}) collective-permute-start(f32[1,512]{1,0:T(1,128)S(1)} %get-tuple-element.187), channel_id=1, source_target_pairs={{16,0},{32,16},{48,32},{64,48},{80,64},{96,80},{112,96},{128,112},... | collective-permute-start | bytes 6152 | tf_op jit(solution)/shard_map/while/body/eval_jaxpr/ppermute | solution.py:25
  305.5 7.5 %all-to-all-start = ((f32[16,1,32]{2,1,0:T(1,128)}), f32[16,1,32]{2,1,0:T(1,128)S(1)}, u32[]{:S(2)}, u32[]{:S(2)}) async-start(f32[16,1,32]{2,1,0:T(1,128)} %broadcast_in_dim.195), calls=%async_computation | async-start | bytes 16384 | tf_op jit(solution)/shard_map/while/body/eval_jaxpr/all_to_all | solution.py:31
  326.5 7.5 %collective-permute-start.1 = (f32[1,512]{1,0:T(1,128)S(1)}, f32[1,512]{1,0:T(1,128)S(1)}, u32[]{:S(2)}, u32[]{:S(2)}) collective-permute-start(f32[1,512]{1,0:T(1,128)S(1)} %get-tuple-element.187), channel_id=1, source_target_pairs={{16,0},{32,16},{48,32},{64,48},{80,64},{96,80},{112,96},{128,112},... | collective-permute-start | bytes 6152 | tf_op jit(solution)/shard_map/while/body/eval_jaxpr/ppermute | solution.py:25
  337.2 7.5 %all-to-all-start = ((f32[16,1,32]{2,1,0:T(1,128)}), f32[16,1,32]{2,1,0:T(1,128)S(1)}, u32[]{:S(2)}, u32[]{:S(2)}) async-start(f32[16,1,32]{2,1,0:T(1,128)} %broadcast_in_dim.195), calls=%async_computation | async-start | bytes 16384 | tf_op jit(solution)/shard_map/while/body/eval_jaxpr/all_to_all | solution.py:31
  358.2 7.5 %collective-permute-start.1 = (f32[1,512]{1,0:T(1,128)S(1)}, f32[1,512]{1,0:T(1,128)S(1)}, u32[]{:S(2)}, u32[]{:S(2)}) collective-permute-start(f32[1,512]{1,0:T(1,128)S(1)} %get-tuple-element.187), channel_id=1, source_target_pairs={{16,0},{32,16},{48,32},{64,48},{80,64},{96,80},{112,96},{128,112},... | collective-permute-start | bytes 6152 | tf_op jit(solution)/shard_map/while/body/eval_jaxpr/ppermute | solution.py:25
  368.9 7.5 %all-to-all-start = ((f32[16,1,32]{2,1,0:T(1,128)}), f32[16,1,32]{2,1,0:T(1,128)S(1)}, u32[]{:S(2)}, u32[]{:S(2)}) async-start(f32[16,1,32]{2,1,0:T(1,128)} %broadcast_in_dim.195), calls=%async_computation | async-start | bytes 16384 | tf_op jit(solution)/shard_map/while/body/eval_jaxpr/all_to_all | solution.py:31
  389.9 7.5 %collective-permute-start.1 = (f32[1,512]{1,0:T(1,128)S(1)}, f32[1,512]{1,0:T(1,128)S(1)}, u32[]{:S(2)}, u32[]{:S(2)}) collective-permute-start(f32[1,512]{1,0:T(1,128)S(1)} %get-tuple-element.187), channel_id=1, source_target_pairs={{16,0},{32,16},{48,32},{64,48},{80,64},{96,80},{112,96},{128,112},... | collective-permute-start | bytes 6152 | tf_op jit(solution)/shard_map/while/body/eval_jaxpr/ppermute | solution.py:25
  400.5 7.5 %all-to-all-start = ((f32[16,1,32]{2,1,0:T(1,128)}), f32[16,1,32]{2,1,0:T(1,128)S(1)}, u32[]{:S(2)}, u32[]{:S(2)}) async-start(f32[16,1,32]{2,1,0:T(1,128)} %broadcast_in_dim.195), calls=%async_computation | async-start | bytes 16384 | tf_op jit(solution)/shard_map/while/body/eval_jaxpr/all_to_all | solution.py:31
  419.6 5.1 %all-to-all-start.11 = ((f32[16,1,64]{2,1,0:T(1,128)}), f32[16,1,64]{2,1,0:T(1,128)S(1)}, u32[]{:S(2)}, u32[]{:S(2)}) async-start(f32[16,1,64]{2,1,0:T(1,128)} %broadcast_in_dim.92), calls=%async_computation.11 | async-start | bytes 16384 | tf_op jit(solution)/shard_map/all_to_all | solution.py:31
  (364 shorter events, 202.1 us)
Async XLA Ops:
  4.6 35.5 %all-to-all-start.1 = ((f32[16,64,512]{2,1,0:T(8,128)}), f32[16,64,512]{2,1,0:T(8,128)}, u32[]{:S(2)}, u32[]{:S(2)}) async-start(f32[16,64,512]{2,1,0:T(8,128)} %maximum_select_fusion), calls=%async_computation.1 | async-start | bytes 4194304 | tf_op jit(solution)/shard_map/all_to_all | solution.py:69
  11.2 25.3 %collective-permute-start.6 = (f32[128,1]{1,0:T(8,128)S(1)}, f32[128,1]{1,0:T(8,128)S(1)}, u32[]{:S(2)}, u32[]{:S(2)}) collective-permute-start(f32[128,1]{1,0:T(8,128)S(1)} %get-tuple-element.119), channel_id=1, source_target_pairs={{0,1},{1,2},{2,3},{3,4},{4,5},{5,6},{6,7},{7,8},{8,9},{9,10},{10,1... | collective-permute-start | bytes 1544 | tf_op jit(solution)/shard_map/ppermute | solution.py:25
  14.6 21.8 %collective-permute-start.7 = (f32[128,1]{1,0:T(8,128)S(1)}, f32[128,1]{1,0:T(8,128)S(1)}, u32[]{:S(2)}, u32[]{:S(2)}) collective-permute-start(f32[128,1]{1,0:T(8,128)S(1)} %get-tuple-element.118), channel_id=1, source_target_pairs={{1,0},{2,1},{3,2},{4,3},{5,4},{6,5},{7,6},{8,7},{9,8},{10,9},{11,1... | collective-permute-start | bytes 1544 | tf_op jit(solution)/shard_map/ppermute | solution.py:25
  16.6 19.9 %collective-permute-start.4 = (f32[1,512]{1,0:T(1,128)S(1)}, f32[1,512]{1,0:T(1,128)S(1)}, u32[]{:S(2)}, u32[]{:S(2)}) collective-permute-start(f32[1,512]{1,0:T(1,128)S(1)} %get-tuple-element.123), channel_id=1, source_target_pairs={{0,16},{16,32},{32,48},{48,64},{64,80},{80,96},{96,112},{112,128},... | collective-permute-start | bytes 6152 | tf_op jit(solution)/shard_map/ppermute | solution.py:25
  20.1 16.3 %collective-permute-start.5 = (f32[1,512]{1,0:T(1,128)S(1)}, f32[1,512]{1,0:T(1,128)S(1)}, u32[]{:S(2)}, u32[]{:S(2)}) collective-permute-start(f32[1,512]{1,0:T(1,128)S(1)} %get-tuple-element.122), channel_id=1, source_target_pairs={{16,0},{32,16},{48,32},{64,48},{80,64},{96,80},{112,96},{128,112},... | collective-permute-start | bytes 6152 | tf_op jit(solution)/shard_map/ppermute | solution.py:25
  56.4 18.6 %collective-permute-start.10 = (f32[128,1]{1,0:T(8,128)S(1)}, f32[128,1]{1,0:T(8,128)S(1)}, u32[]{:S(2)}, u32[]{:S(2)}) collective-permute-start(f32[128,1]{1,0:T(8,128)S(1)} %get-tuple-element.111), channel_id=1, source_target_pairs={{0,1},{1,2},{2,3},{3,4},{4,5},{5,6},{6,7},{7,8},{8,9},{9,10},{10,1... | collective-permute-start | bytes 1544 | tf_op jit(solution)/shard_map/ppermute | solution.py:25
  59.2 15.9 %collective-permute-start.11 = (f32[128,1]{1,0:T(8,128)S(1)}, f32[128,1]{1,0:T(8,128)S(1)}, u32[]{:S(2)}, u32[]{:S(2)}) collective-permute-start(f32[128,1]{1,0:T(8,128)S(1)} %get-tuple-element.110), channel_id=1, source_target_pairs={{1,0},{2,1},{3,2},{4,3},{5,4},{6,5},{7,6},{8,7},{9,8},{10,9},{11,1... | collective-permute-start | bytes 1544 | tf_op jit(solution)/shard_map/ppermute | solution.py:25
  61.1 14.0 %collective-permute-start.8 = (f32[1,512]{1,0:T(1,128)S(1)}, f32[1,512]{1,0:T(1,128)S(1)}, u32[]{:S(2)}, u32[]{:S(2)}) collective-permute-start(f32[1,512]{1,0:T(1,128)S(1)} %get-tuple-element.115), channel_id=1, source_target_pairs={{0,16},{16,32},{32,48},{48,64},{64,80},{80,96},{96,112},{112,128},... | collective-permute-start | bytes 6152 | tf_op jit(solution)/shard_map/ppermute | solution.py:25
  77.3 11.8 %all-to-all-start.3 = ((f32[16,1,32]{2,1,0:T(1,128)}), f32[16,1,32]{2,1,0:T(1,128)S(1)}, u32[]{:S(2)}, u32[]{:S(2)}) async-start(f32[16,1,32]{2,1,0:T(1,128)} %broadcast_in_dim.73), calls=%async_computation.3 | async-start | bytes 16384 | tf_op jit(solution)/shard_map/all_to_all | solution.py:31
  91.3 14.2 %collective-permute-start.14 = (f32[128,1]{1,0:T(8,128)S(1)}, f32[128,1]{1,0:T(8,128)S(1)}, u32[]{:S(2)}, u32[]{:S(2)}) collective-permute-start(f32[128,1]{1,0:T(8,128)S(1)} %get-tuple-element.103), channel_id=1, source_target_pairs={{0,1},{1,2},{2,3},{3,4},{4,5},{5,6},{6,7},{7,8},{8,9},{9,10},{10,1... | collective-permute-start | bytes 1544 | tf_op jit(solution)/shard_map/ppermute | solution.py:25
  107.7 11.8 %all-to-all-start.4 = ((f32[16,1,32]{2,1,0:T(1,128)}), f32[16,1,32]{2,1,0:T(1,128)S(1)}, u32[]{:S(2)}, u32[]{:S(2)}) async-start(f32[16,1,32]{2,1,0:T(1,128)} %broadcast_in_dim.80), calls=%async_computation.4 | async-start | bytes 16384 | tf_op jit(solution)/shard_map/all_to_all | solution.py:31
  121.7 14.2 %collective-permute-start.18 = (f32[128,1]{1,0:T(8,128)S(1)}, f32[128,1]{1,0:T(8,128)S(1)}, u32[]{:S(2)}, u32[]{:S(2)}) collective-permute-start(f32[128,1]{1,0:T(8,128)S(1)} %get-tuple-element.95), channel_id=1, source_target_pairs={{0,1},{1,2},{2,3},{3,4},{4,5},{5,6},{6,7},{7,8},{8,9},{9,10},{10,1... | collective-permute-start | bytes 1544 | tf_op jit(solution)/shard_map/ppermute | solution.py:25
  138.1 11.8 %all-to-all-start.5 = ((f32[16,1,32]{2,1,0:T(1,128)}), f32[16,1,32]{2,1,0:T(1,128)S(1)}, u32[]{:S(2)}, u32[]{:S(2)}) async-start(f32[16,1,32]{2,1,0:T(1,128)} %broadcast_in_dim.81), calls=%async_computation.5 | async-start | bytes 16384 | tf_op jit(solution)/shard_map/all_to_all | solution.py:31
  152.1 14.2 %collective-permute-start.22 = (f32[128,1]{1,0:T(8,128)S(1)}, f32[128,1]{1,0:T(8,128)S(1)}, u32[]{:S(2)}, u32[]{:S(2)}) collective-permute-start(f32[128,1]{1,0:T(8,128)S(1)} %get-tuple-element.87), channel_id=1, source_target_pairs={{0,1},{1,2},{2,3},{3,4},{4,5},{5,6},{6,7},{7,8},{8,9},{9,10},{10,1... | collective-permute-start | bytes 1544 | tf_op jit(solution)/shard_map/ppermute | solution.py:25
  168.5 11.8 %all-to-all-start.6 = ((f32[16,1,32]{2,1,0:T(1,128)}), f32[16,1,32]{2,1,0:T(1,128)S(1)}, u32[]{:S(2)}, u32[]{:S(2)}) async-start(f32[16,1,32]{2,1,0:T(1,128)} %broadcast_in_dim.82), calls=%async_computation.6 | async-start | bytes 16384 | tf_op jit(solution)/shard_map/all_to_all | solution.py:31
  182.5 14.2 %collective-permute-start.26 = (f32[128,1]{1,0:T(8,128)S(1)}, f32[128,1]{1,0:T(8,128)S(1)}, u32[]{:S(2)}, u32[]{:S(2)}) collective-permute-start(f32[128,1]{1,0:T(8,128)S(1)} %get-tuple-element.79), channel_id=1, source_target_pairs={{0,1},{1,2},{2,3},{3,4},{4,5},{5,6},{6,7},{7,8},{8,9},{9,10},{10,1... | collective-permute-start | bytes 1544 | tf_op jit(solution)/shard_map/ppermute | solution.py:25
  198.9 11.8 %all-to-all-start.7 = ((f32[16,1,32]{2,1,0:T(1,128)}), f32[16,1,32]{2,1,0:T(1,128)S(1)}, u32[]{:S(2)}, u32[]{:S(2)}) async-start(f32[16,1,32]{2,1,0:T(1,128)} %broadcast_in_dim.83), calls=%async_computation.7 | async-start | bytes 16384 | tf_op jit(solution)/shard_map/all_to_all | solution.py:31
  222.6 18.5 %all-to-all-start.9 = ((f32[32,1,128]{2,1,0:T(1,128)}), f32[32,1,128]{2,1,0:T(1,128)S(1)}, u32[]{:S(2)}, u32[]{:S(2)}) async-start(f32[32,1,128]{2,1,0:T(1,128)} %broadcast_in_dim.85), calls=%async_computation.9 | async-start | bytes 32768 | tf_op jit(solution)/shard_map/all_to_all | solution.py:31
  256.8 13.8 %collective-permute-start.2 = (f32[128,1]{1,0:T(8,128)S(1)}, f32[128,1]{1,0:T(8,128)S(1)}, u32[]{:S(2)}, u32[]{:S(2)}) collective-permute-start(f32[128,1]{1,0:T(8,128)S(1)} %get-tuple-element.190), channel_id=1, source_target_pairs={{0,1},{1,2},{2,3},{3,4},{4,5},{5,6},{6,7},{7,8},{8,9},{9,10},{10,1... | collective-permute-start | bytes 1544 | tf_op jit(solution)/shard_map/while/body/eval_jaxpr/ppermute | solution.py:25
  273.6 12.1 %all-to-all-start = ((f32[16,1,32]{2,1,0:T(1,128)}), f32[16,1,32]{2,1,0:T(1,128)S(1)}, u32[]{:S(2)}, u32[]{:S(2)}) async-start(f32[16,1,32]{2,1,0:T(1,128)} %broadcast_in_dim.195), calls=%async_computation | async-start | bytes 16384 | tf_op jit(solution)/shard_map/while/body/eval_jaxpr/all_to_all | solution.py:31
  288.2 14.4 %collective-permute-start.2 = (f32[128,1]{1,0:T(8,128)S(1)}, f32[128,1]{1,0:T(8,128)S(1)}, u32[]{:S(2)}, u32[]{:S(2)}) collective-permute-start(f32[128,1]{1,0:T(8,128)S(1)} %get-tuple-element.190), channel_id=1, source_target_pairs={{0,1},{1,2},{2,3},{3,4},{4,5},{5,6},{6,7},{7,8},{8,9},{9,10},{10,1... | collective-permute-start | bytes 1544 | tf_op jit(solution)/shard_map/while/body/eval_jaxpr/ppermute | solution.py:25
  291.0 11.6 %collective-permute-start.3 = (f32[128,1]{1,0:T(8,128)S(1)}, f32[128,1]{1,0:T(8,128)}, u32[]{:S(2)}, u32[]{:S(2)}) collective-permute-start(f32[128,1]{1,0:T(8,128)S(1)} %get-tuple-element.191), channel_id=1, source_target_pairs={{1,0},{2,1},{3,2},{4,3},{5,4},{6,5},{7,6},{8,7},{9,8},{10,9},{11,1... | collective-permute-start | bytes 1544 | tf_op jit(solution)/shard_map/while/body/eval_jaxpr/ppermute | solution.py:25
  305.5 11.8 %all-to-all-start = ((f32[16,1,32]{2,1,0:T(1,128)}), f32[16,1,32]{2,1,0:T(1,128)S(1)}, u32[]{:S(2)}, u32[]{:S(2)}) async-start(f32[16,1,32]{2,1,0:T(1,128)} %broadcast_in_dim.195), calls=%async_computation | async-start | bytes 16384 | tf_op jit(solution)/shard_map/while/body/eval_jaxpr/all_to_all | solution.py:31
  319.9 14.4 %collective-permute-start.2 = (f32[128,1]{1,0:T(8,128)S(1)}, f32[128,1]{1,0:T(8,128)S(1)}, u32[]{:S(2)}, u32[]{:S(2)}) collective-permute-start(f32[128,1]{1,0:T(8,128)S(1)} %get-tuple-element.190), channel_id=1, source_target_pairs={{0,1},{1,2},{2,3},{3,4},{4,5},{5,6},{6,7},{7,8},{8,9},{9,10},{10,1... | collective-permute-start | bytes 1544 | tf_op jit(solution)/shard_map/while/body/eval_jaxpr/ppermute | solution.py:25
  322.7 11.6 %collective-permute-start.3 = (f32[128,1]{1,0:T(8,128)S(1)}, f32[128,1]{1,0:T(8,128)}, u32[]{:S(2)}, u32[]{:S(2)}) collective-permute-start(f32[128,1]{1,0:T(8,128)S(1)} %get-tuple-element.191), channel_id=1, source_target_pairs={{1,0},{2,1},{3,2},{4,3},{5,4},{6,5},{7,6},{8,7},{9,8},{10,9},{11,1... | collective-permute-start | bytes 1544 | tf_op jit(solution)/shard_map/while/body/eval_jaxpr/ppermute | solution.py:25
  337.2 11.8 %all-to-all-start = ((f32[16,1,32]{2,1,0:T(1,128)}), f32[16,1,32]{2,1,0:T(1,128)S(1)}, u32[]{:S(2)}, u32[]{:S(2)}) async-start(f32[16,1,32]{2,1,0:T(1,128)} %broadcast_in_dim.195), calls=%async_computation | async-start | bytes 16384 | tf_op jit(solution)/shard_map/while/body/eval_jaxpr/all_to_all | solution.py:31
  351.6 14.4 %collective-permute-start.2 = (f32[128,1]{1,0:T(8,128)S(1)}, f32[128,1]{1,0:T(8,128)S(1)}, u32[]{:S(2)}, u32[]{:S(2)}) collective-permute-start(f32[128,1]{1,0:T(8,128)S(1)} %get-tuple-element.190), channel_id=1, source_target_pairs={{0,1},{1,2},{2,3},{3,4},{4,5},{5,6},{6,7},{7,8},{8,9},{9,10},{10,1... | collective-permute-start | bytes 1544 | tf_op jit(solution)/shard_map/while/body/eval_jaxpr/ppermute | solution.py:25
  354.3 11.6 %collective-permute-start.3 = (f32[128,1]{1,0:T(8,128)S(1)}, f32[128,1]{1,0:T(8,128)}, u32[]{:S(2)}, u32[]{:S(2)}) collective-permute-start(f32[128,1]{1,0:T(8,128)S(1)} %get-tuple-element.191), channel_id=1, source_target_pairs={{1,0},{2,1},{3,2},{4,3},{5,4},{6,5},{7,6},{8,7},{9,8},{10,9},{11,1... | collective-permute-start | bytes 1544 | tf_op jit(solution)/shard_map/while/body/eval_jaxpr/ppermute | solution.py:25
  368.9 11.8 %all-to-all-start = ((f32[16,1,32]{2,1,0:T(1,128)}), f32[16,1,32]{2,1,0:T(1,128)S(1)}, u32[]{:S(2)}, u32[]{:S(2)}) async-start(f32[16,1,32]{2,1,0:T(1,128)} %broadcast_in_dim.195), calls=%async_computation | async-start | bytes 16384 | tf_op jit(solution)/shard_map/while/body/eval_jaxpr/all_to_all | solution.py:31
  383.2 14.4 %collective-permute-start.2 = (f32[128,1]{1,0:T(8,128)S(1)}, f32[128,1]{1,0:T(8,128)S(1)}, u32[]{:S(2)}, u32[]{:S(2)}) collective-permute-start(f32[128,1]{1,0:T(8,128)S(1)} %get-tuple-element.190), channel_id=1, source_target_pairs={{0,1},{1,2},{2,3},{3,4},{4,5},{5,6},{6,7},{7,8},{8,9},{9,10},{10,1... | collective-permute-start | bytes 1544 | tf_op jit(solution)/shard_map/while/body/eval_jaxpr/ppermute | solution.py:25
  386.0 11.6 %collective-permute-start.3 = (f32[128,1]{1,0:T(8,128)S(1)}, f32[128,1]{1,0:T(8,128)}, u32[]{:S(2)}, u32[]{:S(2)}) collective-permute-start(f32[128,1]{1,0:T(8,128)S(1)} %get-tuple-element.191), channel_id=1, source_target_pairs={{1,0},{2,1},{3,2},{4,3},{5,4},{6,5},{7,6},{8,7},{9,8},{10,9},{11,1... | collective-permute-start | bytes 1544 | tf_op jit(solution)/shard_map/while/body/eval_jaxpr/ppermute | solution.py:25
  400.5 11.8 %all-to-all-start = ((f32[16,1,32]{2,1,0:T(1,128)}), f32[16,1,32]{2,1,0:T(1,128)S(1)}, u32[]{:S(2)}, u32[]{:S(2)}) async-start(f32[16,1,32]{2,1,0:T(1,128)} %broadcast_in_dim.195), calls=%async_computation | async-start | bytes 16384 | tf_op jit(solution)/shard_map/while/body/eval_jaxpr/all_to_all | solution.py:31
  (44 other events, 494.4 us)
